TPU v7x, 1024 devices: a whole 4x4x32 slice. The times are simulated.
1024 devices in a mesh: gy: 16 (over x_hi, y, core), gx: 64 (over x_lo, z).
Axes of the slice: x: 4 (x_hi: 2, x_lo: 2; x = x_hi * 2 + x_lo), y: 4, z: 32, core: 2. Of those that a mesh axis runs over, the one named last changes fastest.
Arguments:
- ocean_blocks: float32 [1024, 4, 8192], P('gy', None, 'gx'), may hold values from -4 to 4
- block_map: int32 [1024, 64], P('gy', 'gx'), may hold values from 0 to 4095, as said below
- velocity: float32 [2, 1024, 8192], P(None, 'gy', 'gx'), may hold values from -2 to 2
- stress: float32 [3, 1024, 8192], P(None, 'gy', 'gx'), may hold values from -3 to 3
- thickness: float32 [5, 1024, 8192], P(None, 'gy', 'gx'), may hold values from 0.05 to 5
- area: float32 [5, 1024, 8192], P(None, 'gy', 'gx'), may hold values from 0.1 to 0.2
- wind: float32 [2, 1024, 8192], P(None, 'gy', 'gx'), may hold values from -3 to 3
- air_temp: float32 [1024, 8192], P('gy', 'gx'), may hold values from -6 to 0
- ice_presence_mask: int32 [1024, 8192], P('gy', 'gx'), may hold values 0 or 1
- ocean_land_mask: int32 [1024, 8192], P('gy', 'gx'), may hold values 0 or 1
- fold_partner_column: int32 [8192], replicated, may hold values from 0 to 8191, as said below
Outputs:
- velocity_out: float32 [2, 1024, 8192], P(None, 'gy', 'gx')
- stress_out: float32 [3, 1024, 8192], P(None, 'gy', 'gx')
- thickness_out: float32 [5, 1024, 8192], P(None, 'gy', 'gx')
Inputs may be any that keep to these rules, and one draw needn't show every extreme that they name: Within each latitude row of devices block_map is a permutation of 0 to 4095; value p * 64 + t names device p, row t. The slots k * 2 to (k + 1) * 2 - 1 of one device all go to one device, into rows k * 2 to (k + 1) * 2 - 1; different k of one device go to different devices. fold_partner_column[i] = (c - i) mod 8192 for one c per draw, so the table is its own inverse.
All inputs are finite; a program needn't handle non-finite values. No bound on the sum of `ice_presence_mask` or of `ocean_land_mask` on one device may be relied on, other than what follows from the above.
Results may differ from a plain program's by a relative error of at most 0.0001.
Values sent between devices are 32-bit elements; how exact they have to be, the bound alone decides.
No kernel may reach another device: no remote copies, remote signals or barrier semaphores. Data moves between devices by JAX's collectives and lax.ppermute only.
A program may use at most 32 MiB of HBM per device.

v0:
```python
import jax
import jax.numpy as jnp
from jax import lax
from jax.sharding import PartitionSpec as P

ITERS = 4


RELAX = 0.5
ECC2 = 4.0
DMIN2 = 0.01
PSTAR = 1.0
CSTAR = 5.0
DTE = 0.3
DRAG = 1.0
FCOR = 0.5
KAPPA = 0.5
GAMMA = 0.3
DTT = 0.5
SREF = 34.0


def with_halo(block, sides, width):
    for axis, dim in sides:
        count = lax.axis_size(axis)
        forward = [(i, i + 1) for i in range(count - 1)]
        forward.append((count - 1, 0))
        backward = [(target, source) for source, target in forward]
        low = lax.ppermute(
            lax.slice_in_dim(block, block.shape[dim] - width, None, axis=dim), axis, forward
        )
        high = lax.ppermute(lax.slice_in_dim(block, 0, width, axis=dim), axis, backward)
        block = jnp.concatenate([low, block, high], axis=dim)
    return block


def regroup_local(ocean_blocks, block_map):
    rows, fields, cols = ocean_blocks.shape
    peers = lax.axis_size("gx")
    group = max(2, rows // peers)
    count = rows // group
    target = block_map[:, 0]
    dest_dev = target[::group] // rows
    dest_row = (target % rows).reshape(count, group)
    chosen = dest_dev[None, :] == jnp.arange(peers, dtype=jnp.int32)[:, None]
    blocks = ocean_blocks.reshape(count, group * fields * cols)
    outgoing = jnp.dot(
        chosen.astype(jnp.float32),
        blocks,
        precision=lax.Precision.HIGHEST,
        preferred_element_type=jnp.float32,
    )
    labels = jnp.sum(jnp.where(chosen[:, :, None], dest_row[None, :, :] + 1, 0), axis=1) - 1
    arrived, arrived_rows = (
        lax.all_to_all(outgoing, "gx", split_axis=0, concat_axis=0, tiled=True),
        lax.all_to_all(labels, "gx", split_axis=0, concat_axis=0, tiled=True),
    )
    flat = arrived.reshape(peers * group, fields * cols)
    picks = (
        arrived_rows.reshape(-1)[None, :] == jnp.arange(rows, dtype=jnp.int32)[:, None]
    ).astype(jnp.float32)
    local = jnp.dot(
        picks, flat, precision=lax.Precision.HIGHEST, preferred_element_type=jnp.float32
    )
    return local.reshape(rows, fields, cols)


def attach_rim_halo(field, signs, width, fold_partner_column):
    rows = field.shape[1]
    cols = field.shape[2]
    padded = with_halo(field, (("gy", 1), ("gx", 2)), width)
    top = jnp.flip(field[:, rows - width :, :], axis=1)
    whole_top = lax.all_gather(top, "gx", axis=2, tiled=True)
    total_cols = whole_top.shape[2]
    columns = (
        lax.axis_index("gx") * cols + jnp.arange(-width, cols + width, dtype=jnp.int32)
    ) % total_cols
    north = jnp.take(whole_top, fold_partner_column[columns], axis=2) * signs
    row_pos = lax.axis_index("gy")
    last_row = lax.axis_size("gy") - 1
    upper = jnp.where(row_pos == last_row, north, padded[:, rows + width :, :])
    lower = jnp.where(row_pos == 0, jnp.zeros_like(north), padded[:, :width, :])
    return jnp.concatenate([lower, padded[:, width : rows + width, :], upper], axis=1)


def compute_strain_rates(u_pad, v_pad):
    strain_rate_east = (u_pad[1:-1, 2:] - u_pad[1:-1, :-2]) * 0.5
    strain_rate_north = (v_pad[2:, 1:-1] - v_pad[:-2, 1:-1]) * 0.5
    strain_rate_shear = (
        u_pad[2:, 1:-1] - u_pad[:-2, 1:-1] + (v_pad[1:-1, 2:] - v_pad[1:-1, :-2])
    ) * 0.25
    return (strain_rate_east, strain_rate_north, strain_rate_shear)


def stress_update(old, strain_rate_east, strain_rate_north, strain_rate_shear, strength):
    divergence = strain_rate_east + strain_rate_north
    tension = strain_rate_east - strain_rate_north
    shear = 2.0 * strain_rate_shear
    delta = jnp.sqrt(divergence * divergence + (tension * tension + shear * shear) / ECC2 + DMIN2)
    zeta = strength / delta
    first = (old[0] + RELAX * (zeta * divergence - strength)) / (1.0 + RELAX)
    second = (old[1] + RELAX * zeta * tension / ECC2) / (1.0 + RELAX)
    third = (old[2] + RELAX * zeta * shear / (2.0 * ECC2)) / (1.0 + RELAX)
    return jnp.stack([first, second, third])


def stress_force(padded):
    normal_x = (padded[0] + padded[1]) * 0.5
    normal_y = (padded[0] - padded[1]) * 0.5
    shear = padded[2]
    eastward_force = (normal_x[1:-1, 2:] - normal_x[1:-1, :-2]) * 0.5 + (
        shear[2:, 1:-1] - shear[:-2, 1:-1]
    ) * 0.5
    northward_force = (shear[1:-1, 2:] - shear[1:-1, :-2]) * 0.5 + (
        normal_y[2:, 1:-1] - normal_y[:-2, 1:-1]
    ) * 0.5
    return (eastward_force, northward_force)


def momentum_solve(
    velocity,
    eastward_force,
    northward_force,
    wind,
    ocean_current_east,
    ocean_current_north,
    ice_mass_per_area,
    coriolis_parameter,
    velocity_mask,
):
    east = velocity[0]
    north = velocity[1]
    implicit_denominator = ice_mass_per_area + DTE * DRAG
    right_side_east = east * ice_mass_per_area + DTE * (
        eastward_force
        + wind[0]
        + DRAG * ocean_current_east
        + ice_mass_per_area * coriolis_parameter * north
    )
    right_side_north = north * ice_mass_per_area + DTE * (
        northward_force
        + wind[1]
        + DRAG * ocean_current_north
        - ice_mass_per_area * coriolis_parameter * east
    )
    return jnp.stack(
        [
            velocity_mask * right_side_east / implicit_denominator,
            velocity_mask * right_side_north / implicit_denominator,
        ]
    )


def column_growth(
    thickness,
    velocity,
    ocean_temp,
    ocean_salt,
    ocean_current_east,
    ocean_current_north,
    air_temp,
    omask,
):
    freeze = -0.054 * (SREF + ocean_salt)
    rel_east = velocity[0] - ocean_current_east
    rel_north = velocity[1] - ocean_current_north
    speed = jnp.sqrt(rel_east * rel_east + rel_north * rel_north + 0.01)
    melt = GAMMA * (ocean_temp - freeze) * speed
    growth = KAPPA * (freeze - air_temp) / (thickness + 0.1)
    return omask * jnp.maximum(thickness + DTT * (growth - melt), 0.0)


def body(
    ocean_blocks,
    block_map,
    velocity,
    stress,
    thickness,
    area,
    wind,
    air_temp,
    ice_presence_mask,
    ocean_land_mask,
    fold_partner_column,
):
    ocean = regroup_local(ocean_blocks, block_map)
    ocean_temp = ocean[:, 0, :]
    ocean_salt = ocean[:, 1, :]
    ocean_current_east = ocean[:, 2, :]
    ocean_current_north = ocean[:, 3, :]
    hsum = jnp.sum(area * thickness, axis=0)
    conc = jnp.sum(area, axis=0)
    strength = PSTAR * hsum * jnp.exp(-CSTAR * (1.0 - conc))
    ice_mass_per_area = hsum + 0.2
    rows = velocity.shape[1]
    total_rows = rows * lax.axis_size("gy")
    row_float = (lax.axis_index("gy") * rows + jnp.arange(rows, dtype=jnp.int32)).astype(
        jnp.float32
    )
    coriolis_parameter = (FCOR * (row_float + 0.5) / float(total_rows))[:, None]
    velocity_mask = (ice_presence_mask * ocean_land_mask).astype(jnp.float32)
    omask = ocean_land_mask.astype(jnp.float32)
    velocity_fold_sign = jnp.array([-1.0, -1.0], dtype=jnp.float32).reshape(2, 1, 1)
    ssign = jnp.ones((3, 1, 1), dtype=jnp.float32)
    for step in range(ITERS):
        velocity_padded = attach_rim_halo(velocity, velocity_fold_sign, 1, fold_partner_column)
        strain_rate_east, strain_rate_north, strain_rate_shear = compute_strain_rates(
            velocity_padded[0], velocity_padded[1]
        )
        stress = stress_update(
            stress, strain_rate_east, strain_rate_north, strain_rate_shear, strength
        )
        spad = attach_rim_halo(stress, ssign, 1, fold_partner_column)
        eastward_force, northward_force = stress_force(spad)
        velocity = momentum_solve(
            velocity,
            eastward_force,
            northward_force,
            wind,
            ocean_current_east,
            ocean_current_north,
            ice_mass_per_area,
            coriolis_parameter,
            velocity_mask,
        )
    thickness_out = column_growth(
        thickness,
        velocity,
        ocean_temp,
        ocean_salt,
        ocean_current_east,
        ocean_current_north,
        air_temp,
        omask,
    )
    return (velocity, stress, thickness_out)


def solution(mesh):
    placed = (
        P("gy", None, "gx"),
        P("gy", "gx"),
        P(None, "gy", "gx"),
        P(None, "gy", "gx"),
        P(None, "gy", "gx"),
        P(None, "gy", "gx"),
        P(None, "gy", "gx"),
        P("gy", "gx"),
        P("gy", "gx"),
        P("gy", "gx"),
        P(),
    )
    return jax.shard_map(
        body,
        mesh=mesh,
        in_specs=placed,
        out_specs=(P(None, "gy", "gx"), P(None, "gy", "gx"), P(None, "gy", "gx")),
        check_vma=False,
    )
```

profile of v0, /device:TPU:2, one launch (start us, length us, event | category | flops | bytes accessed | tf_op | source)
XLA Modules:
  0.0 1187.2 jit_solution(13917788711950681926)
XLA Ops:
  4.4 30.5 %all-to-all-start = ((s32[64,1,2]{2,1,0:T(1,128)}), s32[64,1,2]{2,1,0:T(1,128)S(1)}, u32[]{:S(2)}, u32[]{:S(2)}) async-start(s32[64,1,2]{2,1,0:T(1,128)} %copy.97), calls=%async_computation | async-start | bytes 65536 | tf_op jit(solution)/shard_map/all_to_all | solution.py:56
  35.6 5.4 collective-permute-start.1
  46.8 120.3 %all_gather.24 = f32[2,1,8192]{2,1,0:T(1,128)S(1)} all-gather(f32[2,1,128]{2,1,0:T(1,128)S(1)} %get-tuple-element.99), channel_id=1, replica_groups=mesh['gy'=16,'gx'=64] {'gx'}, dimensions={2}, use_global_device_ids=true | all-gather | bytes 66560 | tf_op jit(solution)/shard_map/all_gather | solution.py:73
  171.0 3.9 collective-permute-start.2
  175.0 2.7 copy.112
  177.6 2.8 gather_fusion.1
  180.8 11.9 %all-to-all-start.1 = ((f32[64,1,1024]{2,1,0:T(1,128)}), f32[64,1,1024]{2,1,0:T(1,128)S(1)}, u32[]{:S(2)}, u32[]{:S(2)}) async-start(f32[64,1,1024]{2,1,0:T(1,128)} %copy.98), calls=%async_computation.1 | async-start | bytes 524288 | tf_op jit(solution)/shard_map/all_to_all | solution.py:55
  195.0 2.4 collective-permute-start.4
  197.4 6.1 collective-permute-done.4
  203.7 4.5 collective-permute-start.7
  210.1 120.7 %all_gather.25 = f32[3,1,8192]{2,1,0:T(1,128)S(1)} all-gather(f32[3,1,128]{2,1,0:T(1,128)S(1)} %get-tuple-element.83), channel_id=1, replica_groups=mesh['gy'=16,'gx'=64] {'gx'}, dimensions={2}, use_global_device_ids=true | all-gather | bytes 99840 | tf_op jit(solution)/shard_map/all_gather | solution.py:73
  330.8 2.7 copy.113
  333.4 2.8 gather_fusion.2
  340.9 2.4 collective-permute-start.8
  343.4 6.1 collective-permute-done.8
  351.5 3.9 collective-permute-start.10
  355.4 118.3 %all_gather.26 = f32[2,1,8192]{2,1,0:T(1,128)S(1)} all-gather(f32[2,1,128]{2,1,0:T(1,128)S(1)} %get-tuple-element.97), channel_id=1, replica_groups=mesh['gy'=16,'gx'=64] {'gx'}, dimensions={2}, use_global_device_ids=true | all-gather | bytes 66560 | tf_op jit(solution)/shard_map/all_gather | solution.py:73
  473.7 2.6 copy.114
  476.3 2.8 gather_fusion.3
  481.8 2.4 collective-permute-start.12
  484.2 6.1 collective-permute-done.12
  492.4 3.9 collective-permute-start.14
  496.3 118.7 %all_gather.27 = f32[3,1,8192]{2,1,0:T(1,128)S(1)} all-gather(f32[3,1,128]{2,1,0:T(1,128)S(1)} %get-tuple-element.81), channel_id=1, replica_groups=mesh['gy'=16,'gx'=64] {'gx'}, dimensions={2}, use_global_device_ids=true | all-gather | bytes 99840 | tf_op jit(solution)/shard_map/all_gather | solution.py:73
  615.0 2.6 copy.115
  617.6 2.8 gather_fusion.4
  623.0 2.4 collective-permute-start.16
  625.4 6.1 collective-permute-done.16
  633.6 3.9 collective-permute-start.18
  637.5 118.5 %all_gather.28 = f32[2,1,8192]{2,1,0:T(1,128)S(1)} all-gather(f32[2,1,128]{2,1,0:T(1,128)S(1)} %get-tuple-element.95), channel_id=1, replica_groups=mesh['gy'=16,'gx'=64] {'gx'}, dimensions={2}, use_global_device_ids=true | all-gather | bytes 66560 | tf_op jit(solution)/shard_map/all_gather | solution.py:73
  756.0 2.6 copy.116
  758.6 2.8 gather_fusion.5
  764.1 2.4 collective-permute-start.20
  766.5 6.2 collective-permute-done.20
  774.8 3.9 collective-permute-start.22
  778.7 118.7 %all_gather.29 = f32[3,1,8192]{2,1,0:T(1,128)S(1)} all-gather(f32[3,1,128]{2,1,0:T(1,128)S(1)} %get-tuple-element.79), channel_id=1, replica_groups=mesh['gy'=16,'gx'=64] {'gx'}, dimensions={2}, use_global_device_ids=true | all-gather | bytes 99840 | tf_op jit(solution)/shard_map/all_gather | solution.py:73
  897.4 2.6 copy.117
  900.0 2.8 gather_fusion.6
  905.4 2.4 collective-permute-start.24
  907.8 6.1 collective-permute-done.24
  915.9 3.9 collective-permute-start.26
  919.9 118.3 %all_gather.30 = f32[2,1,8192]{2,1,0:T(1,128)S(1)} all-gather(f32[2,1,128]{2,1,0:T(1,128)S(1)} %get-tuple-element.93), channel_id=1, replica_groups=mesh['gy'=16,'gx'=64] {'gx'}, dimensions={2}, use_global_device_ids=true | all-gather | bytes 66560 | tf_op jit(solution)/shard_map/all_gather | solution.py:73
  1038.2 2.6 copy.118
  1040.8 2.8 gather_fusion.7
  1048.9 6.2 collective-permute-done.28
  1057.1 3.9 collective-permute-start.30
  1061.1 118.7 %all_gather.31 = f32[3,1,8192]{2,1,0:T(1,128)S(1)} all-gather(f32[3,1,128]{2,1,0:T(1,128)S(1)} %get-tuple-element.77), channel_id=1, replica_groups=mesh['gy'=16,'gx'=64] {'gx'}, dimensions={2}, use_global_device_ids=true | all-gather | bytes 99840 | tf_op jit(solution)/shard_map/all_gather | solution.py:73
  1179.7 2.6 copy.119
  1182.4 2.8 gather_fusion.8
  (179 shorter events, 52.4 us)
Async XLA Ops:
  0.6 42.3 %copy-start = (s32[8192]{0:T(1024)S(1)}, s32[8192]{0:T(1024)}, u32[]{:S(2)}) copy-start(s32[8192]{0:T(1024)} %param.26) | copy-start | bytes 98308
  0.6 179.9 %copy-start.1 = (f32[2,64,128]{2,1,0:T(8,128)S(1)}, f32[2,64,128]{2,1,0:T(8,128)}, u32[]{:S(2)}) copy-start(f32[2,64,128]{2,1,0:T(8,128)} %param.18) | copy-start | bytes 196612
  4.4 176.4 %all-to-all-start = ((s32[64,1,2]{2,1,0:T(1,128)}), s32[64,1,2]{2,1,0:T(1,128)S(1)}, u32[]{:S(2)}, u32[]{:S(2)}) async-start(s32[64,1,2]{2,1,0:T(1,128)} %copy.97), calls=%async_computation | async-start | bytes 65536 | tf_op jit(solution)/shard_map/all_to_all | solution.py:56
  35.6 132.6 %collective-permute-start.1 = (f32[2,1,128]{2,1,0:T(1,128)S(1)}, f32[2,1,128]{2,1,0:T(1,128)S(1)}, u32[]{:S(2)}, u32[]{:S(2)}) collective-permute-start(f32[2,1,128]{2,1,0:T(1,128)S(1)} %get-tuple-element.100), channel_id=1, source_target_pairs={{64,0},{128,64},{192,128},{256,192},{320,256},{384,320},{448,384},... | collective-permute-start | bytes 3080 | tf_op jit(solution)/shard_map/ppermute | solution.py:32
  41.0 127.2 %collective-permute-start = (f32[2,1,128]{2,1,0:T(1,128)S(1)}, f32[2,1,128]{2,1,0:T(1,128)S(1)}, u32[]{:S(2)}, u32[]{:S(2)}) collective-permute-start(f32[2,1,128]{2,1,0:T(1,128)S(1)} %get-tuple-element.99), channel_id=1, source_target_pairs={{0,64},{64,128},{128,192},{192,256},{256,320},{320,384},{384,448},... | collective-permute-start | bytes 3080 | tf_op jit(solution)/shard_map/ppermute | solution.py:29
  44.4 148.4 %copy-start.6 = (f32[3,64,128]{2,1,0:T(8,128)S(1)}, f32[3,64,128]{2,1,0:T(8,128)}, u32[]{:S(2)}) copy-start(f32[3,64,128]{2,1,0:T(8,128)} %param.19) | copy-start | bytes 294916
  169.1 11.4 collective-permute-start.3
  171.0 9.5 collective-permute-start.2
  180.8 156.8 %all-to-all-start.1 = ((f32[64,1,1024]{2,1,0:T(1,128)}), f32[64,1,1024]{2,1,0:T(1,128)S(1)}, u32[]{:S(2)}, u32[]{:S(2)}) async-start(f32[64,1,1024]{2,1,0:T(1,128)} %copy.98), calls=%async_computation.1 | async-start | bytes 524288 | tf_op jit(solution)/shard_map/all_to_all | solution.py:55
  193.1 4.4 collective-permute-start.5
  195.0 8.6 collective-permute-start.4
  203.7 132.7 %collective-permute-start.7 = (f32[3,66,1]{2,1,0:T(8,128)S(1)}, f32[3,66,1]{2,1,0:T(8,128)S(1)}, u32[]{:S(2)}, u32[]{:S(2)}) collective-permute-start(f32[3,66,1]{2,1,0:T(8,128)S(1)} %get-tuple-element.76), channel_id=1, source_target_pairs={{1,0},{2,1},{3,2},{4,3},{5,4},{6,5},{7,6},{8,7},{9,8},{10,9},{11,1... | collective-permute-start | bytes 2384 | tf_op jit(solution)/shard_map/ppermute | solution.py:32
  208.2 128.2 %collective-permute-start.6 = (f32[3,66,1]{2,1,0:T(8,128)S(1)}, f32[3,66,1]{2,1,0:T(8,128)S(1)}, u32[]{:S(2)}, u32[]{:S(2)}) collective-permute-start(f32[3,66,1]{2,1,0:T(8,128)S(1)} %get-tuple-element.75), channel_id=1, source_target_pairs={{0,1},{1,2},{2,3},{3,4},{4,5},{5,6},{6,7},{7,8},{8,9},{9,10},{10,1... | collective-permute-start | bytes 2384 | tf_op jit(solution)/shard_map/ppermute | solution.py:29
  330.8 7.9 copy-start.2
  330.8 7.9 copy-start.4
  330.8 7.9 copy-start.8
  339.0 4.3 collective-permute-start.9
  340.9 8.5 collective-permute-start.8
  349.5 129.7 %collective-permute-start.11 = (f32[2,66,1]{2,1,0:T(8,128)S(1)}, f32[2,66,1]{2,1,0:T(8,128)S(1)}, u32[]{:S(2)}, u32[]{:S(2)}) collective-permute-start(f32[2,66,1]{2,1,0:T(8,128)S(1)} %get-tuple-element.90), channel_id=1, source_target_pairs={{1,0},{2,1},{3,2},{4,3},{5,4},{6,5},{7,6},{8,7},{9,8},{10,9},{11,1... | collective-permute-start | bytes 1592 | tf_op jit(solution)/shard_map/ppermute | solution.py:32
  351.5 127.8 %collective-permute-start.10 = (f32[2,66,1]{2,1,0:T(8,128)S(1)}, f32[2,66,1]{2,1,0:T(8,128)S(1)}, u32[]{:S(2)}, u32[]{:S(2)}) collective-permute-start(f32[2,66,1]{2,1,0:T(8,128)S(1)} %get-tuple-element.89), channel_id=1, source_target_pairs={{0,1},{1,2},{2,3},{3,4},{4,5},{5,6},{6,7},{7,8},{8,9},{9,10},{10,1... | collective-permute-start | bytes 1592 | tf_op jit(solution)/shard_map/ppermute | solution.py:29
  479.5 141.4 %copy-start.7 = (f32[64,128]{1,0:T(8,128)S(1)}, f32[64,128]{1,0:T(8,128)}, u32[]{:S(2)}) copy-start(f32[64,128]{1,0:T(8,128)} %param.23) | copy-start | bytes 98308
  479.8 4.3 collective-permute-start.13
  481.8 8.5 collective-permute-start.12
  490.4 130.1 %collective-permute-start.15 = (f32[3,66,1]{2,1,0:T(8,128)S(1)}, f32[3,66,1]{2,1,0:T(8,128)S(1)}, u32[]{:S(2)}, u32[]{:S(2)}) collective-permute-start(f32[3,66,1]{2,1,0:T(8,128)S(1)} %get-tuple-element.74), channel_id=1, source_target_pairs={{1,0},{2,1},{3,2},{4,3},{5,4},{6,5},{7,6},{8,7},{9,8},{10,9},{11,1... | collective-permute-start | bytes 2384 | tf_op jit(solution)/shard_map/ppermute | solution.py:32
  492.4 128.1 %collective-permute-start.14 = (f32[3,66,1]{2,1,0:T(8,128)S(1)}, f32[3,66,1]{2,1,0:T(8,128)S(1)}, u32[]{:S(2)}, u32[]{:S(2)}) collective-permute-start(f32[3,66,1]{2,1,0:T(8,128)S(1)} %get-tuple-element.73), channel_id=1, source_target_pairs={{0,1},{1,2},{2,3},{3,4},{4,5},{5,6},{6,7},{7,8},{8,9},{9,10},{10,1... | collective-permute-start | bytes 2384 | tf_op jit(solution)/shard_map/ppermute | solution.py:29
  621.1 4.3 collective-permute-start.17
  623.0 8.6 collective-permute-start.16
  631.7 129.9 %collective-permute-start.19 = (f32[2,66,1]{2,1,0:T(8,128)S(1)}, f32[2,66,1]{2,1,0:T(8,128)S(1)}, u32[]{:S(2)}, u32[]{:S(2)}) collective-permute-start(f32[2,66,1]{2,1,0:T(8,128)S(1)} %get-tuple-element.88), channel_id=1, source_target_pairs={{1,0},{2,1},{3,2},{4,3},{5,4},{6,5},{7,6},{8,7},{9,8},{10,9},{11,1... | collective-permute-start | bytes 1592 | tf_op jit(solution)/shard_map/ppermute | solution.py:32
  633.6 128.0 %collective-permute-start.18 = (f32[2,66,1]{2,1,0:T(8,128)S(1)}, f32[2,66,1]{2,1,0:T(8,128)S(1)}, u32[]{:S(2)}, u32[]{:S(2)}) collective-permute-start(f32[2,66,1]{2,1,0:T(8,128)S(1)} %get-tuple-element.87), channel_id=1, source_target_pairs={{0,1},{1,2},{2,3},{3,4},{4,5},{5,6},{6,7},{7,8},{8,9},{9,10},{10,1... | collective-permute-start | bytes 1592 | tf_op jit(solution)/shard_map/ppermute | solution.py:29
  762.2 4.3 collective-permute-start.21
  764.1 8.7 collective-permute-start.20
  772.9 130.1 %collective-permute-start.23 = (f32[3,66,1]{2,1,0:T(8,128)S(1)}, f32[3,66,1]{2,1,0:T(8,128)S(1)}, u32[]{:S(2)}, u32[]{:S(2)}) collective-permute-start(f32[3,66,1]{2,1,0:T(8,128)S(1)} %get-tuple-element.72), channel_id=1, source_target_pairs={{1,0},{2,1},{3,2},{4,3},{5,4},{6,5},{7,6},{8,7},{9,8},{10,9},{11,1... | collective-permute-start | bytes 2384 | tf_op jit(solution)/shard_map/ppermute | solution.py:32
  774.8 128.1 %collective-permute-start.22 = (f32[3,66,1]{2,1,0:T(8,128)S(1)}, f32[3,66,1]{2,1,0:T(8,128)S(1)}, u32[]{:S(2)}, u32[]{:S(2)}) collective-permute-start(f32[3,66,1]{2,1,0:T(8,128)S(1)} %get-tuple-element.71), channel_id=1, source_target_pairs={{0,1},{1,2},{2,3},{3,4},{4,5},{5,6},{6,7},{7,8},{8,9},{9,10},{10,1... | collective-permute-start | bytes 2384 | tf_op jit(solution)/shard_map/ppermute | solution.py:29
  903.5 4.3 collective-permute-start.25
  905.4 8.5 collective-permute-start.24
  914.0 129.7 %collective-permute-start.27 = (f32[2,66,1]{2,1,0:T(8,128)S(1)}, f32[2,66,1]{2,1,0:T(8,128)S(1)}, u32[]{:S(2)}, u32[]{:S(2)}) collective-permute-start(f32[2,66,1]{2,1,0:T(8,128)S(1)} %get-tuple-element.86), channel_id=1, source_target_pairs={{1,0},{2,1},{3,2},{4,3},{5,4},{6,5},{7,6},{8,7},{9,8},{10,9},{11,1... | collective-permute-start | bytes 1592 | tf_op jit(solution)/shard_map/ppermute | solution.py:32
  915.9 127.8 %collective-permute-start.26 = (f32[2,66,1]{2,1,0:T(8,128)S(1)}, f32[2,66,1]{2,1,0:T(8,128)S(1)}, u32[]{:S(2)}, u32[]{:S(2)}) collective-permute-start(f32[2,66,1]{2,1,0:T(8,128)S(1)} %get-tuple-element.85), channel_id=1, source_target_pairs={{0,1},{1,2},{2,3},{3,4},{4,5},{5,6},{6,7},{7,8},{8,9},{9,10},{10,1... | collective-permute-start | bytes 1592 | tf_op jit(solution)/shard_map/ppermute | solution.py:29
  1044.3 142.2 %copy-start.3 = (f32[5,64,128]{2,1,0:T(8,128)S(1)}, f32[5,64,128]{2,1,0:T(8,128)}, u32[]{:S(2)}) copy-start(f32[5,64,128]{2,1,0:T(8,128)} %param.20) | copy-start | bytes 491524
  1044.3 142.8 %copy-start.5 = (f32[3,64,128]{2,1,0:T(8,128)}, f32[3,64,128]{2,1,0:T(8,128)S(1)}, u32[]{:S(2)}) copy-start(f32[3,64,128]{2,1,0:T(8,128)S(1)} %pad_maximum_fusion.20) | copy-start | bytes 294916
  1044.4 4.5 collective-permute-start.29
  1046.4 8.7 collective-permute-start.28
  1055.2 130.1 %collective-permute-start.31 = (f32[3,66,1]{2,1,0:T(8,128)S(1)}, f32[3,66,1]{2,1,0:T(8,128)S(1)}, u32[]{:S(2)}, u32[]{:S(2)}) collective-permute-start(f32[3,66,1]{2,1,0:T(8,128)S(1)} %get-tuple-element.70), channel_id=1, source_target_pairs={{1,0},{2,1},{3,2},{4,3},{5,4},{6,5},{7,6},{8,7},{9,8},{10,9},{11,1... | collective-permute-start | bytes 2384 | tf_op jit(solution)/shard_map/ppermute | solution.py:32
  1057.1 128.1 %collective-permute-start.30 = (f32[3,66,1]{2,1,0:T(8,128)S(1)}, f32[3,66,1]{2,1,0:T(8,128)S(1)}, u32[]{:S(2)}, u32[]{:S(2)}) collective-permute-start(f32[3,66,1]{2,1,0:T(8,128)S(1)} %get-tuple-element.69), channel_id=1, source_target_pairs={{0,1},{1,2},{2,3},{3,4},{4,5},{5,6},{6,7},{7,8},{8,9},{9,10},{10,1... | collective-permute-start | bytes 2384 | tf_op jit(solution)/shard_map/ppermute | solution.py:29
where the time goes:
time: 1190 us
  blocking collectives  952 us (80%)
  starting transfers between devices  127 us (11%)
  local copies, waits for them, and re-layouts  52 us (4%)
  waiting for transfers between devices  43 us (4%)
    all_gather x8, blocking collectives, attach_rim_halo(): whole_top = lax.all_gather(top, 'gx', axis=2, tiled=True)  952 us
    ppermute x16, starting transfers between devices, with_halo(): lax.ppermute(lax.slice_in_dim(block, block.shape[dim] - width, None, axis...  48.1 us
    ppermute x16, waiting for transfers between devices, with_halo(): lax.ppermute(lax.slice_in_dim(block, block.shape[dim] - width, None, axis...  43 us
    ppermute x16, starting transfers between devices, with_halo(): lax.ppermute(lax.slice_in_dim(block, 0, width, axis=dim), axis, backward)  36.9 us
    all_to_all x1, starting transfers between devices, regroup_local(): lax.all_to_all(labels, 'gx', split_axis=0, concat_axis=0, tiled=True)  30.5 us
    gather x17, local copies, waits for them, and re-layouts, attach_rim_halo(): north = jnp.take(whole_top, fold_partner_column[columns], axis=2) * signs  24.8 us
  transfers between devices with their start and end apart: 34, of which 7 were waited for; matrix products, arithmetic and copies ran while one was open for 4% of the time, Pallas kernels for 0%

commit v1 on v0

--- a/solution.py
+++ b/solution.py
@@ -20,18 +20,11 @@
 SREF = 34.0
 
 
-def with_halo(block, sides, width):
-    for axis, dim in sides:
-        count = lax.axis_size(axis)
-        forward = [(i, i + 1) for i in range(count - 1)]
-        forward.append((count - 1, 0))
-        backward = [(target, source) for source, target in forward]
-        low = lax.ppermute(
-            lax.slice_in_dim(block, block.shape[dim] - width, None, axis=dim), axis, forward
-        )
-        high = lax.ppermute(lax.slice_in_dim(block, 0, width, axis=dim), axis, backward)
-        block = jnp.concatenate([low, block, high], axis=dim)
-    return block
+def shift_pairs(count, step, cyclic):
+    pairs = [(i, i + step) for i in range(count) if 0 <= i + step < count]
+    if cyclic:
+        pairs = [(i, (i + step) % count) for i in range(count)]
+    return pairs
 
 
 def regroup_local(ocean_blocks, block_map):
@@ -51,11 +44,10 @@
         preferred_element_type=jnp.float32,
     )
     labels = jnp.sum(jnp.where(chosen[:, :, None], dest_row[None, :, :] + 1, 0), axis=1) - 1
-    arrived, arrived_rows = (
-        lax.all_to_all(outgoing, "gx", split_axis=0, concat_axis=0, tiled=True),
-        lax.all_to_all(labels, "gx", split_axis=0, concat_axis=0, tiled=True),
-    )
-    flat = arrived.reshape(peers * group, fields * cols)
+    packed = jnp.concatenate([outgoing, labels.astype(jnp.float32)], axis=1)
+    arrived = lax.all_to_all(packed, "gx", split_axis=0, concat_axis=0, tiled=True)
+    flat = arrived[:, : group * fields * cols].reshape(peers * group, fields * cols)
+    arrived_rows = arrived[:, group * fields * cols :].astype(jnp.int32)
     picks = (
         arrived_rows.reshape(-1)[None, :] == jnp.arange(rows, dtype=jnp.int32)[:, None]
     ).astype(jnp.float32)
@@ -65,22 +57,47 @@
     return local.reshape(rows, fields, cols)
 
 
-def attach_rim_halo(field, signs, width, fold_partner_column):
-    rows = field.shape[1]
-    cols = field.shape[2]
-    padded = with_halo(field, (("gy", 1), ("gx", 2)), width)
-    top = jnp.flip(field[:, rows - width :, :], axis=1)
-    whole_top = lax.all_gather(top, "gx", axis=2, tiled=True)
-    total_cols = whole_top.shape[2]
-    columns = (
-        lax.axis_index("gx") * cols + jnp.arange(-width, cols + width, dtype=jnp.int32)
-    ) % total_cols
-    north = jnp.take(whole_top, fold_partner_column[columns], axis=2) * signs
-    row_pos = lax.axis_index("gy")
-    last_row = lax.axis_size("gy") - 1
-    upper = jnp.where(row_pos == last_row, north, padded[:, rows + width :, :])
-    lower = jnp.where(row_pos == 0, jnp.zeros_like(north), padded[:, :width, :])
-    return jnp.concatenate([lower, padded[:, width : rows + width, :], upper], axis=1)
+def fold_row(top, fold_start, fold_rest):
+    peers = lax.axis_size("gx")
+    cols = top.shape[-1]
+    low = 8 if peers % 8 == 0 else 1
+    a = fold_start // low
+    b = fold_start % low
+
+    def reflect(aa):
+        return lambda t: lax.ppermute(
+            t, "gx", [(e, (low * aa - e) % peers) for e in range(peers)]
+        )
+
+    def shift(bb):
+        def run(y):
+            near = lax.ppermute(y, "gx", [(e, (e + bb) % peers) for e in range(peers)])
+            far = lax.ppermute(y, "gx", [(e, (e + bb - 1) % peers) for e in range(peers)])
+            return near, far
+
+        return run
+
+    mirrored = lax.switch(a, [reflect(aa) for aa in range(peers // low)], top)
+    near, far = lax.switch(b, [shift(bb) for bb in range(low)], mirrored)
+    both = jnp.concatenate([far, near], axis=-1)
+    picked = lax.dynamic_slice_in_dim(both, fold_rest + 1, cols, axis=-1)
+    return jnp.flip(picked, axis=-1)
+
+
+def attach_rim_halo(field, signs, fold_start, fold_rest):
+    ny = lax.axis_size("gy")
+    nx = lax.axis_size("gx")
+    south = lax.ppermute(field[:, -1:, :], "gy", shift_pairs(ny, 1, False))
+    north = lax.ppermute(field[:, :1, :], "gy", shift_pairs(ny, -1, False))
+    west = lax.ppermute(field[:, :, -1:], "gx", shift_pairs(nx, 1, True))
+    east = lax.ppermute(field[:, :, :1], "gx", shift_pairs(nx, -1, True))
+    folded = fold_row(field[:, -1, :], fold_start, fold_rest)[:, None, :] * signs
+    north = jnp.where(lax.axis_index("gy") == ny - 1, folded, north)
+    rows = jnp.concatenate([south, field, north], axis=1)
+    corner = jnp.zeros_like(rows[:, :, :1])
+    west = jnp.concatenate([corner[:, :1], west, corner[:, :1]], axis=1)
+    east = jnp.concatenate([corner[:, :1], east, corner[:, :1]], axis=1)
+    return jnp.concatenate([west, rows, east], axis=2)
 
 
 def compute_strain_rates(u_pad, v_pad):
@@ -202,15 +219,20 @@
     omask = ocean_land_mask.astype(jnp.float32)
     velocity_fold_sign = jnp.array([-1.0, -1.0], dtype=jnp.float32).reshape(2, 1, 1)
     ssign = jnp.ones((3, 1, 1), dtype=jnp.float32)
-    for step in range(ITERS):
-        velocity_padded = attach_rim_halo(velocity, velocity_fold_sign, 1, fold_partner_column)
+    cols = velocity.shape[2]
+    fold_col = fold_partner_column[0] % (cols * lax.axis_size("gx"))
+    fold_start = fold_col // cols
+    fold_rest = fold_col % cols
+    def subcycle(step, state):
+        velocity, stress = state
+        velocity_padded = attach_rim_halo(velocity, velocity_fold_sign, fold_start, fold_rest)
         strain_rate_east, strain_rate_north, strain_rate_shear = compute_strain_rates(
             velocity_padded[0], velocity_padded[1]
         )
         stress = stress_update(
             stress, strain_rate_east, strain_rate_north, strain_rate_shear, strength
         )
-        spad = attach_rim_halo(stress, ssign, 1, fold_partner_column)
+        spad = attach_rim_halo(stress, ssign, fold_start, fold_rest)
         eastward_force, northward_force = stress_force(spad)
         velocity = momentum_solve(
             velocity,
@@ -223,6 +245,9 @@
             coriolis_parameter,
             velocity_mask,
         )
+        return velocity, stress
+
+    velocity, stress = lax.fori_loop(0, ITERS, subcycle, (velocity, stress))
     thickness_out = column_growth(
         thickness,
         velocity,

time: 1190 us -> 519 us (0.44)
  the two profiles are of different devices: /device:TPU:2 before, /device:TPU:38 now
where the time goes in v1:
time: 519 us; the launch traced here: 517 us
  starting transfers between devices  370 us (71%)
  waiting for transfers between devices  113 us (22%)
  other arithmetic  17.4 us (3%)
  local copies, waits for them, and re-layouts  11.5 us (2%)
    ppermute x8, starting transfers between devices, run(): lax.ppermute(y, 'gx', [(e, (e + bb - 1) % peers) for e in range(peers)])  139 us
    ppermute x8, starting transfers between devices, reflect(): lax.ppermute(t, 'gx', [(e, (low * aa - e) % peers) for e in range(peers)])  63.2 us
    ppermute x8, starting transfers between devices, run(): near = lax.ppermute(y, 'gx', [(e, (e + bb) % peers) for e in range(peers)])  63.1 us
    all_to_all x1, waiting for transfers between devices, regroup_local(): lax.all_to_all(packed, 'gx', split_axis=0, concat_axis=0, tiled=True)  36.1 us
    all_to_all x1, starting transfers between devices, regroup_local(): lax.all_to_all(packed, 'gx', split_axis=0, concat_axis=0, tiled=True)  30.1 us
    ppermute x8, waiting for transfers between devices, reflect(): lax.ppermute(t, 'gx', [(e, (low * aa - e) % peers) for e in range(peers)])  27.9 us
    ppermute x8, starting transfers between devices, attach_rim_halo(): west = lax.ppermute(field[:, :, -1:], 'gx', shift_pairs(nx, 1, True))  27.2 us
    ppermute x8, waiting for transfers between devices, attach_rim_halo(): south = lax.ppermute(field[:, -1:, :], 'gy', shift_pairs(ny, 1, False))  18.6 us
  transfers between devices with their start and end apart: 57, of which 29 were waited for; matrix products, arithmetic and copies ran while one was open for 2% of the time, Pallas kernels for 0%

profile of v1, /device:TPU:38, one launch (start us, length us, event | category | flops | bytes accessed | tf_op | source)
XLA Modules:
  0.0 516.9 jit_solution(1206754335792756645)
XLA Ops:
  4.1 30.1 %all-to-all-start = ((f32[64,1,1026]{2,1,0:T(1,128)}), f32[64,1,1026]{2,1,0:T(1,128)S(1)}, u32[]{:S(2)}, u32[]{:S(2)}) async-start(f32[64,1,1026]{2,1,0:T(1,128)} %copy.161), calls=%async_computation | async-start | bytes 589824 | tf_op jit(solution)/shard_map/all_to_all | solution.py:48
  38.4 36.1 %all-to-all-done = f32[64,1,1026]{2,1,0:T(1,128)S(1)} async-done(((f32[64,1,1026]{2,1,0:T(1,128)}), f32[64,1,1026]{2,1,0:T(1,128)S(1)}, u32[]{:S(2)}, u32[]{:S(2)}) %all-to-all-start) | async-done | bytes 262688 | tf_op jit(solution)/shard_map/all_to_all | solution.py:48
  76.0 439.4 %while.18 = (s32[]{:T(128)}, f32[2,64,128]{2,1,0:T(8,128)S(1)}, f32[3,64,128]{2,1,0:T(8,128)S(1)}, f32[64,128]{1,0:T(8,128)S(1)}, s32[]{:T(128)}, /*index=5*/s32...) while((s32[]{:T(128)}, f32[2,64,128]{2,1,0:T(8,128)S(1)}, ...), condition=%wide.region_36.37_spmd.clone.clone, body=%wide.region_3.36_spmd.sunk.clone.clone.sunk | while | flops 1034430 | bytes 3128104 | solution.py:250
  78.1 5.7 %collective-permute-start.48 = (f32[2,64,1]{1,0,2:T(2,128)S(1)}, f32[2,64,1]{1,0,2:T(2,128)S(1)}, u32[]{:S(2)}, u32[]{:S(2)}) collective-permute-start(f32[2,64,1]{1,0,2:T(2,128)S(1)} %get-tuple-element.808), channel_id=1, source_target_pairs={{0,1},{1,2},{2,3},{3,4},{4,5},{5,6},{6,7},{7,8},{8,9},{9,10},{10,1... | collective-permute-start | bytes 1544 | tf_op jit(solution)/shard_map/while/body/eval_jaxpr/ppermute | solution.py:92
  86.3 11.5 %conditional.20 = (f32[2,128]{1,0:T(2,128)}) conditional(s32[]{:T(128)} %get-tuple-element.906, f32[2,128]{1,0:T(2,128)} %bitcast.160, f32[2,128]{1,0:T(2,128)} %bitcast.160, f32[2,128]{1,0:T(2,128)} %bitcast.160, f32[2,128]{1,0:T(2,128)} %bitcast.160, f32[2,128]{1,0:T(2,128)} %bitcast.160, ...), branch_computations={%region_4.4_spmd, %region_5.5_spmd, %region_6.6_spmd, %region_7.7_... | conditional | bytes 4144 | solution.py:80
  86.3 4.4 collective-permute-start.1
  90.8 7.1 %collective-permute-done.1 = f32[2,128]{1,0:T(2,128)} collective-permute-done((f32[2,128]{1,0:T(2,128)}, f32[2,128]{1,0:T(2,128)}, u32[]{:S(2)}, u32[]{:S(2)}) %collective-permute-start.1) | collective-permute-done | bytes 1056 | tf_op jit(solution)/shard_map/while/body/eval_jaxpr/cond/branch_1_fun/ppermute | solution.py:68
  97.9 23.7 %conditional.21 = (f32[2,128]{1,0:T(2,128)}, f32[2,128]{1,0:T(2,128)}) conditional(s32[]{:T(128)} %get-tuple-element.907, f32[2,128]{1,0:T(2,128)} %get-tuple-element.920, f32[2,128]{1,0:T(2,128)} %get-tuple-element.920, f32[2,128]{1,0:T(2,128)} %get-tuple-element.920, f32[2,128]{1,0:T(2,128)} %get-tuple-element.920, ...), branch_computations={%region_12.12_spmd, %region_13.13_spmd, %region_14.14_spmd, %regio... | conditional | bytes 8288 | solution.py:81
  102.2 17.8 %collective-permute-start.21 = (f32[2,128]{1,0:T(2,128)}, f32[2,128]{1,0:T(2,128)}, u32[]{:S(2)}, u32[]{:S(2)}) collective-permute-start(f32[2,128]{1,0:T(2,128)} %param.14), channel_id=1, source_target_pairs={{0,5},{1,6},{2,7},{3,8},{4,9},{5,10},{6,11},{7,12},{8,13},{9,14},{... | collective-permute-start | bytes 3080 | tf_op jit(solution)/shard_map/while/body/eval_jaxpr/cond/branch_6_fun/ppermute | solution.py:75
  128.1 11.3 %conditional.22 = (f32[3,128]{1,0:T(4,128)}) conditional(s32[]{:T(128)} %get-tuple-element.906, f32[3,128]{1,0:T(4,128)S(1)} %get-tuple-element.822, f32[3,128]{1,0:T(4,128)S(1)} %get-tuple-element.822, f32[3,128]{1,0:T(4,128)S(1)} %get-tuple-element.822, f32[3,128]{1,0:T(4,128)S(1)} %get-tuple-element.822, ...), branch_computations={%region_20.20_spmd, %region_21.21_spmd, %region_22.22_spmd, %regio... | conditional | bytes 6192 | solution.py:80
  128.1 8.3 %collective-permute-start.25 = (f32[3,128]{1,0:T(4,128)S(1)}, f32[3,128]{1,0:T(4,128)}, u32[]{:S(2)}, u32[]{:S(2)}) collective-permute-start(f32[3,128]{1,0:T(4,128)S(1)} %param.17), channel_id=1, source_target_pairs={{0,8},{1,7},{2,6},{3,5},{4,4},{5,3},{6,2},{7,1},{8,0},{9,63},{10,6... | collective-permute-start | bytes 4616 | tf_op jit(solution)/shard_map/while/body/eval_jaxpr/cond/branch_1_fun/ppermute | solution.py:68
  139.4 27.2 %conditional.23 = (f32[3,128]{1,0:T(4,128)}, f32[3,128]{1,0:T(4,128)}) conditional(s32[]{:T(128)} %get-tuple-element.907, f32[3,128]{1,0:T(4,128)} %get-tuple-element.921, f32[3,128]{1,0:T(4,128)} %get-tuple-element.921, f32[3,128]{1,0:T(4,128)} %get-tuple-element.921, f32[3,128]{1,0:T(4,128)} %get-tuple-element.921, ...), branch_computations={%region_28.28_spmd, %region_29.29_spmd, %region_30.30_spmd, %regio... | conditional | bytes 12384 | solution.py:81
  139.4 8.3 %collective-permute-start.44 = (f32[3,128]{1,0:T(4,128)}, f32[3,128]{1,0:T(4,128)}, u32[]{:S(2)}, u32[]{:S(2)}) collective-permute-start(f32[3,128]{1,0:T(4,128)} %param.30), channel_id=1, source_target_pairs={{0,6},{1,7},{2,8},{3,9},{4,10},{5,11},{6,12},{7,13},{8,14},{9,15},... | collective-permute-start | bytes 4616 | tf_op jit(solution)/shard_map/while/body/eval_jaxpr/cond/branch_6_fun/ppermute | solution.py:74
  147.7 17.5 %collective-permute-start.45 = (f32[3,128]{1,0:T(4,128)}, f32[3,128]{1,0:T(4,128)}, u32[]{:S(2)}, u32[]{:S(2)}) collective-permute-start(f32[3,128]{1,0:T(4,128)} %param.30), channel_id=1, source_target_pairs={{0,5},{1,6},{2,7},{3,8},{4,9},{5,10},{6,11},{7,12},{8,13},{9,14},{... | collective-permute-start | bytes 4616 | tf_op jit(solution)/shard_map/while/body/eval_jaxpr/cond/branch_6_fun/ppermute | solution.py:75
  179.1 4.7 collective-permute-done.54
  192.7 11.5 %conditional.20 = (f32[2,128]{1,0:T(2,128)}) conditional(s32[]{:T(128)} %get-tuple-element.906, f32[2,128]{1,0:T(2,128)} %bitcast.160, f32[2,128]{1,0:T(2,128)} %bitcast.160, f32[2,128]{1,0:T(2,128)} %bitcast.160, f32[2,128]{1,0:T(2,128)} %bitcast.160, f32[2,128]{1,0:T(2,128)} %bitcast.160, ...), branch_computations={%region_4.4_spmd, %region_5.5_spmd, %region_6.6_spmd, %region_7.7_... | conditional | bytes 4144 | solution.py:80
  192.7 8.5 %collective-permute-start.1 = (f32[2,128]{1,0:T(2,128)}, f32[2,128]{1,0:T(2,128)}, u32[]{:S(2)}, u32[]{:S(2)}) collective-permute-start(f32[2,128]{1,0:T(2,128)} %param.1), channel_id=1, source_target_pairs={{0,8},{1,7},{2,6},{3,5},{4,4},{5,3},{6,2},{7,1},{8,0},{9,63},{10,6... | collective-permute-start | bytes 3080 | tf_op jit(solution)/shard_map/while/body/eval_jaxpr/cond/branch_1_fun/ppermute | solution.py:68
  204.2 27.2 %conditional.21 = (f32[2,128]{1,0:T(2,128)}, f32[2,128]{1,0:T(2,128)}) conditional(s32[]{:T(128)} %get-tuple-element.907, f32[2,128]{1,0:T(2,128)} %get-tuple-element.920, f32[2,128]{1,0:T(2,128)} %get-tuple-element.920, f32[2,128]{1,0:T(2,128)} %get-tuple-element.920, f32[2,128]{1,0:T(2,128)} %get-tuple-element.920, ...), branch_computations={%region_12.12_spmd, %region_13.13_spmd, %region_14.14_spmd, %regio... | conditional | bytes 8288 | solution.py:81
  204.2 8.5 %collective-permute-start.20 = (f32[2,128]{1,0:T(2,128)}, f32[2,128]{1,0:T(2,128)}, u32[]{:S(2)}, u32[]{:S(2)}) collective-permute-start(f32[2,128]{1,0:T(2,128)} %param.14), channel_id=1, source_target_pairs={{0,6},{1,7},{2,8},{3,9},{4,10},{5,11},{6,12},{7,13},{8,14},{9,15},... | collective-permute-start | bytes 3080 | tf_op jit(solution)/shard_map/while/body/eval_jaxpr/cond/branch_6_fun/ppermute | solution.py:74
  212.8 17.2 %collective-permute-start.21 = (f32[2,128]{1,0:T(2,128)}, f32[2,128]{1,0:T(2,128)}, u32[]{:S(2)}, u32[]{:S(2)}) collective-permute-start(f32[2,128]{1,0:T(2,128)} %param.14), channel_id=1, source_target_pairs={{0,5},{1,6},{2,7},{3,8},{4,9},{5,10},{6,11},{7,12},{8,13},{9,14},{... | collective-permute-start | bytes 3080 | tf_op jit(solution)/shard_map/while/body/eval_jaxpr/cond/branch_6_fun/ppermute | solution.py:75
  237.9 11.3 %conditional.22 = (f32[3,128]{1,0:T(4,128)}) conditional(s32[]{:T(128)} %get-tuple-element.906, f32[3,128]{1,0:T(4,128)S(1)} %get-tuple-element.822, f32[3,128]{1,0:T(4,128)S(1)} %get-tuple-element.822, f32[3,128]{1,0:T(4,128)S(1)} %get-tuple-element.822, f32[3,128]{1,0:T(4,128)S(1)} %get-tuple-element.822, ...), branch_computations={%region_20.20_spmd, %region_21.21_spmd, %region_22.22_spmd, %regio... | conditional | bytes 6192 | solution.py:80
  238.0 8.3 %collective-permute-start.25 = (f32[3,128]{1,0:T(4,128)S(1)}, f32[3,128]{1,0:T(4,128)}, u32[]{:S(2)}, u32[]{:S(2)}) collective-permute-start(f32[3,128]{1,0:T(4,128)S(1)} %param.17), channel_id=1, source_target_pairs={{0,8},{1,7},{2,6},{3,5},{4,4},{5,3},{6,2},{7,1},{8,0},{9,63},{10,6... | collective-permute-start | bytes 4616 | tf_op jit(solution)/shard_map/while/body/eval_jaxpr/cond/branch_1_fun/ppermute | solution.py:68
  249.3 27.2 %conditional.23 = (f32[3,128]{1,0:T(4,128)}, f32[3,128]{1,0:T(4,128)}) conditional(s32[]{:T(128)} %get-tuple-element.907, f32[3,128]{1,0:T(4,128)} %get-tuple-element.921, f32[3,128]{1,0:T(4,128)} %get-tuple-element.921, f32[3,128]{1,0:T(4,128)} %get-tuple-element.921, f32[3,128]{1,0:T(4,128)} %get-tuple-element.921, ...), branch_computations={%region_28.28_spmd, %region_29.29_spmd, %region_30.30_spmd, %regio... | conditional | bytes 12384 | solution.py:81
  249.3 8.3 %collective-permute-start.44 = (f32[3,128]{1,0:T(4,128)}, f32[3,128]{1,0:T(4,128)}, u32[]{:S(2)}, u32[]{:S(2)}) collective-permute-start(f32[3,128]{1,0:T(4,128)} %param.30), channel_id=1, source_target_pairs={{0,6},{1,7},{2,8},{3,9},{4,10},{5,11},{6,12},{7,13},{8,14},{9,15},... | collective-permute-start | bytes 4616 | tf_op jit(solution)/shard_map/while/body/eval_jaxpr/cond/branch_6_fun/ppermute | solution.py:74
  257.5 17.5 %collective-permute-start.45 = (f32[3,128]{1,0:T(4,128)}, f32[3,128]{1,0:T(4,128)}, u32[]{:S(2)}, u32[]{:S(2)}) collective-permute-start(f32[3,128]{1,0:T(4,128)} %param.30), channel_id=1, source_target_pairs={{0,5},{1,6},{2,7},{3,8},{4,9},{5,10},{6,11},{7,12},{8,13},{9,14},{... | collective-permute-start | bytes 4616 | tf_op jit(solution)/shard_map/while/body/eval_jaxpr/cond/branch_6_fun/ppermute | solution.py:75
  289.0 4.7 collective-permute-done.54
  302.6 11.5 %conditional.20 = (f32[2,128]{1,0:T(2,128)}) conditional(s32[]{:T(128)} %get-tuple-element.906, f32[2,128]{1,0:T(2,128)} %bitcast.160, f32[2,128]{1,0:T(2,128)} %bitcast.160, f32[2,128]{1,0:T(2,128)} %bitcast.160, f32[2,128]{1,0:T(2,128)} %bitcast.160, f32[2,128]{1,0:T(2,128)} %bitcast.160, ...), branch_computations={%region_4.4_spmd, %region_5.5_spmd, %region_6.6_spmd, %region_7.7_... | conditional | bytes 4144 | solution.py:80
  302.6 8.5 %collective-permute-start.1 = (f32[2,128]{1,0:T(2,128)}, f32[2,128]{1,0:T(2,128)}, u32[]{:S(2)}, u32[]{:S(2)}) collective-permute-start(f32[2,128]{1,0:T(2,128)} %param.1), channel_id=1, source_target_pairs={{0,8},{1,7},{2,6},{3,5},{4,4},{5,3},{6,2},{7,1},{8,0},{9,63},{10,6... | collective-permute-start | bytes 3080 | tf_op jit(solution)/shard_map/while/body/eval_jaxpr/cond/branch_1_fun/ppermute | solution.py:68
  314.1 27.2 %conditional.21 = (f32[2,128]{1,0:T(2,128)}, f32[2,128]{1,0:T(2,128)}) conditional(s32[]{:T(128)} %get-tuple-element.907, f32[2,128]{1,0:T(2,128)} %get-tuple-element.920, f32[2,128]{1,0:T(2,128)} %get-tuple-element.920, f32[2,128]{1,0:T(2,128)} %get-tuple-element.920, f32[2,128]{1,0:T(2,128)} %get-tuple-element.920, ...), branch_computations={%region_12.12_spmd, %region_13.13_spmd, %region_14.14_spmd, %regio... | conditional | bytes 8288 | solution.py:81
  314.1 8.5 %collective-permute-start.20 = (f32[2,128]{1,0:T(2,128)}, f32[2,128]{1,0:T(2,128)}, u32[]{:S(2)}, u32[]{:S(2)}) collective-permute-start(f32[2,128]{1,0:T(2,128)} %param.14), channel_id=1, source_target_pairs={{0,6},{1,7},{2,8},{3,9},{4,10},{5,11},{6,12},{7,13},{8,14},{9,15},... | collective-permute-start | bytes 3080 | tf_op jit(solution)/shard_map/while/body/eval_jaxpr/cond/branch_6_fun/ppermute | solution.py:74
  322.6 17.2 %collective-permute-start.21 = (f32[2,128]{1,0:T(2,128)}, f32[2,128]{1,0:T(2,128)}, u32[]{:S(2)}, u32[]{:S(2)}) collective-permute-start(f32[2,128]{1,0:T(2,128)} %param.14), channel_id=1, source_target_pairs={{0,5},{1,6},{2,7},{3,8},{4,9},{5,10},{6,11},{7,12},{8,13},{9,14},{... | collective-permute-start | bytes 3080 | tf_op jit(solution)/shard_map/while/body/eval_jaxpr/cond/branch_6_fun/ppermute | solution.py:75
  347.8 11.3 %conditional.22 = (f32[3,128]{1,0:T(4,128)}) conditional(s32[]{:T(128)} %get-tuple-element.906, f32[3,128]{1,0:T(4,128)S(1)} %get-tuple-element.822, f32[3,128]{1,0:T(4,128)S(1)} %get-tuple-element.822, f32[3,128]{1,0:T(4,128)S(1)} %get-tuple-element.822, f32[3,128]{1,0:T(4,128)S(1)} %get-tuple-element.822, ...), branch_computations={%region_20.20_spmd, %region_21.21_spmd, %region_22.22_spmd, %regio... | conditional | bytes 6192 | solution.py:80
  347.9 8.3 %collective-permute-start.25 = (f32[3,128]{1,0:T(4,128)S(1)}, f32[3,128]{1,0:T(4,128)}, u32[]{:S(2)}, u32[]{:S(2)}) collective-permute-start(f32[3,128]{1,0:T(4,128)S(1)} %param.17), channel_id=1, source_target_pairs={{0,8},{1,7},{2,6},{3,5},{4,4},{5,3},{6,2},{7,1},{8,0},{9,63},{10,6... | collective-permute-start | bytes 4616 | tf_op jit(solution)/shard_map/while/body/eval_jaxpr/cond/branch_1_fun/ppermute | solution.py:68
  359.1 27.2 %conditional.23 = (f32[3,128]{1,0:T(4,128)}, f32[3,128]{1,0:T(4,128)}) conditional(s32[]{:T(128)} %get-tuple-element.907, f32[3,128]{1,0:T(4,128)} %get-tuple-element.921, f32[3,128]{1,0:T(4,128)} %get-tuple-element.921, f32[3,128]{1,0:T(4,128)} %get-tuple-element.921, f32[3,128]{1,0:T(4,128)} %get-tuple-element.921, ...), branch_computations={%region_28.28_spmd, %region_29.29_spmd, %region_30.30_spmd, %regio... | conditional | bytes 12384 | solution.py:81
  359.1 8.3 %collective-permute-start.44 = (f32[3,128]{1,0:T(4,128)}, f32[3,128]{1,0:T(4,128)}, u32[]{:S(2)}, u32[]{:S(2)}) collective-permute-start(f32[3,128]{1,0:T(4,128)} %param.30), channel_id=1, source_target_pairs={{0,6},{1,7},{2,8},{3,9},{4,10},{5,11},{6,12},{7,13},{8,14},{9,15},... | collective-permute-start | bytes 4616 | tf_op jit(solution)/shard_map/while/body/eval_jaxpr/cond/branch_6_fun/ppermute | solution.py:74
  367.4 17.5 %collective-permute-start.45 = (f32[3,128]{1,0:T(4,128)}, f32[3,128]{1,0:T(4,128)}, u32[]{:S(2)}, u32[]{:S(2)}) collective-permute-start(f32[3,128]{1,0:T(4,128)} %param.30), channel_id=1, source_target_pairs={{0,5},{1,6},{2,7},{3,8},{4,9},{5,10},{6,11},{7,12},{8,13},{9,14},{... | collective-permute-start | bytes 4616 | tf_op jit(solution)/shard_map/while/body/eval_jaxpr/cond/branch_6_fun/ppermute | solution.py:75
  398.9 4.7 collective-permute-done.54
  412.5 11.5 %conditional.20 = (f32[2,128]{1,0:T(2,128)}) conditional(s32[]{:T(128)} %get-tuple-element.906, f32[2,128]{1,0:T(2,128)} %bitcast.160, f32[2,128]{1,0:T(2,128)} %bitcast.160, f32[2,128]{1,0:T(2,128)} %bitcast.160, f32[2,128]{1,0:T(2,128)} %bitcast.160, f32[2,128]{1,0:T(2,128)} %bitcast.160, ...), branch_computations={%region_4.4_spmd, %region_5.5_spmd, %region_6.6_spmd, %region_7.7_... | conditional | bytes 4144 | solution.py:80
  412.5 8.5 %collective-permute-start.1 = (f32[2,128]{1,0:T(2,128)}, f32[2,128]{1,0:T(2,128)}, u32[]{:S(2)}, u32[]{:S(2)}) collective-permute-start(f32[2,128]{1,0:T(2,128)} %param.1), channel_id=1, source_target_pairs={{0,8},{1,7},{2,6},{3,5},{4,4},{5,3},{6,2},{7,1},{8,0},{9,63},{10,6... | collective-permute-start | bytes 3080 | tf_op jit(solution)/shard_map/while/body/eval_jaxpr/cond/branch_1_fun/ppermute | solution.py:68
  424.0 27.2 %conditional.21 = (f32[2,128]{1,0:T(2,128)}, f32[2,128]{1,0:T(2,128)}) conditional(s32[]{:T(128)} %get-tuple-element.907, f32[2,128]{1,0:T(2,128)} %get-tuple-element.920, f32[2,128]{1,0:T(2,128)} %get-tuple-element.920, f32[2,128]{1,0:T(2,128)} %get-tuple-element.920, f32[2,128]{1,0:T(2,128)} %get-tuple-element.920, ...), branch_computations={%region_12.12_spmd, %region_13.13_spmd, %region_14.14_spmd, %regio... | conditional | bytes 8288 | solution.py:81
  424.0 8.5 %collective-permute-start.20 = (f32[2,128]{1,0:T(2,128)}, f32[2,128]{1,0:T(2,128)}, u32[]{:S(2)}, u32[]{:S(2)}) collective-permute-start(f32[2,128]{1,0:T(2,128)} %param.14), channel_id=1, source_target_pairs={{0,6},{1,7},{2,8},{3,9},{4,10},{5,11},{6,12},{7,13},{8,14},{9,15},... | collective-permute-start | bytes 3080 | tf_op jit(solution)/shard_map/while/body/eval_jaxpr/cond/branch_6_fun/ppermute | solution.py:74
  432.5 17.2 %collective-permute-start.21 = (f32[2,128]{1,0:T(2,128)}, f32[2,128]{1,0:T(2,128)}, u32[]{:S(2)}, u32[]{:S(2)}) collective-permute-start(f32[2,128]{1,0:T(2,128)} %param.14), channel_id=1, source_target_pairs={{0,5},{1,6},{2,7},{3,8},{4,9},{5,10},{6,11},{7,12},{8,13},{9,14},{... | collective-permute-start | bytes 3080 | tf_op jit(solution)/shard_map/while/body/eval_jaxpr/cond/branch_6_fun/ppermute | solution.py:75
  457.7 11.3 %conditional.22 = (f32[3,128]{1,0:T(4,128)}) conditional(s32[]{:T(128)} %get-tuple-element.906, f32[3,128]{1,0:T(4,128)S(1)} %get-tuple-element.822, f32[3,128]{1,0:T(4,128)S(1)} %get-tuple-element.822, f32[3,128]{1,0:T(4,128)S(1)} %get-tuple-element.822, f32[3,128]{1,0:T(4,128)S(1)} %get-tuple-element.822, ...), branch_computations={%region_20.20_spmd, %region_21.21_spmd, %region_22.22_spmd, %regio... | conditional | bytes 6192 | solution.py:80
  457.7 8.3 %collective-permute-start.25 = (f32[3,128]{1,0:T(4,128)S(1)}, f32[3,128]{1,0:T(4,128)}, u32[]{:S(2)}, u32[]{:S(2)}) collective-permute-start(f32[3,128]{1,0:T(4,128)S(1)} %param.17), channel_id=1, source_target_pairs={{0,8},{1,7},{2,6},{3,5},{4,4},{5,3},{6,2},{7,1},{8,0},{9,63},{10,6... | collective-permute-start | bytes 4616 | tf_op jit(solution)/shard_map/while/body/eval_jaxpr/cond/branch_1_fun/ppermute | solution.py:68
  469.0 27.2 %conditional.23 = (f32[3,128]{1,0:T(4,128)}, f32[3,128]{1,0:T(4,128)}) conditional(s32[]{:T(128)} %get-tuple-element.907, f32[3,128]{1,0:T(4,128)} %get-tuple-element.921, f32[3,128]{1,0:T(4,128)} %get-tuple-element.921, f32[3,128]{1,0:T(4,128)} %get-tuple-element.921, f32[3,128]{1,0:T(4,128)} %get-tuple-element.921, ...), branch_computations={%region_28.28_spmd, %region_29.29_spmd, %region_30.30_spmd, %regio... | conditional | bytes 12384 | solution.py:81
  469.0 8.3 %collective-permute-start.44 = (f32[3,128]{1,0:T(4,128)}, f32[3,128]{1,0:T(4,128)}, u32[]{:S(2)}, u32[]{:S(2)}) collective-permute-start(f32[3,128]{1,0:T(4,128)} %param.30), channel_id=1, source_target_pairs={{0,6},{1,7},{2,8},{3,9},{4,10},{5,11},{6,12},{7,13},{8,14},{9,15},... | collective-permute-start | bytes 4616 | tf_op jit(solution)/shard_map/while/body/eval_jaxpr/cond/branch_6_fun/ppermute | solution.py:74
  477.3 17.5 %collective-permute-start.45 = (f32[3,128]{1,0:T(4,128)}, f32[3,128]{1,0:T(4,128)}, u32[]{:S(2)}, u32[]{:S(2)}) collective-permute-start(f32[3,128]{1,0:T(4,128)} %param.30), channel_id=1, source_target_pairs={{0,5},{1,6},{2,7},{3,8},{4,9},{5,10},{6,11},{7,12},{8,13},{9,14},{... | collective-permute-start | bytes 4616 | tf_op jit(solution)/shard_map/while/body/eval_jaxpr/cond/branch_6_fun/ppermute | solution.py:75
  508.8 4.7 collective-permute-done.54
  (265 shorter events, 153.7 us)
Async XLA Ops:
  4.1 70.3 %all-to-all-start = ((f32[64,1,1026]{2,1,0:T(1,128)}), f32[64,1,1026]{2,1,0:T(1,128)S(1)}, u32[]{:S(2)}, u32[]{:S(2)}) async-start(f32[64,1,1026]{2,1,0:T(1,128)} %copy.161), calls=%async_computation | async-start | bytes 589824 | tf_op jit(solution)/shard_map/all_to_all | solution.py:48
  76.0 51.3 %collective-permute-start.50 = (f32[2,1,128]{2,0,1:T(2,128)S(1)}, f32[2,1,128]{2,0,1:T(2,128)S(1)}, u32[]{:S(2)}, u32[]{:S(2)}) collective-permute-start(f32[2,1,128]{2,0,1:T(2,128)S(1)} %slice.676), channel_id=1, source_target_pairs={{64,0},{128,64},{192,128},{256,192},{320,256},{384,320},{448,384},... | collective-permute-start | bytes 3080 | tf_op jit(solution)/shard_map/while/body/eval_jaxpr/ppermute | solution.py:91
  78.1 46.3 %collective-permute-start.48 = (f32[2,64,1]{1,0,2:T(2,128)S(1)}, f32[2,64,1]{1,0,2:T(2,128)S(1)}, u32[]{:S(2)}, u32[]{:S(2)}) collective-permute-start(f32[2,64,1]{1,0,2:T(2,128)S(1)} %get-tuple-element.808), channel_id=1, source_target_pairs={{0,1},{1,2},{2,3},{3,4},{4,5},{5,6},{6,7},{7,8},{8,9},{9,10},{10,1... | collective-permute-start | bytes 1544 | tf_op jit(solution)/shard_map/while/body/eval_jaxpr/ppermute | solution.py:92
  84.4 43.0 %collective-permute-start.51 = (f32[2,1,128]{2,1,0:T(1,128)}, f32[2,1,128]{2,1,0:T(1,128)S(1)}, u32[]{:S(2)}, u32[]{:S(2)}) collective-permute-start(f32[2,1,128]{2,1,0:T(1,128)} %slice.677), channel_id=1, source_target_pairs={{0,64},{64,128},{128,192},{192,256},{256,320},{320,384},{384,448},... | collective-permute-start | bytes 3080 | tf_op jit(solution)/shard_map/while/body/eval_jaxpr/ppermute | solution.py:90
  86.3 11.5 %collective-permute-start.1 = (f32[2,128]{1,0:T(2,128)}, f32[2,128]{1,0:T(2,128)}, u32[]{:S(2)}, u32[]{:S(2)}) collective-permute-start(f32[2,128]{1,0:T(2,128)} %param.1), channel_id=1, source_target_pairs={{0,8},{1,7},{2,6},{3,5},{4,4},{5,3},{6,2},{7,1},{8,0},{9,63},{10,6... | collective-permute-start | bytes 3080 | tf_op jit(solution)/shard_map/while/body/eval_jaxpr/cond/branch_1_fun/ppermute | solution.py:68
  97.9 22.2 %collective-permute-start.20 = (f32[2,128]{1,0:T(2,128)}, f32[2,128]{1,0:T(2,128)}, u32[]{:S(2)}, u32[]{:S(2)}) collective-permute-start(f32[2,128]{1,0:T(2,128)} %param.14), channel_id=1, source_target_pairs={{0,6},{1,7},{2,8},{3,9},{4,10},{5,11},{6,12},{7,13},{8,14},{9,15},... | collective-permute-start | bytes 3080 | tf_op jit(solution)/shard_map/while/body/eval_jaxpr/cond/branch_6_fun/ppermute | solution.py:74
  102.2 19.3 %collective-permute-start.21 = (f32[2,128]{1,0:T(2,128)}, f32[2,128]{1,0:T(2,128)}, u32[]{:S(2)}, u32[]{:S(2)}) collective-permute-start(f32[2,128]{1,0:T(2,128)} %param.14), channel_id=1, source_target_pairs={{0,5},{1,6},{2,7},{3,8},{4,9},{5,10},{6,11},{7,12},{8,13},{9,14},{... | collective-permute-start | bytes 3080 | tf_op jit(solution)/shard_map/while/body/eval_jaxpr/cond/branch_6_fun/ppermute | solution.py:75
  128.1 11.3 %collective-permute-start.25 = (f32[3,128]{1,0:T(4,128)S(1)}, f32[3,128]{1,0:T(4,128)}, u32[]{:S(2)}, u32[]{:S(2)}) collective-permute-start(f32[3,128]{1,0:T(4,128)S(1)} %param.17), channel_id=1, source_target_pairs={{0,8},{1,7},{2,6},{3,5},{4,4},{5,3},{6,2},{7,1},{8,0},{9,63},{10,6... | collective-permute-start | bytes 4616 | tf_op jit(solution)/shard_map/while/body/eval_jaxpr/cond/branch_1_fun/ppermute | solution.py:68
  139.4 25.7 %collective-permute-start.44 = (f32[3,128]{1,0:T(4,128)}, f32[3,128]{1,0:T(4,128)}, u32[]{:S(2)}, u32[]{:S(2)}) collective-permute-start(f32[3,128]{1,0:T(4,128)} %param.30), channel_id=1, source_target_pairs={{0,6},{1,7},{2,8},{3,9},{4,10},{5,11},{6,12},{7,13},{8,14},{9,15},... | collective-permute-start | bytes 4616 | tf_op jit(solution)/shard_map/while/body/eval_jaxpr/cond/branch_6_fun/ppermute | solution.py:74
  147.7 19.0 %collective-permute-start.45 = (f32[3,128]{1,0:T(4,128)}, f32[3,128]{1,0:T(4,128)}, u32[]{:S(2)}, u32[]{:S(2)}) collective-permute-start(f32[3,128]{1,0:T(4,128)} %param.30), channel_id=1, source_target_pairs={{0,5},{1,6},{2,7},{3,8},{4,9},{5,10},{6,11},{7,12},{8,13},{9,14},{... | collective-permute-start | bytes 4616 | tf_op jit(solution)/shard_map/while/body/eval_jaxpr/cond/branch_6_fun/ppermute | solution.py:75
  166.6 10.6 %collective-permute-start.53 = (f32[3,1,128]{2,0,1:T(4,128)S(1)}, f32[3,1,128]{2,0,1:T(4,128)S(1)}, u32[]{:S(2)}, u32[]{:S(2)}) collective-permute-start(f32[3,1,128]{2,0,1:T(4,128)S(1)} %get-tuple-element.821), channel_id=1, source_target_pairs={{64,0},{128,64},{192,128},{256,192},{320,256},{384,320},{448,384},... | collective-permute-start | bytes 4616 | tf_op jit(solution)/shard_map/while/body/eval_jaxpr/ppermute | solution.py:91
  169.4 7.8 %collective-permute-start.52 = (f32[3,64,1]{2,0,1:T(4,128)S(1)}, f32[3,64,1]{2,0,1:T(4,128)S(1)}, u32[]{:S(2)}, u32[]{:S(2)}) collective-permute-start(f32[3,64,1]{2,0,1:T(4,128)S(1)} %get-tuple-element.820), channel_id=1, source_target_pairs={{0,63},{1,0},{2,1},{3,2},{4,3},{5,4},{6,5},{7,6},{8,7},{9,8},{10,9... | collective-permute-start | bytes 2312 | tf_op jit(solution)/shard_map/while/body/eval_jaxpr/ppermute | solution.py:93
  175.3 8.5 %collective-permute-start.54 = (f32[3,1,128]{2,0,1:T(4,128)S(1)}, f32[3,1,128]{2,0,1:T(4,128)S(1)}, u32[]{:S(2)}, u32[]{:S(2)}) collective-permute-start(f32[3,1,128]{2,0,1:T(4,128)S(1)} %get-tuple-element.825), channel_id=1, source_target_pairs={{0,64},{64,128},{128,192},{192,256},{256,320},{320,384},{384,448},... | collective-permute-start | bytes 4616 | tf_op jit(solution)/shard_map/while/body/eval_jaxpr/ppermute | solution.py:90
  185.8 51.5 %collective-permute-start.50 = (f32[2,1,128]{2,0,1:T(2,128)S(1)}, f32[2,1,128]{2,0,1:T(2,128)S(1)}, u32[]{:S(2)}, u32[]{:S(2)}) collective-permute-start(f32[2,1,128]{2,0,1:T(2,128)S(1)} %slice.676), channel_id=1, source_target_pairs={{64,0},{128,64},{192,128},{256,192},{320,256},{384,320},{448,384},... | collective-permute-start | bytes 3080 | tf_op jit(solution)/shard_map/while/body/eval_jaxpr/ppermute | solution.py:91
  187.8 46.4 %collective-permute-start.48 = (f32[2,64,1]{1,0,2:T(2,128)S(1)}, f32[2,64,1]{1,0,2:T(2,128)S(1)}, u32[]{:S(2)}, u32[]{:S(2)}) collective-permute-start(f32[2,64,1]{1,0,2:T(2,128)S(1)} %get-tuple-element.808), channel_id=1, source_target_pairs={{0,1},{1,2},{2,3},{3,4},{4,5},{5,6},{6,7},{7,8},{8,9},{9,10},{10,1... | collective-permute-start | bytes 1544 | tf_op jit(solution)/shard_map/while/body/eval_jaxpr/ppermute | solution.py:92
  190.3 47.0 %collective-permute-start.51 = (f32[2,1,128]{2,1,0:T(1,128)}, f32[2,1,128]{2,1,0:T(1,128)S(1)}, u32[]{:S(2)}, u32[]{:S(2)}) collective-permute-start(f32[2,1,128]{2,1,0:T(1,128)} %slice.677), channel_id=1, source_target_pairs={{0,64},{64,128},{128,192},{192,256},{256,320},{320,384},{384,448},... | collective-permute-start | bytes 3080 | tf_op jit(solution)/shard_map/while/body/eval_jaxpr/ppermute | solution.py:90
  192.7 11.5 %collective-permute-start.1 = (f32[2,128]{1,0:T(2,128)}, f32[2,128]{1,0:T(2,128)}, u32[]{:S(2)}, u32[]{:S(2)}) collective-permute-start(f32[2,128]{1,0:T(2,128)} %param.1), channel_id=1, source_target_pairs={{0,8},{1,7},{2,6},{3,5},{4,4},{5,3},{6,2},{7,1},{8,0},{9,63},{10,6... | collective-permute-start | bytes 3080 | tf_op jit(solution)/shard_map/while/body/eval_jaxpr/cond/branch_1_fun/ppermute | solution.py:68
  204.2 25.8 %collective-permute-start.20 = (f32[2,128]{1,0:T(2,128)}, f32[2,128]{1,0:T(2,128)}, u32[]{:S(2)}, u32[]{:S(2)}) collective-permute-start(f32[2,128]{1,0:T(2,128)} %param.14), channel_id=1, source_target_pairs={{0,6},{1,7},{2,8},{3,9},{4,10},{5,11},{6,12},{7,13},{8,14},{9,15},... | collective-permute-start | bytes 3080 | tf_op jit(solution)/shard_map/while/body/eval_jaxpr/cond/branch_6_fun/ppermute | solution.py:74
  212.8 18.7 %collective-permute-start.21 = (f32[2,128]{1,0:T(2,128)}, f32[2,128]{1,0:T(2,128)}, u32[]{:S(2)}, u32[]{:S(2)}) collective-permute-start(f32[2,128]{1,0:T(2,128)} %param.14), channel_id=1, source_target_pairs={{0,5},{1,6},{2,7},{3,8},{4,9},{5,10},{6,11},{7,12},{8,13},{9,14},{... | collective-permute-start | bytes 3080 | tf_op jit(solution)/shard_map/while/body/eval_jaxpr/cond/branch_6_fun/ppermute | solution.py:75
  238.0 11.3 %collective-permute-start.25 = (f32[3,128]{1,0:T(4,128)S(1)}, f32[3,128]{1,0:T(4,128)}, u32[]{:S(2)}, u32[]{:S(2)}) collective-permute-start(f32[3,128]{1,0:T(4,128)S(1)} %param.17), channel_id=1, source_target_pairs={{0,8},{1,7},{2,6},{3,5},{4,4},{5,3},{6,2},{7,1},{8,0},{9,63},{10,6... | collective-permute-start | bytes 4616 | tf_op jit(solution)/shard_map/while/body/eval_jaxpr/cond/branch_1_fun/ppermute | solution.py:68
  249.3 25.7 %collective-permute-start.44 = (f32[3,128]{1,0:T(4,128)}, f32[3,128]{1,0:T(4,128)}, u32[]{:S(2)}, u32[]{:S(2)}) collective-permute-start(f32[3,128]{1,0:T(4,128)} %param.30), channel_id=1, source_target_pairs={{0,6},{1,7},{2,8},{3,9},{4,10},{5,11},{6,12},{7,13},{8,14},{9,15},... | collective-permute-start | bytes 4616 | tf_op jit(solution)/shard_map/while/body/eval_jaxpr/cond/branch_6_fun/ppermute | solution.py:74
  257.5 19.0 %collective-permute-start.45 = (f32[3,128]{1,0:T(4,128)}, f32[3,128]{1,0:T(4,128)}, u32[]{:S(2)}, u32[]{:S(2)}) collective-permute-start(f32[3,128]{1,0:T(4,128)} %param.30), channel_id=1, source_target_pairs={{0,5},{1,6},{2,7},{3,8},{4,9},{5,10},{6,11},{7,12},{8,13},{9,14},{... | collective-permute-start | bytes 4616 | tf_op jit(solution)/shard_map/while/body/eval_jaxpr/cond/branch_6_fun/ppermute | solution.py:75
  276.5 10.6 %collective-permute-start.53 = (f32[3,1,128]{2,0,1:T(4,128)S(1)}, f32[3,1,128]{2,0,1:T(4,128)S(1)}, u32[]{:S(2)}, u32[]{:S(2)}) collective-permute-start(f32[3,1,128]{2,0,1:T(4,128)S(1)} %get-tuple-element.821), channel_id=1, source_target_pairs={{64,0},{128,64},{192,128},{256,192},{320,256},{384,320},{448,384},... | collective-permute-start | bytes 4616 | tf_op jit(solution)/shard_map/while/body/eval_jaxpr/ppermute | solution.py:91
  279.3 7.8 %collective-permute-start.52 = (f32[3,64,1]{2,0,1:T(4,128)S(1)}, f32[3,64,1]{2,0,1:T(4,128)S(1)}, u32[]{:S(2)}, u32[]{:S(2)}) collective-permute-start(f32[3,64,1]{2,0,1:T(4,128)S(1)} %get-tuple-element.820), channel_id=1, source_target_pairs={{0,63},{1,0},{2,1},{3,2},{4,3},{5,4},{6,5},{7,6},{8,7},{9,8},{10,9... | collective-permute-start | bytes 2312 | tf_op jit(solution)/shard_map/while/body/eval_jaxpr/ppermute | solution.py:93
  285.1 8.5 %collective-permute-start.54 = (f32[3,1,128]{2,0,1:T(4,128)S(1)}, f32[3,1,128]{2,0,1:T(4,128)S(1)}, u32[]{:S(2)}, u32[]{:S(2)}) collective-permute-start(f32[3,1,128]{2,0,1:T(4,128)S(1)} %get-tuple-element.825), channel_id=1, source_target_pairs={{0,64},{64,128},{128,192},{192,256},{256,320},{320,384},{384,448},... | collective-permute-start | bytes 4616 | tf_op jit(solution)/shard_map/while/body/eval_jaxpr/ppermute | solution.py:90
  295.6 51.5 %collective-permute-start.50 = (f32[2,1,128]{2,0,1:T(2,128)S(1)}, f32[2,1,128]{2,0,1:T(2,128)S(1)}, u32[]{:S(2)}, u32[]{:S(2)}) collective-permute-start(f32[2,1,128]{2,0,1:T(2,128)S(1)} %slice.676), channel_id=1, source_target_pairs={{64,0},{128,64},{192,128},{256,192},{320,256},{384,320},{448,384},... | collective-permute-start | bytes 3080 | tf_op jit(solution)/shard_map/while/body/eval_jaxpr/ppermute | solution.py:91
  297.7 46.4 %collective-permute-start.48 = (f32[2,64,1]{1,0,2:T(2,128)S(1)}, f32[2,64,1]{1,0,2:T(2,128)S(1)}, u32[]{:S(2)}, u32[]{:S(2)}) collective-permute-start(f32[2,64,1]{1,0,2:T(2,128)S(1)} %get-tuple-element.808), channel_id=1, source_target_pairs={{0,1},{1,2},{2,3},{3,4},{4,5},{5,6},{6,7},{7,8},{8,9},{9,10},{10,1... | collective-permute-start | bytes 1544 | tf_op jit(solution)/shard_map/while/body/eval_jaxpr/ppermute | solution.py:92
  300.2 47.0 %collective-permute-start.51 = (f32[2,1,128]{2,1,0:T(1,128)}, f32[2,1,128]{2,1,0:T(1,128)S(1)}, u32[]{:S(2)}, u32[]{:S(2)}) collective-permute-start(f32[2,1,128]{2,1,0:T(1,128)} %slice.677), channel_id=1, source_target_pairs={{0,64},{64,128},{128,192},{192,256},{256,320},{320,384},{384,448},... | collective-permute-start | bytes 3080 | tf_op jit(solution)/shard_map/while/body/eval_jaxpr/ppermute | solution.py:90
  302.6 11.5 %collective-permute-start.1 = (f32[2,128]{1,0:T(2,128)}, f32[2,128]{1,0:T(2,128)}, u32[]{:S(2)}, u32[]{:S(2)}) collective-permute-start(f32[2,128]{1,0:T(2,128)} %param.1), channel_id=1, source_target_pairs={{0,8},{1,7},{2,6},{3,5},{4,4},{5,3},{6,2},{7,1},{8,0},{9,63},{10,6... | collective-permute-start | bytes 3080 | tf_op jit(solution)/shard_map/while/body/eval_jaxpr/cond/branch_1_fun/ppermute | solution.py:68
  314.1 25.8 %collective-permute-start.20 = (f32[2,128]{1,0:T(2,128)}, f32[2,128]{1,0:T(2,128)}, u32[]{:S(2)}, u32[]{:S(2)}) collective-permute-start(f32[2,128]{1,0:T(2,128)} %param.14), channel_id=1, source_target_pairs={{0,6},{1,7},{2,8},{3,9},{4,10},{5,11},{6,12},{7,13},{8,14},{9,15},... | collective-permute-start | bytes 3080 | tf_op jit(solution)/shard_map/while/body/eval_jaxpr/cond/branch_6_fun/ppermute | solution.py:74
  322.6 18.7 %collective-permute-start.21 = (f32[2,128]{1,0:T(2,128)}, f32[2,128]{1,0:T(2,128)}, u32[]{:S(2)}, u32[]{:S(2)}) collective-permute-start(f32[2,128]{1,0:T(2,128)} %param.14), channel_id=1, source_target_pairs={{0,5},{1,6},{2,7},{3,8},{4,9},{5,10},{6,11},{7,12},{8,13},{9,14},{... | collective-permute-start | bytes 3080 | tf_op jit(solution)/shard_map/while/body/eval_jaxpr/cond/branch_6_fun/ppermute | solution.py:75
  347.9 11.3 %collective-permute-start.25 = (f32[3,128]{1,0:T(4,128)S(1)}, f32[3,128]{1,0:T(4,128)}, u32[]{:S(2)}, u32[]{:S(2)}) collective-permute-start(f32[3,128]{1,0:T(4,128)S(1)} %param.17), channel_id=1, source_target_pairs={{0,8},{1,7},{2,6},{3,5},{4,4},{5,3},{6,2},{7,1},{8,0},{9,63},{10,6... | collective-permute-start | bytes 4616 | tf_op jit(solution)/shard_map/while/body/eval_jaxpr/cond/branch_1_fun/ppermute | solution.py:68
  359.1 25.7 %collective-permute-start.44 = (f32[3,128]{1,0:T(4,128)}, f32[3,128]{1,0:T(4,128)}, u32[]{:S(2)}, u32[]{:S(2)}) collective-permute-start(f32[3,128]{1,0:T(4,128)} %param.30), channel_id=1, source_target_pairs={{0,6},{1,7},{2,8},{3,9},{4,10},{5,11},{6,12},{7,13},{8,14},{9,15},... | collective-permute-start | bytes 4616 | tf_op jit(solution)/shard_map/while/body/eval_jaxpr/cond/branch_6_fun/ppermute | solution.py:74
  367.4 19.0 %collective-permute-start.45 = (f32[3,128]{1,0:T(4,128)}, f32[3,128]{1,0:T(4,128)}, u32[]{:S(2)}, u32[]{:S(2)}) collective-permute-start(f32[3,128]{1,0:T(4,128)} %param.30), channel_id=1, source_target_pairs={{0,5},{1,6},{2,7},{3,8},{4,9},{5,10},{6,11},{7,12},{8,13},{9,14},{... | collective-permute-start | bytes 4616 | tf_op jit(solution)/shard_map/while/body/eval_jaxpr/cond/branch_6_fun/ppermute | solution.py:75
  386.4 10.6 %collective-permute-start.53 = (f32[3,1,128]{2,0,1:T(4,128)S(1)}, f32[3,1,128]{2,0,1:T(4,128)S(1)}, u32[]{:S(2)}, u32[]{:S(2)}) collective-permute-start(f32[3,1,128]{2,0,1:T(4,128)S(1)} %get-tuple-element.821), channel_id=1, source_target_pairs={{64,0},{128,64},{192,128},{256,192},{320,256},{384,320},{448,384},... | collective-permute-start | bytes 4616 | tf_op jit(solution)/shard_map/while/body/eval_jaxpr/ppermute | solution.py:91
  389.2 7.8 %collective-permute-start.52 = (f32[3,64,1]{2,0,1:T(4,128)S(1)}, f32[3,64,1]{2,0,1:T(4,128)S(1)}, u32[]{:S(2)}, u32[]{:S(2)}) collective-permute-start(f32[3,64,1]{2,0,1:T(4,128)S(1)} %get-tuple-element.820), channel_id=1, source_target_pairs={{0,63},{1,0},{2,1},{3,2},{4,3},{5,4},{6,5},{7,6},{8,7},{9,8},{10,9... | collective-permute-start | bytes 2312 | tf_op jit(solution)/shard_map/while/body/eval_jaxpr/ppermute | solution.py:93
  395.0 8.5 %collective-permute-start.54 = (f32[3,1,128]{2,0,1:T(4,128)S(1)}, f32[3,1,128]{2,0,1:T(4,128)S(1)}, u32[]{:S(2)}, u32[]{:S(2)}) collective-permute-start(f32[3,1,128]{2,0,1:T(4,128)S(1)} %get-tuple-element.825), channel_id=1, source_target_pairs={{0,64},{64,128},{128,192},{192,256},{256,320},{320,384},{384,448},... | collective-permute-start | bytes 4616 | tf_op jit(solution)/shard_map/while/body/eval_jaxpr/ppermute | solution.py:90
  405.5 51.5 %collective-permute-start.50 = (f32[2,1,128]{2,0,1:T(2,128)S(1)}, f32[2,1,128]{2,0,1:T(2,128)S(1)}, u32[]{:S(2)}, u32[]{:S(2)}) collective-permute-start(f32[2,1,128]{2,0,1:T(2,128)S(1)} %slice.676), channel_id=1, source_target_pairs={{64,0},{128,64},{192,128},{256,192},{320,256},{384,320},{448,384},... | collective-permute-start | bytes 3080 | tf_op jit(solution)/shard_map/while/body/eval_jaxpr/ppermute | solution.py:91
  407.6 46.4 %collective-permute-start.48 = (f32[2,64,1]{1,0,2:T(2,128)S(1)}, f32[2,64,1]{1,0,2:T(2,128)S(1)}, u32[]{:S(2)}, u32[]{:S(2)}) collective-permute-start(f32[2,64,1]{1,0,2:T(2,128)S(1)} %get-tuple-element.808), channel_id=1, source_target_pairs={{0,1},{1,2},{2,3},{3,4},{4,5},{5,6},{6,7},{7,8},{8,9},{9,10},{10,1... | collective-permute-start | bytes 1544 | tf_op jit(solution)/shard_map/while/body/eval_jaxpr/ppermute | solution.py:92
  410.1 47.0 %collective-permute-start.51 = (f32[2,1,128]{2,1,0:T(1,128)}, f32[2,1,128]{2,1,0:T(1,128)S(1)}, u32[]{:S(2)}, u32[]{:S(2)}) collective-permute-start(f32[2,1,128]{2,1,0:T(1,128)} %slice.677), channel_id=1, source_target_pairs={{0,64},{64,128},{128,192},{192,256},{256,320},{320,384},{384,448},... | collective-permute-start | bytes 3080 | tf_op jit(solution)/shard_map/while/body/eval_jaxpr/ppermute | solution.py:90
  412.5 11.5 %collective-permute-start.1 = (f32[2,128]{1,0:T(2,128)}, f32[2,128]{1,0:T(2,128)}, u32[]{:S(2)}, u32[]{:S(2)}) collective-permute-start(f32[2,128]{1,0:T(2,128)} %param.1), channel_id=1, source_target_pairs={{0,8},{1,7},{2,6},{3,5},{4,4},{5,3},{6,2},{7,1},{8,0},{9,63},{10,6... | collective-permute-start | bytes 3080 | tf_op jit(solution)/shard_map/while/body/eval_jaxpr/cond/branch_1_fun/ppermute | solution.py:68
  424.0 25.8 %collective-permute-start.20 = (f32[2,128]{1,0:T(2,128)}, f32[2,128]{1,0:T(2,128)}, u32[]{:S(2)}, u32[]{:S(2)}) collective-permute-start(f32[2,128]{1,0:T(2,128)} %param.14), channel_id=1, source_target_pairs={{0,6},{1,7},{2,8},{3,9},{4,10},{5,11},{6,12},{7,13},{8,14},{9,15},... | collective-permute-start | bytes 3080 | tf_op jit(solution)/shard_map/while/body/eval_jaxpr/cond/branch_6_fun/ppermute | solution.py:74
  432.5 18.7 %collective-permute-start.21 = (f32[2,128]{1,0:T(2,128)}, f32[2,128]{1,0:T(2,128)}, u32[]{:S(2)}, u32[]{:S(2)}) collective-permute-start(f32[2,128]{1,0:T(2,128)} %param.14), channel_id=1, source_target_pairs={{0,5},{1,6},{2,7},{3,8},{4,9},{5,10},{6,11},{7,12},{8,13},{9,14},{... | collective-permute-start | bytes 3080 | tf_op jit(solution)/shard_map/while/body/eval_jaxpr/cond/branch_6_fun/ppermute | solution.py:75
  457.7 11.3 %collective-permute-start.25 = (f32[3,128]{1,0:T(4,128)S(1)}, f32[3,128]{1,0:T(4,128)}, u32[]{:S(2)}, u32[]{:S(2)}) collective-permute-start(f32[3,128]{1,0:T(4,128)S(1)} %param.17), channel_id=1, source_target_pairs={{0,8},{1,7},{2,6},{3,5},{4,4},{5,3},{6,2},{7,1},{8,0},{9,63},{10,6... | collective-permute-start | bytes 4616 | tf_op jit(solution)/shard_map/while/body/eval_jaxpr/cond/branch_1_fun/ppermute | solution.py:68
  469.0 25.7 %collective-permute-start.44 = (f32[3,128]{1,0:T(4,128)}, f32[3,128]{1,0:T(4,128)}, u32[]{:S(2)}, u32[]{:S(2)}) collective-permute-start(f32[3,128]{1,0:T(4,128)} %param.30), channel_id=1, source_target_pairs={{0,6},{1,7},{2,8},{3,9},{4,10},{5,11},{6,12},{7,13},{8,14},{9,15},... | collective-permute-start | bytes 4616 | tf_op jit(solution)/shard_map/while/body/eval_jaxpr/cond/branch_6_fun/ppermute | solution.py:74
  477.3 19.0 %collective-permute-start.45 = (f32[3,128]{1,0:T(4,128)}, f32[3,128]{1,0:T(4,128)}, u32[]{:S(2)}, u32[]{:S(2)}) collective-permute-start(f32[3,128]{1,0:T(4,128)} %param.30), channel_id=1, source_target_pairs={{0,5},{1,6},{2,7},{3,8},{4,9},{5,10},{6,11},{7,12},{8,13},{9,14},{... | collective-permute-start | bytes 4616 | tf_op jit(solution)/shard_map/while/body/eval_jaxpr/cond/branch_6_fun/ppermute | solution.py:75
  496.3 10.6 %collective-permute-start.53 = (f32[3,1,128]{2,0,1:T(4,128)S(1)}, f32[3,1,128]{2,0,1:T(4,128)S(1)}, u32[]{:S(2)}, u32[]{:S(2)}) collective-permute-start(f32[3,1,128]{2,0,1:T(4,128)S(1)} %get-tuple-element.821), channel_id=1, source_target_pairs={{64,0},{128,64},{192,128},{256,192},{320,256},{384,320},{448,384},... | collective-permute-start | bytes 4616 | tf_op jit(solution)/shard_map/while/body/eval_jaxpr/ppermute | solution.py:91
  504.9 8.5 %collective-permute-start.54 = (f32[3,1,128]{2,0,1:T(4,128)S(1)}, f32[3,1,128]{2,0,1:T(4,128)S(1)}, u32[]{:S(2)}, u32[]{:S(2)}) collective-permute-start(f32[3,1,128]{2,0,1:T(4,128)S(1)} %get-tuple-element.825), channel_id=1, source_target_pairs={{0,64},{64,128},{128,192},{192,256},{256,320},{320,384},{384,448},... | collective-permute-start | bytes 4616 | tf_op jit(solution)/shard_map/while/body/eval_jaxpr/ppermute | solution.py:90
  (21 other events, 136.5 us)

commit v2 on v1

--- a/solution.py
+++ b/solution.py
@@ -57,7 +57,7 @@
     return local.reshape(rows, fields, cols)
 
 
-def fold_row(top, fold_start, fold_rest):
+def fold_strip(top, fold_start, fold_rest, width):
     peers = lax.axis_size("gx")
     cols = top.shape[-1]
     low = 8 if peers % 8 == 0 else 1
@@ -70,34 +70,61 @@
         )
 
     def shift(bb):
-        def run(y):
-            near = lax.ppermute(y, "gx", [(e, (e + bb) % peers) for e in range(peers)])
-            far = lax.ppermute(y, "gx", [(e, (e + bb - 1) % peers) for e in range(peers)])
-            return near, far
-
-        return run
+        return lambda y: tuple(
+            lax.ppermute(y, "gx", [(e, (e + bb + t) % peers) for e in range(peers)])
+            for t in (-2, -1, 0, 1)
+        )
 
     mirrored = lax.switch(a, [reflect(aa) for aa in range(peers // low)], top)
-    near, far = lax.switch(b, [shift(bb) for bb in range(low)], mirrored)
-    both = jnp.concatenate([far, near], axis=-1)
-    picked = lax.dynamic_slice_in_dim(both, fold_rest + 1, cols, axis=-1)
-    return jnp.flip(picked, axis=-1)
-
-
-def attach_rim_halo(field, signs, fold_start, fold_rest):
+    parts = lax.switch(b, [shift(bb) for bb in range(low)], mirrored)
+    strip = jnp.concatenate(parts, axis=-1)
+    first = 2 * cols + fold_rest - (cols - 1) - width
+    window = lax.dynamic_slice_in_dim(strip, first, cols + 2 * width, axis=2)
+    return jnp.flip(window, axis=(1, 2))
+
+
+def exchange(stack, width, signs, fold_start, fold_rest):
     ny = lax.axis_size("gy")
     nx = lax.axis_size("gx")
-    south = lax.ppermute(field[:, -1:, :], "gy", shift_pairs(ny, 1, False))
-    north = lax.ppermute(field[:, :1, :], "gy", shift_pairs(ny, -1, False))
-    west = lax.ppermute(field[:, :, -1:], "gx", shift_pairs(nx, 1, True))
-    east = lax.ppermute(field[:, :, :1], "gx", shift_pairs(nx, -1, True))
-    folded = fold_row(field[:, -1, :], fold_start, fold_rest)[:, None, :] * signs
-    north = jnp.where(lax.axis_index("gy") == ny - 1, folded, north)
-    rows = jnp.concatenate([south, field, north], axis=1)
-    corner = jnp.zeros_like(rows[:, :, :1])
-    west = jnp.concatenate([corner[:, :1], west, corner[:, :1]], axis=1)
-    east = jnp.concatenate([corner[:, :1], east, corner[:, :1]], axis=1)
-    return jnp.concatenate([west, rows, east], axis=2)
+    w = width
+
+    def diag(dy, dx):
+        return [
+            (y * nx + x, (y + dy) * nx + (x + dx) % nx)
+            for y in range(ny)
+            for x in range(nx)
+            if 0 <= y + dy < ny
+        ]
+
+    both = ("gy", "gx")
+    south = lax.ppermute(stack[:, -w:, :], "gy", shift_pairs(ny, 1, False))
+    north = lax.ppermute(stack[:, :w, :], "gy", shift_pairs(ny, -1, False))
+    west = lax.ppermute(stack[:, :, -w:], "gx", shift_pairs(nx, 1, True))
+    east = lax.ppermute(stack[:, :, :w], "gx", shift_pairs(nx, -1, True))
+    south_west = lax.ppermute(stack[:, -w:, -w:], both, diag(1, 1))
+    south_east = lax.ppermute(stack[:, -w:, :w], both, diag(1, -1))
+    north_west = lax.ppermute(stack[:, :w, -w:], both, diag(-1, 1))
+    north_east = lax.ppermute(stack[:, :w, :w], both, diag(-1, -1))
+    folded = fold_strip(stack[:, -w:, :], fold_start, fold_rest, w) * signs
+    at_top = lax.axis_index("gy") == ny - 1
+    cols = stack.shape[-1]
+    north = jnp.where(at_top, folded[:, :, w : w + cols], north)
+    north_west = jnp.where(at_top, folded[:, :, :w], north_west)
+    north_east = jnp.where(at_top, folded[:, :, w + cols :], north_east)
+    return jnp.concatenate(
+        [
+            jnp.concatenate([south_west, south, south_east], axis=2),
+            jnp.concatenate([west, stack, east], axis=2),
+            jnp.concatenate([north_west, north, north_east], axis=2),
+        ],
+        axis=1,
+    )
+
+
+def crop(x, n):
+    if n == 0:
+        return x
+    return x[..., n : x.shape[-2] - n, n : x.shape[-1] - n]
 
 
 def compute_strain_rates(u_pad, v_pad):
@@ -210,44 +237,71 @@
     strength = PSTAR * hsum * jnp.exp(-CSTAR * (1.0 - conc))
     ice_mass_per_area = hsum + 0.2
     rows = velocity.shape[1]
+    cols = velocity.shape[2]
     total_rows = rows * lax.axis_size("gy")
-    row_float = (lax.axis_index("gy") * rows + jnp.arange(rows, dtype=jnp.int32)).astype(
-        jnp.float32
-    )
-    coriolis_parameter = (FCOR * (row_float + 0.5) / float(total_rows))[:, None]
     velocity_mask = (ice_presence_mask * ocean_land_mask).astype(jnp.float32)
     omask = ocean_land_mask.astype(jnp.float32)
-    velocity_fold_sign = jnp.array([-1.0, -1.0], dtype=jnp.float32).reshape(2, 1, 1)
-    ssign = jnp.ones((3, 1, 1), dtype=jnp.float32)
-    cols = velocity.shape[2]
     fold_col = fold_partner_column[0] % (cols * lax.axis_size("gx"))
     fold_start = fold_col // cols
     fold_rest = fold_col % cols
-    def subcycle(step, state):
-        velocity, stress = state
-        velocity_padded = attach_rim_halo(velocity, velocity_fold_sign, fold_start, fold_rest)
-        strain_rate_east, strain_rate_north, strain_rate_shear = compute_strain_rates(
-            velocity_padded[0], velocity_padded[1]
+
+    width = 2 * ITERS
+    stack = jnp.concatenate(
+        [
+            velocity,
+            stress,
+            strength[None],
+            ice_mass_per_area[None],
+            wind,
+            ocean_current_east[None],
+            ocean_current_north[None],
+            velocity_mask[None],
+        ],
+        axis=0,
+    )
+    signs = jnp.array(
+        [-1.0, -1.0, 1.0, 1.0, 1.0, 1.0, 1.0, -1.0, -1.0, -1.0, -1.0, 1.0], jnp.float32
+    ).reshape(-1, 1, 1)
+    ext = exchange(stack, width, signs, fold_start, fold_rest)
+    grid_row = lax.axis_index("gy") * rows + jnp.arange(-width, rows + width, dtype=jnp.int32)
+    true_row = jnp.where(grid_row > total_rows - 1, 2 * total_rows - 1 - grid_row, grid_row)
+    coriolis_ext = (FCOR * (true_row.astype(jnp.float32) + 0.5) / float(total_rows))[:, None]
+    inside_ext = (grid_row >= 0)[:, None]
+
+    def rows_crop(x, n):
+        return x if n == 0 else x[n : x.shape[0] - n]
+
+    vel = ext[0:2]
+    st = ext[2:5]
+    st_radius = width
+    for step in range(ITERS):
+        radius = width - 2 * step
+        e11, e22, e12 = compute_strain_rates(vel[0], vel[1])
+        st = stress_update(
+            crop(st, st_radius - (radius - 1)),
+            e11,
+            e22,
+            e12,
+            crop(ext[5], width - (radius - 1)),
         )
-        stress = stress_update(
-            stress, strain_rate_east, strain_rate_north, strain_rate_shear, strength
-        )
-        spad = attach_rim_halo(stress, ssign, fold_start, fold_rest)
-        eastward_force, northward_force = stress_force(spad)
-        velocity = momentum_solve(
-            velocity,
+        st = jnp.where(rows_crop(inside_ext, width - (radius - 1)), st, 0.0)
+        st_radius = radius - 1
+        eastward_force, northward_force = stress_force(st)
+        n = width - (radius - 2)
+        vel = momentum_solve(
+            crop(vel, 2),
             eastward_force,
             northward_force,
-            wind,
-            ocean_current_east,
-            ocean_current_north,
-            ice_mass_per_area,
-            coriolis_parameter,
-            velocity_mask,
+            crop(ext[7:9], n),
+            crop(ext[9], n),
+            crop(ext[10], n),
+            crop(ext[6], n),
+            rows_crop(coriolis_ext, n),
+            crop(ext[11], n),
         )
-        return velocity, stress
-
-    velocity, stress = lax.fori_loop(0, ITERS, subcycle, (velocity, stress))
+        vel = jnp.where(rows_crop(inside_ext, n), vel, 0.0)
+    velocity = vel
+    stress = crop(st, st_radius)
     thickness_out = column_growth(
         thickness,
         velocity,

time: 519 us -> 181 us (0.35)
  the two profiles are of different devices: /device:TPU:38 before, /device:TPU:25 now
where the time goes in v2:
time: 181 us; the launch traced here: 180 us
  starting transfers between devices  95.6 us (53%)
  waiting for transfers between devices  61.7 us (34%)
  local copies, waits for them, and re-layouts  11 us (6%)
  other arithmetic  7.75 us (4%)
  between operations  3.2 us (2%)
    all_to_all x1, waiting for transfers between devices, regroup_local(): lax.all_to_all(packed, 'gx', split_axis=0, concat_axis=0, tiled=True)  33.1 us
    all_to_all x1, starting transfers between devices, regroup_local(): lax.all_to_all(packed, 'gx', split_axis=0, concat_axis=0, tiled=True)  30.1 us
    ppermute x4, starting transfers between devices, shift(): lax.ppermute(y, 'gx', [(e, (e + bb + t) % peers) for e in range(peers)])  19.6 us
    ppermute x4, waiting for transfers between devices, shift(): lax.ppermute(y, 'gx', [(e, (e + bb + t) % peers) for e in range(peers)])  11.1 us
    ppermute x1, starting transfers between devices, exchange(): south = lax.ppermute(stack[:, -w:, :], 'gy', shift_pairs(ny, 1, False))  9.21 us
    ppermute x1, waiting for transfers between devices, reflect(): lax.ppermute(t, 'gx', [(e, (low * aa - e) % peers) for e in range(peers)])  9.19 us
    ppermute x1, starting transfers between devices, exchange(): south_east = lax.ppermute(stack[:, -w:, :w], both, diag(1, -1))  6.67 us
    ppermute x1, waiting for transfers between devices, exchange(): west = lax.ppermute(stack[:, :, -w:], 'gx', shift_pairs(nx, 1, True))  6.51 us
  transfers between devices with their start and end apart: 14, of which 6 were waited for; matrix products, arithmetic and copies ran while one was open for 2% of the time, Pallas kernels for 0%

profile of v2, /device:TPU:25, one launch (start us, length us, event | category | flops | bytes accessed | tf_op | source)
XLA Modules:
  0.0 180.0 jit_solution(9671715126218916934)
XLA Ops:
  0.6 0.6 copy-done.10
  1.4 1.0 reshape.177
  2.5 0.4 fusion.150
  2.8 0.5 broadcast.423
  3.4 0.7 reduce.3
  4.5 1.0 copy.28
  5.5 30.1 %all-to-all-start = ((f32[64,1,1026]{2,1,0:T(1,128)}), f32[64,1,1026]{2,1,0:T(1,128)S(1)}, u32[]{:S(2)}, u32[]{:S(2)}) async-start(f32[64,1,1026]{2,1,0:T(1,128)} %copy.28), calls=%async_computation | async-start | bytes 589824 | tf_op jit(solution)/shard_map/all_to_all | solution.py:48
  35.6 1.2 slice.644
  39.8 0.8 copy-done.5
  40.9 0.8 copy-done.2
  41.7 33.1 %all-to-all-done = f32[64,1,1026]{2,1,0:T(1,128)S(1)} async-done(((f32[64,1,1026]{2,1,0:T(1,128)}), f32[64,1,1026]{2,1,0:T(1,128)S(1)}, u32[]{:S(2)}, u32[]{:S(2)}) %all-to-all-start) | async-done | bytes 262688 | tf_op jit(solution)/shard_map/all_to_all | solution.py:48
  75.1 0.3 fusion.139
  75.4 0.7 copy-done.7
  76.2 0.6 fusion.158
  77.1 9.2 %collective-permute-start.41 = (f32[12,8,128]{2,1,0:T(8,128)}, f32[12,8,128]{2,1,0:T(8,128)S(1)}, u32[]{:S(2)}, u32[]{:S(2)}) collective-permute-start(f32[12,8,128]{2,1,0:T(8,128)} %get-tuple-element.66), channel_id=1, source_target_pairs={{0,64},{64,128},{128,192},{192,256},{256,320},{320,384},{384,448},... | collective-permute-start | bytes 147464 | tf_op jit(solution)/shard_map/ppermute | solution.py:100
  86.3 13.9 %conditional.2 = (f32[12,8,128]{2,1,0:T(8,128)}) conditional(s32[]{:T(128)} %clamp.7, f32[12,8,128]{2,1,0:T(8,128)} %get-tuple-element.66, f32[12,8,128]{2,1,0:T(8,128)} %get-tuple-element.66, f32[12,8,128]{2,1,0:T(8,128)} %get-tuple-element.66, f32[12,8,128]{2,1,0:T(8,128)} %get-tuple-element.66, ...), branch_computations={%region_3.4_spmd, %region_4.5_spmd, %region_5.6_spmd, %region_6.7_... | conditional | bytes 196656 | solution.py:78
  86.3 4.7 %collective-permute-start.3 = (f32[12,8,128]{2,1,0:T(8,128)}, f32[12,8,128]{2,1,0:T(8,128)}, u32[]{:S(2)}, u32[]{:S(2)}) collective-permute-start(f32[12,8,128]{2,1,0:T(8,128)} %param.3), channel_id=1, source_target_pairs={{0,24},{1,23},{2,22},{3,21},{4,20},{5,19},{6,18},{7,17},{8,16},{9,... | collective-permute-start | bytes 147464 | tf_op jit(solution)/shard_map/cond/branch_3_fun/ppermute | solution.py:68
  91.0 9.2 %collective-permute-done.3 = f32[12,8,128]{2,1,0:T(8,128)} collective-permute-done((f32[12,8,128]{2,1,0:T(8,128)}, f32[12,8,128]{2,1,0:T(8,128)}, u32[]{:S(2)}, u32[]{:S(2)}) %collective-permute-start.3) | collective-permute-done | bytes 49184 | tf_op jit(solution)/shard_map/cond/branch_3_fun/ppermute | solution.py:68
  100.2 30.8 %conditional.3 = (f32[12,8,128]{2,1,0:T(8,128)}, f32[12,8,128]{2,1,0:T(8,128)}, f32[12,8,128]{2,1,0:T(8,128)}, f32[12,8,128]{2,1,0:T(8,128)}) conditional(s32[]{:T(128)} %clamp.6, f32[12,8,128]{2,1,0:T(8,128)} %get-tuple-element.125, f32[12,8,128]{2,1,0:T(8,128)} %get-tuple-element.125, ...), branch_computations={%region_11.12_spmd, %region_12.13_spmd, %region_13.14_spmd, %regio... | conditional | bytes 786624 | solution.py:79
  100.2 7.1 %collective-permute-start.24 = (f32[12,8,128]{2,1,0:T(8,128)}, f32[12,8,128]{2,1,0:T(8,128)}, u32[]{:S(2)}, u32[]{:S(2)}) collective-permute-start(f32[12,8,128]{2,1,0:T(8,128)} %param.12), channel_id=1, source_target_pairs={{0,2},{1,3},{2,4},{3,5},{4,6},{5,7},{6,8},{7,9},{8,10},{9,11},{10,... | collective-permute-start | bytes 147464 | tf_op jit(solution)/shard_map/cond/branch_4_fun/ppermute | solution.py:74
  107.3 6.0 %collective-permute-start.25 = (f32[12,8,128]{2,1,0:T(8,128)}, f32[12,8,128]{2,1,0:T(8,128)}, u32[]{:S(2)}, u32[]{:S(2)}) collective-permute-start(f32[12,8,128]{2,1,0:T(8,128)} %param.12), channel_id=1, source_target_pairs={{0,3},{1,4},{2,5},{3,6},{4,7},{5,8},{6,9},{7,10},{8,11},{9,12},{10... | collective-permute-start | bytes 147464 | tf_op jit(solution)/shard_map/cond/branch_4_fun/ppermute | solution.py:74
  113.3 4.6 %collective-permute-start.26 = (f32[12,8,128]{2,1,0:T(8,128)}, f32[12,8,128]{2,1,0:T(8,128)}, u32[]{:S(2)}, u32[]{:S(2)}) collective-permute-start(f32[12,8,128]{2,1,0:T(8,128)} %param.12), channel_id=1, source_target_pairs={{0,4},{1,5},{2,6},{3,7},{4,8},{5,9},{6,10},{7,11},{8,12},{9,13},{1... | collective-permute-start | bytes 147464 | tf_op jit(solution)/shard_map/cond/branch_4_fun/ppermute | solution.py:74
  117.9 1.9 %collective-permute-start.27 = (f32[12,8,128]{2,1,0:T(8,128)}, f32[12,8,128]{2,1,0:T(8,128)}, u32[]{:S(2)}, u32[]{:S(2)}) collective-permute-start(f32[12,8,128]{2,1,0:T(8,128)} %param.12), channel_id=1, source_target_pairs={{0,5},{1,6},{2,7},{3,8},{4,9},{5,10},{6,11},{7,12},{8,13},{9,14},{... | collective-permute-start | bytes 147464 | tf_op jit(solution)/shard_map/cond/branch_4_fun/ppermute | solution.py:74
  119.9 5.1 %collective-permute-done.26 = f32[12,8,128]{2,1,0:T(8,128)} collective-permute-done((f32[12,8,128]{2,1,0:T(8,128)}, f32[12,8,128]{2,1,0:T(8,128)}, u32[]{:S(2)}, u32[]{:S(2)}) %collective-permute-start.26) | collective-permute-done | bytes 49184 | tf_op jit(solution)/shard_map/cond/branch_4_fun/ppermute | solution.py:74
  124.9 6.0 %collective-permute-done.27 = f32[12,8,128]{2,1,0:T(8,128)} collective-permute-done((f32[12,8,128]{2,1,0:T(8,128)}, f32[12,8,128]{2,1,0:T(8,128)}, u32[]{:S(2)}, u32[]{:S(2)}) %collective-permute-start.27) | collective-permute-done | bytes 49184 | tf_op jit(solution)/shard_map/cond/branch_4_fun/ppermute | solution.py:74
  131.0 1.0 fusion.2
  132.1 5.9 %collective-permute-start.46 = (f32[12,8,128]{2,1,0:T(8,128)S(1)}, f32[12,8,128]{2,1,0:T(8,128)S(1)}, u32[]{:S(2)}, u32[]{:S(2)}) collective-permute-start(f32[12,8,128]{2,1,0:T(8,128)S(1)} %get-tuple-element.65), channel_id=1, source_target_pairs={{64,0},{128,64},{192,128},{256,192},{320,256},{384,320},{448,384},... | collective-permute-start | bytes 147464 | tf_op jit(solution)/shard_map/ppermute | solution.py:101
  138.1 1.9 %collective-permute-start.45 = (f32[12,8,8]{2,1,0:T(8,128)S(1)}, f32[12,8,8]{2,1,0:T(8,128)S(1)}, u32[]{:S(2)}, u32[]{:S(2)}) collective-permute-start(f32[12,8,8]{2,1,0:T(8,128)S(1)} %get-tuple-element.61), channel_id=1, source_target_pairs={{64,1},{65,2},{66,3},{67,4},{68,5},{69,6},{70,7},{71,8},{72,9},{73... | collective-permute-start | bytes 9224 | tf_op jit(solution)/shard_map/ppermute | solution.py:106
  140.0 5.4 %collective-permute-start.47 = (f32[12,8,8]{2,1,0:T(8,128)S(1)}, f32[12,8,8]{2,1,0:T(8,128)S(1)}, u32[]{:S(2)}, u32[]{:S(2)}) collective-permute-start(f32[12,8,8]{2,1,0:T(8,128)S(1)} %get-tuple-element.60), channel_id=1, source_target_pairs={{64,63},{65,0},{66,1},{67,2},{68,3},{69,4},{70,5},{71,6},{72,7},{7... | collective-permute-start | bytes 9224 | tf_op jit(solution)/shard_map/ppermute | solution.py:107
  145.4 4.7 %collective-permute-start.40 = (f32[12,8,8]{2,1,0:T(8,128)S(1)}, f32[12,8,8]{2,1,0:T(8,128)S(1)}, u32[]{:S(2)}, u32[]{:S(2)}) collective-permute-start(f32[12,8,8]{2,1,0:T(8,128)S(1)} %get-tuple-element.59), channel_id=1, source_target_pairs={{0,65},{1,66},{2,67},{3,68},{4,69},{5,70},{6,71},{7,72},{8,73},{9,... | collective-permute-start | bytes 9224 | tf_op jit(solution)/shard_map/ppermute | solution.py:104
  150.3 6.7 %collective-permute-start.42 = (f32[12,8,8]{2,1,0:T(8,128)S(1)}, f32[12,8,8]{2,1,0:T(8,128)S(1)}, u32[]{:S(2)}, u32[]{:S(2)}) collective-permute-start(f32[12,8,8]{2,1,0:T(8,128)S(1)} %get-tuple-element.62), channel_id=1, source_target_pairs={{0,127},{1,64},{2,65},{3,66},{4,67},{5,68},{6,69},{7,70},{8,71},{9... | collective-permute-start | bytes 9224 | tf_op jit(solution)/shard_map/ppermute | solution.py:105
  157.0 1.9 %collective-permute-start.43 = (f32[12,64,8]{2,1,0:T(8,128)S(1)}, f32[12,64,8]{2,1,0:T(8,128)S(1)}, u32[]{:S(2)}, u32[]{:S(2)}) collective-permute-start(f32[12,64,8]{2,1,0:T(8,128)S(1)} %get-tuple-element.63), channel_id=1, source_target_pairs={{0,1},{1,2},{2,3},{3,4},{4,5},{5,6},{6,7},{7,8},{8,9},{9,10},{10,1... | collective-permute-start | bytes 73736 | tf_op jit(solution)/shard_map/ppermute | solution.py:102
  159.0 5.5 %collective-permute-start.44 = (f32[12,64,8]{2,1,0:T(8,128)S(1)}, f32[12,64,8]{2,1,0:T(8,128)S(1)}, u32[]{:S(2)}, u32[]{:S(2)}) collective-permute-start(f32[12,64,8]{2,1,0:T(8,128)S(1)} %get-tuple-element.64), channel_id=1, source_target_pairs={{0,63},{1,0},{2,1},{3,2},{4,3},{5,4},{6,5},{7,6},{8,7},{9,8},{10,9... | collective-permute-start | bytes 73736 | tf_op jit(solution)/shard_map/ppermute | solution.py:103
  164.6 6.5 %collective-permute-done.43 = f32[12,64,8]{2,1,0:T(8,128)S(1)} collective-permute-done((f32[12,64,8]{2,1,0:T(8,128)S(1)}, f32[12,64,8]{2,1,0:T(8,128)S(1)}, u32[]{:S(2)}, u32[]{:S(2)}) %collective-permute-start.43) | collective-permute-done | bytes 24608 | tf_op jit(solution)/shard_map/ppermute | solution.py:102
  171.1 1.8 %collective-permute-done.44 = f32[12,64,8]{2,1,0:T(8,128)S(1)} collective-permute-done((f32[12,64,8]{2,1,0:T(8,128)S(1)}, f32[12,64,8]{2,1,0:T(8,128)S(1)}, u32[]{:S(2)}, u32[]{:S(2)}) %collective-permute-start.44) | collective-permute-done | bytes 24608 | tf_op jit(solution)/shard_map/ppermute | solution.py:103
  172.9 0.4 maximum_maximum_fusion
  173.4 0.2 fusion.46
  174.0 0.3 fusion.30
  174.3 0.3 fusion.21
  174.7 0.2 fusion.15
  175.2 0.3 fusion.105
  175.5 0.3 fusion.96
  175.9 0.2 fusion.90
  176.4 0.3 fusion.74
  176.6 0.3 fusion.65
  177.5 0.7 slice.954
  178.7 0.6 copy-done.1
  179.3 0.7 maximum_multiply_fusion
  (96 shorter events, 5.0 us)
Async XLA Ops:
  0.6 0.7 copy-start.10
  5.5 34.3 %copy-start.6 = (f32[2,64,128]{2,1,0:T(8,128)S(1)}, f32[2,64,128]{2,1,0:T(8,128)}, u32[]{:S(2)}) copy-start(f32[2,64,128]{2,1,0:T(8,128)} %param.30) | copy-start | bytes 196612
  5.5 69.3 %all-to-all-start = ((f32[64,1,1026]{2,1,0:T(1,128)}), f32[64,1,1026]{2,1,0:T(1,128)S(1)}, u32[]{:S(2)}, u32[]{:S(2)}) async-start(f32[64,1,1026]{2,1,0:T(1,128)} %copy.28), calls=%async_computation | async-start | bytes 589824 | tf_op jit(solution)/shard_map/all_to_all | solution.py:48
  38.8 0.9 copy-start.4
  39.8 0.9 copy-start.5
  39.8 1.0 copy-start.3
  39.8 1.0 copy-start
  40.8 0.8 copy-start.2
  75.4 0.8 copy-start.7
  77.1 95.8 %collective-permute-start.41 = (f32[12,8,128]{2,1,0:T(8,128)}, f32[12,8,128]{2,1,0:T(8,128)S(1)}, u32[]{:S(2)}, u32[]{:S(2)}) collective-permute-start(f32[12,8,128]{2,1,0:T(8,128)} %get-tuple-element.66), channel_id=1, source_target_pairs={{0,64},{64,128},{128,192},{192,256},{256,320},{320,384},{384,448},... | collective-permute-start | bytes 147464 | tf_op jit(solution)/shard_map/ppermute | solution.py:100
  86.3 13.9 %collective-permute-start.3 = (f32[12,8,128]{2,1,0:T(8,128)}, f32[12,8,128]{2,1,0:T(8,128)}, u32[]{:S(2)}, u32[]{:S(2)}) collective-permute-start(f32[12,8,128]{2,1,0:T(8,128)} %param.3), channel_id=1, source_target_pairs={{0,24},{1,23},{2,22},{3,21},{4,20},{5,19},{6,18},{7,17},{8,16},{9,... | collective-permute-start | bytes 147464 | tf_op jit(solution)/shard_map/cond/branch_3_fun/ppermute | solution.py:68
  100.2 19.6 %collective-permute-start.24 = (f32[12,8,128]{2,1,0:T(8,128)}, f32[12,8,128]{2,1,0:T(8,128)}, u32[]{:S(2)}, u32[]{:S(2)}) collective-permute-start(f32[12,8,128]{2,1,0:T(8,128)} %param.12), channel_id=1, source_target_pairs={{0,2},{1,3},{2,4},{3,5},{4,6},{5,7},{6,8},{7,9},{8,10},{9,11},{10,... | collective-permute-start | bytes 147464 | tf_op jit(solution)/shard_map/cond/branch_4_fun/ppermute | solution.py:74
  107.3 12.5 %collective-permute-start.25 = (f32[12,8,128]{2,1,0:T(8,128)}, f32[12,8,128]{2,1,0:T(8,128)}, u32[]{:S(2)}, u32[]{:S(2)}) collective-permute-start(f32[12,8,128]{2,1,0:T(8,128)} %param.12), channel_id=1, source_target_pairs={{0,3},{1,4},{2,5},{3,6},{4,7},{5,8},{6,9},{7,10},{8,11},{9,12},{10... | collective-permute-start | bytes 147464 | tf_op jit(solution)/shard_map/cond/branch_4_fun/ppermute | solution.py:74
  113.3 11.6 %collective-permute-start.26 = (f32[12,8,128]{2,1,0:T(8,128)}, f32[12,8,128]{2,1,0:T(8,128)}, u32[]{:S(2)}, u32[]{:S(2)}) collective-permute-start(f32[12,8,128]{2,1,0:T(8,128)} %param.12), channel_id=1, source_target_pairs={{0,4},{1,5},{2,6},{3,7},{4,8},{5,9},{6,10},{7,11},{8,12},{9,13},{1... | collective-permute-start | bytes 147464 | tf_op jit(solution)/shard_map/cond/branch_4_fun/ppermute | solution.py:74
  117.9 13.0 %collective-permute-start.27 = (f32[12,8,128]{2,1,0:T(8,128)}, f32[12,8,128]{2,1,0:T(8,128)}, u32[]{:S(2)}, u32[]{:S(2)}) collective-permute-start(f32[12,8,128]{2,1,0:T(8,128)} %param.12), channel_id=1, source_target_pairs={{0,5},{1,6},{2,7},{3,8},{4,9},{5,10},{6,11},{7,12},{8,13},{9,14},{... | collective-permute-start | bytes 147464 | tf_op jit(solution)/shard_map/cond/branch_4_fun/ppermute | solution.py:74
  132.1 26.8 %collective-permute-start.46 = (f32[12,8,128]{2,1,0:T(8,128)S(1)}, f32[12,8,128]{2,1,0:T(8,128)S(1)}, u32[]{:S(2)}, u32[]{:S(2)}) collective-permute-start(f32[12,8,128]{2,1,0:T(8,128)S(1)} %get-tuple-element.65), channel_id=1, source_target_pairs={{64,0},{128,64},{192,128},{256,192},{320,256},{384,320},{448,384},... | collective-permute-start | bytes 147464 | tf_op jit(solution)/shard_map/ppermute | solution.py:101
  138.1 12.2 %collective-permute-start.45 = (f32[12,8,8]{2,1,0:T(8,128)S(1)}, f32[12,8,8]{2,1,0:T(8,128)S(1)}, u32[]{:S(2)}, u32[]{:S(2)}) collective-permute-start(f32[12,8,8]{2,1,0:T(8,128)S(1)} %get-tuple-element.61), channel_id=1, source_target_pairs={{64,1},{65,2},{66,3},{67,4},{68,5},{69,6},{70,7},{71,8},{72,9},{73... | collective-permute-start | bytes 9224 | tf_op jit(solution)/shard_map/ppermute | solution.py:106
  140.0 10.1 %copy-start.9 = (f32[12]{0:T(128)S(1)}, f32[12]{0:T(128)}, u32[]{:S(2)}) copy-start(f32[12]{0:T(128)} %constant.204.clone) | copy-start | bytes 148
  140.0 16.9 %collective-permute-start.47 = (f32[12,8,8]{2,1,0:T(8,128)S(1)}, f32[12,8,8]{2,1,0:T(8,128)S(1)}, u32[]{:S(2)}, u32[]{:S(2)}) collective-permute-start(f32[12,8,8]{2,1,0:T(8,128)S(1)} %get-tuple-element.60), channel_id=1, source_target_pairs={{64,63},{65,0},{66,1},{67,2},{68,3},{69,4},{70,5},{71,6},{72,7},{7... | collective-permute-start | bytes 9224 | tf_op jit(solution)/shard_map/ppermute | solution.py:107
  145.4 4.8 %copy-start.8 = (f32[64,128]{1,0:T(8,128)S(1)}, f32[64,128]{1,0:T(8,128)}, u32[]{:S(2)}) copy-start(f32[64,128]{1,0:T(8,128)} %param.35) | copy-start | bytes 98308
  145.4 19.1 %collective-permute-start.40 = (f32[12,8,8]{2,1,0:T(8,128)S(1)}, f32[12,8,8]{2,1,0:T(8,128)S(1)}, u32[]{:S(2)}, u32[]{:S(2)}) collective-permute-start(f32[12,8,8]{2,1,0:T(8,128)S(1)} %get-tuple-element.59), channel_id=1, source_target_pairs={{0,65},{1,66},{2,67},{3,68},{4,69},{5,70},{6,71},{7,72},{8,73},{9,... | collective-permute-start | bytes 9224 | tf_op jit(solution)/shard_map/ppermute | solution.py:104
  150.3 14.3 %collective-permute-start.42 = (f32[12,8,8]{2,1,0:T(8,128)S(1)}, f32[12,8,8]{2,1,0:T(8,128)S(1)}, u32[]{:S(2)}, u32[]{:S(2)}) collective-permute-start(f32[12,8,8]{2,1,0:T(8,128)S(1)} %get-tuple-element.62), channel_id=1, source_target_pairs={{0,127},{1,64},{2,65},{3,66},{4,67},{5,68},{6,69},{7,70},{8,71},{9... | collective-permute-start | bytes 9224 | tf_op jit(solution)/shard_map/ppermute | solution.py:105
  157.0 14.1 %collective-permute-start.43 = (f32[12,64,8]{2,1,0:T(8,128)S(1)}, f32[12,64,8]{2,1,0:T(8,128)S(1)}, u32[]{:S(2)}, u32[]{:S(2)}) collective-permute-start(f32[12,64,8]{2,1,0:T(8,128)S(1)} %get-tuple-element.63), channel_id=1, source_target_pairs={{0,1},{1,2},{2,3},{3,4},{4,5},{5,6},{6,7},{7,8},{8,9},{9,10},{10,1... | collective-permute-start | bytes 73736 | tf_op jit(solution)/shard_map/ppermute | solution.py:102
  159.0 13.9 %collective-permute-start.44 = (f32[12,64,8]{2,1,0:T(8,128)S(1)}, f32[12,64,8]{2,1,0:T(8,128)S(1)}, u32[]{:S(2)}, u32[]{:S(2)}) collective-permute-start(f32[12,64,8]{2,1,0:T(8,128)S(1)} %get-tuple-element.64), channel_id=1, source_target_pairs={{0,63},{1,0},{2,1},{3,2},{4,3},{5,4},{6,5},{7,6},{8,7},{9,8},{10,9... | collective-permute-start | bytes 73736 | tf_op jit(solution)/shard_map/ppermute | solution.py:103
  178.7 0.6 copy-start.1

commit v3 on v2

--- a/solution.py
+++ b/solution.py
@@ -57,68 +57,54 @@
     return local.reshape(rows, fields, cols)
 
 
-def fold_strip(top, fold_start, fold_rest, width):
-    peers = lax.axis_size("gx")
-    cols = top.shape[-1]
-    low = 8 if peers % 8 == 0 else 1
-    a = fold_start // low
-    b = fold_start % low
-
-    def reflect(aa):
-        return lambda t: lax.ppermute(
-            t, "gx", [(e, (low * aa - e) % peers) for e in range(peers)]
-        )
-
-    def shift(bb):
-        return lambda y: tuple(
-            lax.ppermute(y, "gx", [(e, (e + bb + t) % peers) for e in range(peers)])
-            for t in (-2, -1, 0, 1)
-        )
-
-    mirrored = lax.switch(a, [reflect(aa) for aa in range(peers // low)], top)
-    parts = lax.switch(b, [shift(bb) for bb in range(low)], mirrored)
-    strip = jnp.concatenate(parts, axis=-1)
-    first = 2 * cols + fold_rest - (cols - 1) - width
-    window = lax.dynamic_slice_in_dim(strip, first, cols + 2 * width, axis=2)
-    return jnp.flip(window, axis=(1, 2))
-
-
 def exchange(stack, width, signs, fold_start, fold_rest):
     ny = lax.axis_size("gy")
     nx = lax.axis_size("gx")
     w = width
-
-    def diag(dy, dx):
-        return [
-            (y * nx + x, (y + dy) * nx + (x + dx) % nx)
-            for y in range(ny)
-            for x in range(nx)
-            if 0 <= y + dy < ny
-        ]
-
-    both = ("gy", "gx")
-    south = lax.ppermute(stack[:, -w:, :], "gy", shift_pairs(ny, 1, False))
-    north = lax.ppermute(stack[:, :w, :], "gy", shift_pairs(ny, -1, False))
-    west = lax.ppermute(stack[:, :, -w:], "gx", shift_pairs(nx, 1, True))
-    east = lax.ppermute(stack[:, :, :w], "gx", shift_pairs(nx, -1, True))
-    south_west = lax.ppermute(stack[:, -w:, -w:], both, diag(1, 1))
-    south_east = lax.ppermute(stack[:, -w:, :w], both, diag(1, -1))
-    north_west = lax.ppermute(stack[:, :w, -w:], both, diag(-1, 1))
-    north_east = lax.ppermute(stack[:, :w, :w], both, diag(-1, -1))
-    folded = fold_strip(stack[:, -w:, :], fold_start, fold_rest, w) * signs
-    at_top = lax.axis_index("gy") == ny - 1
     cols = stack.shape[-1]
-    north = jnp.where(at_top, folded[:, :, w : w + cols], north)
-    north_west = jnp.where(at_top, folded[:, :, :w], north_west)
-    north_east = jnp.where(at_top, folded[:, :, w + cols :], north_east)
-    return jnp.concatenate(
-        [
-            jnp.concatenate([south_west, south, south_east], axis=2),
-            jnp.concatenate([west, stack, east], axis=2),
-            jnp.concatenate([north_west, north, north_east], axis=2),
-        ],
-        axis=1,
-    )
+    low = 8 if nx % 8 == 0 else 1
+    a = fold_start // low
+    b = fold_start % low
+
+    def stage_one(aa):
+        def run(top, west_in, east_in):
+            mirrored = lax.ppermute(top, "gx", [(e, (low * aa - e) % nx) for e in range(nx)])
+            west = lax.ppermute(west_in, "gx", shift_pairs(nx, 1, True))
+            east = lax.ppermute(east_in, "gx", shift_pairs(nx, -1, True))
+            return mirrored, west, east
+
+        return run
+
+    mirrored, west, east = lax.switch(
+        a,
+        [stage_one(aa) for aa in range(nx // low)],
+        stack[:, -w:, :],
+        stack[:, :, -w:],
+        stack[:, :, :w],
+    )
+    wide = jnp.concatenate([west, stack, east], axis=2)
+
+    def stage_two(bb):
+        def run(y, south_in, north_in):
+            parts = tuple(
+                lax.ppermute(y, "gx", [(e, (e + bb + t) % nx) for e in range(nx)])
+                for t in (-2, -1, 0, 1)
+            )
+            south = lax.ppermute(south_in, "gy", shift_pairs(ny, 1, False))
+            north = lax.ppermute(north_in, "gy", shift_pairs(ny, -1, False))
+            return parts, south, north
+
+        return run
+
+    parts, south, north = lax.switch(
+        b, [stage_two(bb) for bb in range(low)], mirrored, wide[:, -w:, :], wide[:, :w, :]
+    )
+    strip = jnp.concatenate(parts, axis=-1)
+    first = 2 * cols + fold_rest - (cols - 1) - w
+    window = lax.dynamic_slice_in_dim(strip, first, cols + 2 * w, axis=2)
+    folded = jnp.flip(window, axis=(1, 2)) * signs
+    north = jnp.where(lax.axis_index("gy") == ny - 1, folded, north)
+    return jnp.concatenate([south, wide, north], axis=1)
 
 
 def crop(x, n):

time: 181 us -> 136 us (0.75)
  the two profiles are of different devices: /device:TPU:25 before, /device:TPU:4 now
where the time goes in v3:
time: 136 us; the launch traced here: 135 us
  starting transfers between devices  63.5 us (47%)
  waiting for transfers between devices  46.6 us (34%)
  local copies, waits for them, and re-layouts  11.7 us (9%)
  other arithmetic  9.44 us (7%)
  between operations  3.08 us (2%)
    all_to_all x1, waiting for transfers between devices, regroup_local(): lax.all_to_all(packed, 'gx', split_axis=0, concat_axis=0, tiled=True)  37.4 us
    all_to_all x1, starting transfers between devices, regroup_local(): lax.all_to_all(packed, 'gx', split_axis=0, concat_axis=0, tiled=True)  30.1 us
    ppermute x4, starting transfers between devices, run(): lax.ppermute(y, 'gx', [(e, (e + bb + t) % nx) for e in range(nx)])  11.4 us
    ppermute x4, waiting for transfers between devices, run(): lax.ppermute(y, 'gx', [(e, (e + bb + t) % nx) for e in range(nx)])  7.39 us
    ppermute x1, starting transfers between devices, run(): north = lax.ppermute(north_in, 'gy', shift_pairs(ny, -1, False))  7.26 us
    ppermute x1, starting transfers between devices, run(): east = lax.ppermute(east_in, 'gx', shift_pairs(nx, -1, True))  5.53 us
    unnamed x30, local copies, waits for them, and re-layouts  5.33 us
    ppermute x1, starting transfers between devices, run(): lax.ppermute(top, 'gx', [(e, (low * aa - e) % nx) for e in range(nx)])  4.84 us
  transfers between devices with their start and end apart: 10, of which 6 were waited for; matrix products, arithmetic and copies ran while one was open for 2% of the time, Pallas kernels for 0%

profile of v3, /device:TPU:4, one launch (start us, length us, event | category | flops | bytes accessed | tf_op | source)
XLA Modules:
  0.0 135.1 jit_solution(10029561929553594002)
XLA Ops:
  0.6 0.6 copy-done.10
  1.4 1.0 reshape.177
  2.5 0.4 fusion.150
  2.9 0.5 broadcast.423
  3.4 0.7 reduce.3
  4.5 1.0 copy.100
  5.5 30.1 %all-to-all-start = ((f32[64,1,1026]{2,1,0:T(1,128)}), f32[64,1,1026]{2,1,0:T(1,128)S(1)}, u32[]{:S(2)}, u32[]{:S(2)}) async-start(f32[64,1,1026]{2,1,0:T(1,128)} %copy.100), calls=%async_computation | async-start | bytes 589824 | tf_op jit(solution)/shard_map/all_to_all | solution.py:48
  35.6 1.2 slice.591
  39.8 0.8 copy-done.5
  40.9 0.8 copy-done.2
  41.7 37.4 %all-to-all-done = f32[64,1,1026]{2,1,0:T(1,128)S(1)} async-done(((f32[64,1,1026]{2,1,0:T(1,128)}), f32[64,1,1026]{2,1,0:T(1,128)S(1)}, u32[]{:S(2)}, u32[]{:S(2)}) %all-to-all-start) | async-done | bytes 262688 | tf_op jit(solution)/shard_map/all_to_all | solution.py:48
  79.5 0.3 fusion.139
  79.8 0.7 copy-done.7
  80.5 15.4 %conditional.2 = (f32[12,8,128]{2,1,0:T(8,128)}, f32[12,64,8]{2,1,0:T(8,128)S(1)}, f32[12,64,8]{2,1,0:T(8,128)S(1)}) conditional(s32[]{:T(128)} %clamp.7, (f32[12,64,128]{2,1,0:T(8,128)S(1)}, f32[12,64,128]{2,1,0:T(8,128)S(1)}, f32[12,64,128]{2,1,0:T(8,128)S(1)}) %tuple.72, (f32[12,64,128]{2,1,0:T(8,128)S(1)}, ...), branch_computations={%region_3.4_spmd, %region_4.5_spmd, %region_5.6_spmd, %region_6.7_... | conditional | bytes 737424 | solution.py:78
  80.5 4.8 %collective-permute-start.3 = (f32[12,8,128]{2,1,0:T(8,128)S(1)}, f32[12,8,128]{2,1,0:T(8,128)}, u32[]{:S(2)}, u32[]{:S(2)}) collective-permute-start(f32[12,8,128]{2,1,0:T(8,128)S(1)} %slice.756), channel_id=1, source_target_pairs={{0,8},{1,7},{2,6},{3,5},{4,4},{5,3},{6,2},{7,1},{8,0},{9,63},{10,6... | collective-permute-start | bytes 147464 | tf_op jit(solution)/shard_map/cond/branch_1_fun/ppermute | solution.py:71
  85.7 2.4 %collective-permute-start.4 = (f32[12,64,8]{1,2,0:T(8,128)S(1)}, f32[12,64,8]{1,2,0:T(8,128)S(1)}, u32[]{:S(2)}, u32[]{:S(2)}) collective-permute-start(f32[12,64,8]{1,2,0:T(8,128)S(1)} %copy.104), channel_id=1, source_target_pairs={{0,1},{1,2},{2,3},{3,4},{4,5},{5,6},{6,7},{7,8},{8,9},{9,10},{10,1... | collective-permute-start | bytes 73736 | tf_op jit(solution)/shard_map/cond/branch_1_fun/ppermute | solution.py:72
  88.3 5.5 %collective-permute-start.5 = (f32[12,64,8]{1,2,0:T(8,128)S(1)}, f32[12,64,8]{1,2,0:T(8,128)S(1)}, u32[]{:S(2)}, u32[]{:S(2)}) collective-permute-start(f32[12,64,8]{1,2,0:T(8,128)S(1)} %copy.105), channel_id=1, source_target_pairs={{0,63},{1,0},{2,1},{3,2},{4,3},{5,4},{6,5},{7,6},{8,7},{9,8},{10,9... | collective-permute-start | bytes 73736 | tf_op jit(solution)/shard_map/cond/branch_1_fun/ppermute | solution.py:73
  93.8 0.5 collective-permute-done.4
  94.5 1.1 collective-permute-done.5
  95.7 0.3 collective-permute-done.3
  96.1 28.0 %conditional.3 = (f32[12,8,128]{2,1,0:T(8,128)}, f32[12,8,128]{2,1,0:T(8,128)}, f32[12,8,128]{2,1,0:T(8,128)}, f32[12,8,128]{2,1,0:T(8,128)}, f32[12,8,144]{2,1,0:T(8,128)}, /*index=5*/f32[12,8,144]{2,1,0:T(8,128)}) conditional(s32[]{:T(128)} %clamp.6, (f32[12,8,128]{2,1,0:T(8,128)}, f32[12,8,144]{2,1,0:T(8,128)S(1)}, ...), branch_computations={%region_11.12_spmd, %region_12.13_spmd, %region_13.14_spmd, %regio... | conditional | bytes 1229088 | solution.py:99
  96.1 6.1 %collective-permute-start.30 = (f32[12,8,128]{2,1,0:T(8,128)}, f32[12,8,128]{2,1,0:T(8,128)}, u32[]{:S(2)}, u32[]{:S(2)}) collective-permute-start(f32[12,8,128]{2,1,0:T(8,128)} %get-tuple-element.123), channel_id=1, source_target_pairs={{0,63},{1,0},{2,1},{3,2},{4,3},{5,4},{6,5},{7,6},{8,7},{9,8},{10,9... | collective-permute-start | bytes 147464 | tf_op jit(solution)/shard_map/cond/branch_1_fun/ppermute | solution.py:90
  102.3 1.9 %collective-permute-start.34 = (f32[12,8,144]{2,1,0:T(8,128)S(1)}, f32[12,8,144]{2,1,0:T(8,128)}, u32[]{:S(2)}, u32[]{:S(2)}) collective-permute-start(f32[12,8,144]{2,1,0:T(8,128)S(1)} %get-tuple-element.124), channel_id=1, source_target_pairs={{0,64},{64,128},{128,192},{192,256},{256,320},{320,384},{384,448},... | collective-permute-start | bytes 165896 | tf_op jit(solution)/shard_map/cond/branch_1_fun/ppermute | solution.py:93
  104.2 7.3 %collective-permute-start.35 = (f32[12,8,144]{2,1,0:T(8,128)S(1)}, f32[12,8,144]{2,1,0:T(8,128)}, u32[]{:S(2)}, u32[]{:S(2)}) collective-permute-start(f32[12,8,144]{2,1,0:T(8,128)S(1)} %get-tuple-element.125), channel_id=1, source_target_pairs={{64,0},{128,64},{192,128},{256,192},{320,256},{384,320},{448,384},... | collective-permute-start | bytes 165896 | tf_op jit(solution)/shard_map/cond/branch_1_fun/ppermute | solution.py:94
  111.5 1.4 %collective-permute-start.31 = (f32[12,8,128]{2,1,0:T(8,128)}, f32[12,8,128]{2,1,0:T(8,128)}, u32[]{:S(2)}, u32[]{:S(2)}) collective-permute-start(f32[12,8,128]{2,1,0:T(8,128)} %get-tuple-element.123), channel_id=1, source_target_pairs={{0,0},{1,1},{2,2},{3,3},{4,4},{5,5},{6,6},{7,7},{8,8},{9,9},{10,10... | collective-permute-start | bytes 147464 | tf_op jit(solution)/shard_map/cond/branch_1_fun/ppermute | solution.py:90
  112.9 1.9 %collective-permute-start.32 = (f32[12,8,128]{2,1,0:T(8,128)}, f32[12,8,128]{2,1,0:T(8,128)}, u32[]{:S(2)}, u32[]{:S(2)}) collective-permute-start(f32[12,8,128]{2,1,0:T(8,128)} %get-tuple-element.123), channel_id=1, source_target_pairs={{0,1},{1,2},{2,3},{3,4},{4,5},{5,6},{6,7},{7,8},{8,9},{9,10},{10,1... | collective-permute-start | bytes 147464 | tf_op jit(solution)/shard_map/cond/branch_1_fun/ppermute | solution.py:90
  114.8 1.9 %collective-permute-start.33 = (f32[12,8,128]{2,1,0:T(8,128)}, f32[12,8,128]{2,1,0:T(8,128)}, u32[]{:S(2)}, u32[]{:S(2)}) collective-permute-start(f32[12,8,128]{2,1,0:T(8,128)} %get-tuple-element.123), channel_id=1, source_target_pairs={{0,2},{1,3},{2,4},{3,5},{4,6},{5,7},{6,8},{7,9},{8,10},{9,11},{10,... | collective-permute-start | bytes 147464 | tf_op jit(solution)/shard_map/cond/branch_1_fun/ppermute | solution.py:90
  116.7 4.5 %collective-permute-done.32 = f32[12,8,128]{2,1,0:T(8,128)} collective-permute-done((f32[12,8,128]{2,1,0:T(8,128)}, f32[12,8,128]{2,1,0:T(8,128)}, u32[]{:S(2)}, u32[]{:S(2)}) %collective-permute-start.32) | collective-permute-done | bytes 49184 | tf_op jit(solution)/shard_map/cond/branch_1_fun/ppermute | solution.py:90
  121.3 2.9 %collective-permute-done.33 = f32[12,8,128]{2,1,0:T(8,128)} collective-permute-done((f32[12,8,128]{2,1,0:T(8,128)}, f32[12,8,128]{2,1,0:T(8,128)}, u32[]{:S(2)}, u32[]{:S(2)}) %collective-permute-start.33) | collective-permute-done | bytes 49184 | tf_op jit(solution)/shard_map/cond/branch_1_fun/ppermute | solution.py:90
  124.1 1.0 fusion.2
  125.2 0.2 reverse
  125.3 0.7 copy-done.9
  126.0 1.0 multiply_select_fusion
  127.0 1.3 pad_maximum_fusion
  128.3 0.2 fusion.46
  128.6 0.2 fusion.39
  128.9 0.3 fusion.30
  129.2 0.3 fusion.21
  129.6 0.2 fusion.15
  130.1 0.3 fusion.105
  130.4 0.3 fusion.96
  130.8 0.2 fusion.90
  131.3 0.3 fusion.74
  131.6 0.3 fusion.65
  131.9 0.2 fusion.59
  132.5 0.7 slice.918
  133.6 0.6 copy-done.1
  134.4 0.7 maximum_multiply_fusion
  (90 shorter events, 4.9 us)
Async XLA Ops:
  0.6 0.7 copy-start.10
  5.5 34.3 %copy-start.6 = (f32[2,64,128]{2,1,0:T(8,128)S(1)}, f32[2,64,128]{2,1,0:T(8,128)}, u32[]{:S(2)}) copy-start(f32[2,64,128]{2,1,0:T(8,128)} %param.30) | copy-start | bytes 196612
  5.5 73.6 %all-to-all-start = ((f32[64,1,1026]{2,1,0:T(1,128)}), f32[64,1,1026]{2,1,0:T(1,128)S(1)}, u32[]{:S(2)}, u32[]{:S(2)}) async-start(f32[64,1,1026]{2,1,0:T(1,128)} %copy.100), calls=%async_computation | async-start | bytes 589824 | tf_op jit(solution)/shard_map/all_to_all | solution.py:48
  38.8 0.9 copy-start.4
  39.7 0.9 copy-start.5
  39.7 1.0 copy-start.3
  39.8 1.0 copy-start
  40.8 0.8 copy-start.2
  79.8 0.8 copy-start.7
  80.5 15.4 %collective-permute-start.3 = (f32[12,8,128]{2,1,0:T(8,128)S(1)}, f32[12,8,128]{2,1,0:T(8,128)}, u32[]{:S(2)}, u32[]{:S(2)}) collective-permute-start(f32[12,8,128]{2,1,0:T(8,128)S(1)} %slice.756), channel_id=1, source_target_pairs={{0,8},{1,7},{2,6},{3,5},{4,4},{5,3},{6,2},{7,1},{8,0},{9,63},{10,6... | collective-permute-start | bytes 147464 | tf_op jit(solution)/shard_map/cond/branch_1_fun/ppermute | solution.py:71
  85.7 8.6 %collective-permute-start.4 = (f32[12,64,8]{1,2,0:T(8,128)S(1)}, f32[12,64,8]{1,2,0:T(8,128)S(1)}, u32[]{:S(2)}, u32[]{:S(2)}) collective-permute-start(f32[12,64,8]{1,2,0:T(8,128)S(1)} %copy.104), channel_id=1, source_target_pairs={{0,1},{1,2},{2,3},{3,4},{4,5},{5,6},{6,7},{7,8},{8,9},{9,10},{10,1... | collective-permute-start | bytes 73736 | tf_op jit(solution)/shard_map/cond/branch_1_fun/ppermute | solution.py:72
  88.3 7.3 %collective-permute-start.5 = (f32[12,64,8]{1,2,0:T(8,128)S(1)}, f32[12,64,8]{1,2,0:T(8,128)S(1)}, u32[]{:S(2)}, u32[]{:S(2)}) collective-permute-start(f32[12,64,8]{1,2,0:T(8,128)S(1)} %copy.105), channel_id=1, source_target_pairs={{0,63},{1,0},{2,1},{3,2},{4,3},{5,4},{6,5},{7,6},{8,7},{9,8},{10,9... | collective-permute-start | bytes 73736 | tf_op jit(solution)/shard_map/cond/branch_1_fun/ppermute | solution.py:73
  96.1 18.7 %collective-permute-start.30 = (f32[12,8,128]{2,1,0:T(8,128)}, f32[12,8,128]{2,1,0:T(8,128)}, u32[]{:S(2)}, u32[]{:S(2)}) collective-permute-start(f32[12,8,128]{2,1,0:T(8,128)} %get-tuple-element.123), channel_id=1, source_target_pairs={{0,63},{1,0},{2,1},{3,2},{4,3},{5,4},{6,5},{7,6},{8,7},{9,8},{10,9... | collective-permute-start | bytes 147464 | tf_op jit(solution)/shard_map/cond/branch_1_fun/ppermute | solution.py:90
  102.3 21.9 %collective-permute-start.34 = (f32[12,8,144]{2,1,0:T(8,128)S(1)}, f32[12,8,144]{2,1,0:T(8,128)}, u32[]{:S(2)}, u32[]{:S(2)}) collective-permute-start(f32[12,8,144]{2,1,0:T(8,128)S(1)} %get-tuple-element.124), channel_id=1, source_target_pairs={{0,64},{64,128},{128,192},{192,256},{256,320},{320,384},{384,448},... | collective-permute-start | bytes 165896 | tf_op jit(solution)/shard_map/cond/branch_1_fun/ppermute | solution.py:93
  104.2 19.9 %collective-permute-start.35 = (f32[12,8,144]{2,1,0:T(8,128)S(1)}, f32[12,8,144]{2,1,0:T(8,128)}, u32[]{:S(2)}, u32[]{:S(2)}) collective-permute-start(f32[12,8,144]{2,1,0:T(8,128)S(1)} %get-tuple-element.125), channel_id=1, source_target_pairs={{64,0},{128,64},{192,128},{256,192},{320,256},{384,320},{448,384},... | collective-permute-start | bytes 165896 | tf_op jit(solution)/shard_map/cond/branch_1_fun/ppermute | solution.py:94
  111.5 5.3 %collective-permute-start.31 = (f32[12,8,128]{2,1,0:T(8,128)}, f32[12,8,128]{2,1,0:T(8,128)}, u32[]{:S(2)}, u32[]{:S(2)}) collective-permute-start(f32[12,8,128]{2,1,0:T(8,128)} %get-tuple-element.123), channel_id=1, source_target_pairs={{0,0},{1,1},{2,2},{3,3},{4,4},{5,5},{6,6},{7,7},{8,8},{9,9},{10,10... | collective-permute-start | bytes 147464 | tf_op jit(solution)/shard_map/cond/branch_1_fun/ppermute | solution.py:90
  112.9 8.4 %collective-permute-start.32 = (f32[12,8,128]{2,1,0:T(8,128)}, f32[12,8,128]{2,1,0:T(8,128)}, u32[]{:S(2)}, u32[]{:S(2)}) collective-permute-start(f32[12,8,128]{2,1,0:T(8,128)} %get-tuple-element.123), channel_id=1, source_target_pairs={{0,1},{1,2},{2,3},{3,4},{4,5},{5,6},{6,7},{7,8},{8,9},{9,10},{10,1... | collective-permute-start | bytes 147464 | tf_op jit(solution)/shard_map/cond/branch_1_fun/ppermute | solution.py:90
  114.8 9.3 %collective-permute-start.33 = (f32[12,8,128]{2,1,0:T(8,128)}, f32[12,8,128]{2,1,0:T(8,128)}, u32[]{:S(2)}, u32[]{:S(2)}) collective-permute-start(f32[12,8,128]{2,1,0:T(8,128)} %get-tuple-element.123), channel_id=1, source_target_pairs={{0,2},{1,3},{2,4},{3,5},{4,6},{5,7},{6,8},{7,9},{8,10},{9,11},{10,... | collective-permute-start | bytes 147464 | tf_op jit(solution)/shard_map/cond/branch_1_fun/ppermute | solution.py:90
  125.3 0.7 copy-start.9
  133.6 0.6 copy-start.1
  133.6 0.8 copy-start.8

commit v4 on v3

--- a/solution.py
+++ b/solution.py
@@ -65,10 +65,15 @@
     low = 8 if nx % 8 == 0 else 1
     a = fold_start // low
     b = fold_start % low
+    top_row = (ny - 1) * nx
+    both = ("gy", "gx")
+
+    def on_top(target):
+        return [(top_row + e, top_row + target(e) % nx) for e in range(nx)]
 
     def stage_one(aa):
         def run(top, west_in, east_in):
-            mirrored = lax.ppermute(top, "gx", [(e, (low * aa - e) % nx) for e in range(nx)])
+            mirrored = lax.ppermute(top, both, on_top(lambda e: low * aa - e))
             west = lax.ppermute(west_in, "gx", shift_pairs(nx, 1, True))
             east = lax.ppermute(east_in, "gx", shift_pairs(nx, -1, True))
             return mirrored, west, east
@@ -83,24 +88,30 @@
         stack[:, :, :w],
     )
     wide = jnp.concatenate([west, stack, east], axis=2)
-
-    def stage_two(bb):
+    spans = ((-2, -1, 0), (-1, 0, 1))
+    span = jnp.where(fold_rest < w - 1, 0, 1)
+
+    def stage_two(bb, ts):
         def run(y, south_in, north_in):
-            parts = tuple(
-                lax.ppermute(y, "gx", [(e, (e + bb + t) % nx) for e in range(nx)])
-                for t in (-2, -1, 0, 1)
-            )
+            parts = [
+                lax.ppermute(y, both, on_top(lambda e, t=t: e + bb + t)) for t in ts
+            ]
             south = lax.ppermute(south_in, "gy", shift_pairs(ny, 1, False))
             north = lax.ppermute(north_in, "gy", shift_pairs(ny, -1, False))
-            return parts, south, north
+            return tuple(parts), south, north
 
         return run
 
     parts, south, north = lax.switch(
-        b, [stage_two(bb) for bb in range(low)], mirrored, wide[:, -w:, :], wide[:, :w, :]
+        b * len(spans) + span,
+        [stage_two(bb, ts) for bb in range(low) for ts in spans],
+        mirrored,
+        wide[:, -w:, :],
+        wide[:, :w, :],
     )
     strip = jnp.concatenate(parts, axis=-1)
-    first = 2 * cols + fold_rest - (cols - 1) - w
+    lowest = jnp.where(span == 0, 2, 1)
+    first = lowest * cols + fold_rest - (cols - 1) - w
     window = lax.dynamic_slice_in_dim(strip, first, cols + 2 * w, axis=2)
     folded = jnp.flip(window, axis=(1, 2)) * signs
     north = jnp.where(lax.axis_index("gy") == ny - 1, folded, north)
@@ -151,9 +162,7 @@
     velocity,
     eastward_force,
     northward_force,
-    wind,
-    ocean_current_east,
-    ocean_current_north,
+    forcing,
     ice_mass_per_area,
     coriolis_parameter,
     velocity_mask,
@@ -162,16 +171,10 @@
     north = velocity[1]
     implicit_denominator = ice_mass_per_area + DTE * DRAG
     right_side_east = east * ice_mass_per_area + DTE * (
-        eastward_force
-        + wind[0]
-        + DRAG * ocean_current_east
-        + ice_mass_per_area * coriolis_parameter * north
+        eastward_force + forcing[0] + ice_mass_per_area * coriolis_parameter * north
     )
     right_side_north = north * ice_mass_per_area + DTE * (
-        northward_force
-        + wind[1]
-        + DRAG * ocean_current_north
-        - ice_mass_per_area * coriolis_parameter * east
+        northward_force + forcing[1] - ice_mass_per_area * coriolis_parameter * east
     )
     return jnp.stack(
         [
@@ -238,15 +241,13 @@
             stress,
             strength[None],
             ice_mass_per_area[None],
-            wind,
-            ocean_current_east[None],
-            ocean_current_north[None],
+            wind + DRAG * jnp.stack([ocean_current_east, ocean_current_north]),
             velocity_mask[None],
         ],
         axis=0,
     )
     signs = jnp.array(
-        [-1.0, -1.0, 1.0, 1.0, 1.0, 1.0, 1.0, -1.0, -1.0, -1.0, -1.0, 1.0], jnp.float32
+        [-1.0, -1.0, 1.0, 1.0, 1.0, 1.0, 1.0, -1.0, -1.0, 1.0], jnp.float32
     ).reshape(-1, 1, 1)
     ext = exchange(stack, width, signs, fold_start, fold_rest)
     grid_row = lax.axis_index("gy") * rows + jnp.arange(-width, rows + width, dtype=jnp.int32)
@@ -279,11 +280,9 @@
             eastward_force,
             northward_force,
             crop(ext[7:9], n),
-            crop(ext[9], n),
-            crop(ext[10], n),
             crop(ext[6], n),
             rows_crop(coriolis_ext, n),
-            crop(ext[11], n),
+            crop(ext[9], n),
         )
         vel = jnp.where(rows_crop(inside_ext, n), vel, 0.0)
     velocity = vel

time: 136 us -> 121 us (0.89)
  the two profiles are of different devices: /device:TPU:4 before, /device:TPU:63 now
where the time goes in v4:
time: 121 us; the launch traced here: 120 us
  starting transfers between devices  59.4 us (49%)
  waiting for transfers between devices  38.2 us (32%)
  local copies, waits for them, and re-layouts  11.4 us (9%)
  other arithmetic  7.67 us (6%)
  between operations  3.04 us (3%)
    all_to_all x1, waiting for transfers between devices, regroup_local(): lax.all_to_all(packed, 'gx', split_axis=0, concat_axis=0, tiled=True)  31.7 us
    all_to_all x1, starting transfers between devices, regroup_local(): lax.all_to_all(packed, 'gx', split_axis=0, concat_axis=0, tiled=True)  29.4 us
    ppermute x3, starting transfers between devices, run(): lax.ppermute(y, both, on_top(lambda e, t=t: e + bb + t))  12.7 us
    ppermute x1, starting transfers between devices, run(): north = lax.ppermute(north_in, 'gy', shift_pairs(ny, -1, False))  6.48 us
    ppermute x1, starting transfers between devices, run(): west = lax.ppermute(west_in, 'gx', shift_pairs(nx, 1, True))  5.6 us
    unnamed x27, local copies, waits for them, and re-layouts  5.12 us
    ppermute x3, waiting for transfers between devices, run(): lax.ppermute(y, both, on_top(lambda e, t=t: e + bb + t))  3.46 us
    ppermute x1, waiting for transfers between devices, run(): east = lax.ppermute(east_in, 'gx', shift_pairs(nx, -1, True))  2.95 us
  transfers between devices with their start and end apart: 9, of which 3 were waited for; matrix products, arithmetic and copies ran while one was open for 2% of the time, Pallas kernels for 0%

profile of v4, /device:TPU:63, one launch (start us, length us, event | category | flops | bytes accessed | tf_op | source)
XLA Modules:
  0.0 120.4 jit_solution(973626567649045978)
XLA Ops:
  0.6 0.5 broadcast.423
  1.3 0.7 reduce.3
  2.6 1.0 reshape.177
  3.5 0.4 fusion.147
  4.0 1.0 copy.100
  5.0 29.4 %all-to-all-start = ((f32[64,1,1026]{2,1,0:T(1,128)}), f32[64,1,1026]{2,1,0:T(1,128)S(1)}, u32[]{:S(2)}, u32[]{:S(2)}) async-start(f32[64,1,1026]{2,1,0:T(1,128)} %copy.100), calls=%async_computation | async-start | bytes 589824 | tf_op jit(solution)/shard_map/all_to_all | solution.py:48
  34.4 1.2 slice.555
  38.6 0.3 copy-done.3
  38.9 0.5 copy-done.4
  39.5 0.3 copy-done.2
  39.9 31.7 %all-to-all-done = f32[64,1,1026]{2,1,0:T(1,128)S(1)} async-done(((f32[64,1,1026]{2,1,0:T(1,128)}), f32[64,1,1026]{2,1,0:T(1,128)S(1)}, u32[]{:S(2)}, u32[]{:S(2)}) %all-to-all-start) | async-done | bytes 262688 | tf_op jit(solution)/shard_map/all_to_all | solution.py:48
  71.9 0.1 eq.47
  72.0 0.3 fusion.138
  72.4 0.8 copy-done.6
  73.2 0.7 copy-done.7
  73.9 13.2 %conditional.2 = (f32[10,8,128]{2,1,0:T(8,128)}, f32[10,64,8]{2,1,0:T(8,128)S(1)}, f32[10,64,8]{2,1,0:T(8,128)S(1)}) conditional(s32[]{:T(128)} %clamp.7, (f32[10,64,128]{2,1,0:T(8,128)S(1)}, f32[10,64,128]{2,1,0:T(8,128)S(1)}, f32[10,64,128]{2,1,0:T(8,128)S(1)}) %tuple.104, (f32[10,64,128]{2,1,0:T(8,128)S(1)}, ...), branch_computations={%region_3.4_spmd, %region_4.5_spmd, %region_5.6_spmd, %region_6.7_... | conditional | bytes 614544 | solution.py:83
  74.0 1.9 %collective-permute-start = (f32[10,8,128]{2,1,0:T(8,128)S(1)}, f32[10,8,128]{2,1,0:T(8,128)}, u32[]{:S(2)}, u32[]{:S(2)}) collective-permute-start(f32[10,8,128]{2,1,0:T(8,128)S(1)} %slice.709), channel_id=1, source_target_pairs={{960,960},{961,1023},{962,1022},{963,1021},{964,1020},{965,1019},{... | collective-permute-start | bytes 122888 | tf_op jit(solution)/shard_map/cond/branch_0_fun/ppermute | solution.py:76
  75.9 0.1 slice.717
  76.2 5.6 %collective-permute-start.1 = (f32[10,64,8]{1,2,0:T(8,128)S(1)}, f32[10,64,8]{1,2,0:T(8,128)S(1)}, u32[]{:S(2)}, u32[]{:S(2)}) collective-permute-start(f32[10,64,8]{1,2,0:T(8,128)S(1)} %copy.102), channel_id=1, source_target_pairs={{0,1},{1,2},{2,3},{3,4},{4,5},{5,6},{6,7},{7,8},{8,9},{9,10},{10,1... | collective-permute-start | bytes 61448 | tf_op jit(solution)/shard_map/cond/branch_0_fun/ppermute | solution.py:77
  81.9 1.9 %collective-permute-start.2 = (f32[10,64,8]{1,2,0:T(8,128)S(1)}, f32[10,64,8]{1,2,0:T(8,128)S(1)}, u32[]{:S(2)}, u32[]{:S(2)}) collective-permute-start(f32[10,64,8]{1,2,0:T(8,128)S(1)} %copy.103), channel_id=1, source_target_pairs={{0,63},{1,0},{2,1},{3,2},{4,3},{5,4},{6,5},{7,6},{8,7},{9,8},{10,9... | collective-permute-start | bytes 61448 | tf_op jit(solution)/shard_map/cond/branch_0_fun/ppermute | solution.py:78
  84.0 3.0 %collective-permute-done.2 = f32[10,64,8]{1,2,0:T(8,128)S(1)} collective-permute-done((f32[10,64,8]{1,2,0:T(8,128)S(1)}, f32[10,64,8]{1,2,0:T(8,128)S(1)}, u32[]{:S(2)}, u32[]{:S(2)}) %collective-permute-start.2) | collective-permute-done | bytes 20512 | tf_op jit(solution)/shard_map/cond/branch_0_fun/ppermute | solution.py:78
  87.3 24.0 %conditional.3 = (f32[10,8,128]{2,1,0:T(8,128)}, f32[10,8,128]{2,1,0:T(8,128)}, f32[10,8,128]{2,1,0:T(8,128)}, f32[10,8,144]{2,1,0:T(8,128)}, f32[10,8,144]{2,1,0:T(8,128)}) conditional(s32[]{:T(128)} %clamp.6, (f32[10,8,128]{2,1,0:T(8,128)}, f32[10,8,144]{2,1,0:T(8,128)S(1)}, ...), branch_computations={%region_11.12_spmd, %region_12.13_spmd, %region_13.14_spmd, %regio... | conditional | bytes 860400 | solution.py:105
  87.3 1.3 %collective-permute-start.42 = (f32[10,8,144]{2,1,0:T(8,128)S(1)}, f32[10,8,144]{2,1,0:T(8,128)}, u32[]{:S(2)}, u32[]{:S(2)}) collective-permute-start(f32[10,8,144]{2,1,0:T(8,128)S(1)} %get-tuple-element.178), channel_id=1, source_target_pairs={{0,64},{64,128},{128,192},{192,256},{256,320},{320,384},{384,448},... | collective-permute-start | bytes 138248 | tf_op jit(solution)/shard_map/cond/branch_3_fun/ppermute | solution.py:99
  88.6 6.5 %collective-permute-start.43 = (f32[10,8,144]{2,1,0:T(8,128)S(1)}, f32[10,8,144]{2,1,0:T(8,128)}, u32[]{:S(2)}, u32[]{:S(2)}) collective-permute-start(f32[10,8,144]{2,1,0:T(8,128)S(1)} %get-tuple-element.179), channel_id=1, source_target_pairs={{64,0},{128,64},{192,128},{256,192},{320,256},{384,320},{448,384},... | collective-permute-start | bytes 138248 | tf_op jit(solution)/shard_map/cond/branch_3_fun/ppermute | solution.py:100
  95.1 2.0 %collective-permute-start.39 = (f32[10,8,128]{2,1,0:T(8,128)}, f32[10,8,128]{2,1,0:T(8,128)}, u32[]{:S(2)}, u32[]{:S(2)}) collective-permute-start(f32[10,8,128]{2,1,0:T(8,128)} %get-tuple-element.177), channel_id=1, source_target_pairs={{960,960},{961,961},{962,962},{963,963},{964,964},{965,965},{966,9... | collective-permute-start | bytes 122888 | tf_op jit(solution)/shard_map/cond/branch_3_fun/ppermute | solution.py:97
  97.1 6.1 %collective-permute-start.40 = (f32[10,8,128]{2,1,0:T(8,128)}, f32[10,8,128]{2,1,0:T(8,128)}, u32[]{:S(2)}, u32[]{:S(2)}) collective-permute-start(f32[10,8,128]{2,1,0:T(8,128)} %get-tuple-element.177), channel_id=1, source_target_pairs={{960,961},{961,962},{962,963},{963,964},{964,965},{965,966},{966,9... | collective-permute-start | bytes 122888 | tf_op jit(solution)/shard_map/cond/branch_3_fun/ppermute | solution.py:97
  103.2 4.6 %collective-permute-start.41 = (f32[10,8,128]{2,1,0:T(8,128)}, f32[10,8,128]{2,1,0:T(8,128)}, u32[]{:S(2)}, u32[]{:S(2)}) collective-permute-start(f32[10,8,128]{2,1,0:T(8,128)} %get-tuple-element.177), channel_id=1, source_target_pairs={{960,962},{961,963},{962,964},{963,965},{964,966},{965,967},{966,9... | collective-permute-start | bytes 122888 | tf_op jit(solution)/shard_map/cond/branch_3_fun/ppermute | solution.py:97
  107.8 3.5 %collective-permute-done.41 = f32[10,8,128]{2,1,0:T(8,128)} collective-permute-done((f32[10,8,128]{2,1,0:T(8,128)}, f32[10,8,128]{2,1,0:T(8,128)}, u32[]{:S(2)}, u32[]{:S(2)}) %collective-permute-start.41) | collective-permute-done | bytes 40992 | tf_op jit(solution)/shard_map/cond/branch_3_fun/ppermute | solution.py:97
  111.3 0.9 fusion.1
  112.2 0.2 reverse
  112.4 0.7 copy-done.9
  113.2 1.2 %pad_maximum_fusion = f32[10,80,144]{2,1,0:T(8,128)S(1)} fusion(f32[10,8,144]{2,1,0:T(8,128)S(1)} %multiply_select_fusion, f32[10,64,8]{2,1,0:T(8,128)S(1)} %get-tuple-element.356, f32[10,64,128]{2,1,0:T(8,128)S(1)} %bitcast_dynamic-update-slice_fusion, f32[10,64,8]{2,1,0:T(8,128)S(1)} %get-tuple-element.355, f32[10,8,144]{2,1,0:T(8,128)} %get-tuple-element.230), kind=kLoop, calls=%fused_computation | loop fusion | flops 460800 | bytes 921600 | tf_op jit(solution)/shard_map/concatenate | solution.py:118
  114.4 0.2 fusion.45
  114.7 0.2 fusion.38
  115.0 0.3 fusion.30
  115.4 0.2 fusion.14
  115.7 0.2 fusion.7
  116.0 0.3 fusion.105
  116.4 0.2 fusion.89
  116.7 0.2 fusion.82
  117.0 0.3 fusion.74
  117.4 0.2 fusion.58
  117.6 0.2 fusion.51
  117.9 0.7 slice.864
  118.7 0.2 fusion.133
  119.0 0.6 copy-done.1
  119.5 0.2 copy-done.8
  119.7 0.7 maximum_multiply_fusion
  (83 shorter events, 3.7 us)
Async XLA Ops:
  0.6 0.7 copy-start.10
  5.0 66.7 %all-to-all-start = ((f32[64,1,1026]{2,1,0:T(1,128)}), f32[64,1,1026]{2,1,0:T(1,128)S(1)}, u32[]{:S(2)}, u32[]{:S(2)}) async-start(f32[64,1,1026]{2,1,0:T(1,128)} %copy.100), calls=%async_computation | async-start | bytes 589824 | tf_op jit(solution)/shard_map/all_to_all | solution.py:48
  37.6 1.3 %copy-start.5 = (f32[2,64,128]{2,1,0:T(8,128)S(1)}, f32[2,64,128]{2,1,0:T(8,128)}, u32[]{:S(2)}) copy-start(f32[2,64,128]{2,1,0:T(8,128)} %param.38) | copy-start | bytes 196612
  38.1 0.8 copy-start.3
  38.6 0.9 copy-start.4
  38.9 0.9 copy-start.2
  38.9 1.0 copy-start
  72.3 0.8 copy-start.6
  73.2 0.8 copy-start.7
  74.0 13.1 %collective-permute-start = (f32[10,8,128]{2,1,0:T(8,128)S(1)}, f32[10,8,128]{2,1,0:T(8,128)}, u32[]{:S(2)}, u32[]{:S(2)}) collective-permute-start(f32[10,8,128]{2,1,0:T(8,128)S(1)} %slice.709), channel_id=1, source_target_pairs={{960,960},{961,1023},{962,1022},{963,1021},{964,1020},{965,1019},{... | collective-permute-start | bytes 122888 | tf_op jit(solution)/shard_map/cond/branch_0_fun/ppermute | solution.py:76
  76.2 7.7 %collective-permute-start.1 = (f32[10,64,8]{1,2,0:T(8,128)S(1)}, f32[10,64,8]{1,2,0:T(8,128)S(1)}, u32[]{:S(2)}, u32[]{:S(2)}) collective-permute-start(f32[10,64,8]{1,2,0:T(8,128)S(1)} %copy.102), channel_id=1, source_target_pairs={{0,1},{1,2},{2,3},{3,4},{4,5},{5,6},{6,7},{7,8},{8,9},{9,10},{10,1... | collective-permute-start | bytes 61448 | tf_op jit(solution)/shard_map/cond/branch_0_fun/ppermute | solution.py:77
  81.9 5.0 %collective-permute-start.2 = (f32[10,64,8]{1,2,0:T(8,128)S(1)}, f32[10,64,8]{1,2,0:T(8,128)S(1)}, u32[]{:S(2)}, u32[]{:S(2)}) collective-permute-start(f32[10,64,8]{1,2,0:T(8,128)S(1)} %copy.103), channel_id=1, source_target_pairs={{0,63},{1,0},{2,1},{3,2},{4,3},{5,4},{6,5},{7,6},{8,7},{9,8},{10,9... | collective-permute-start | bytes 61448 | tf_op jit(solution)/shard_map/cond/branch_0_fun/ppermute | solution.py:78
  87.3 24.0 %collective-permute-start.42 = (f32[10,8,144]{2,1,0:T(8,128)S(1)}, f32[10,8,144]{2,1,0:T(8,128)}, u32[]{:S(2)}, u32[]{:S(2)}) collective-permute-start(f32[10,8,144]{2,1,0:T(8,128)S(1)} %get-tuple-element.178), channel_id=1, source_target_pairs={{0,64},{64,128},{128,192},{192,256},{256,320},{320,384},{384,448},... | collective-permute-start | bytes 138248 | tf_op jit(solution)/shard_map/cond/branch_3_fun/ppermute | solution.py:99
  88.6 22.7 %collective-permute-start.43 = (f32[10,8,144]{2,1,0:T(8,128)S(1)}, f32[10,8,144]{2,1,0:T(8,128)}, u32[]{:S(2)}, u32[]{:S(2)}) collective-permute-start(f32[10,8,144]{2,1,0:T(8,128)S(1)} %get-tuple-element.179), channel_id=1, source_target_pairs={{64,0},{128,64},{192,128},{256,192},{320,256},{384,320},{448,384},... | collective-permute-start | bytes 138248 | tf_op jit(solution)/shard_map/cond/branch_3_fun/ppermute | solution.py:100
  95.1 12.7 %collective-permute-start.39 = (f32[10,8,128]{2,1,0:T(8,128)}, f32[10,8,128]{2,1,0:T(8,128)}, u32[]{:S(2)}, u32[]{:S(2)}) collective-permute-start(f32[10,8,128]{2,1,0:T(8,128)} %get-tuple-element.177), channel_id=1, source_target_pairs={{960,960},{961,961},{962,962},{963,963},{964,964},{965,965},{966,9... | collective-permute-start | bytes 122888 | tf_op jit(solution)/shard_map/cond/branch_3_fun/ppermute | solution.py:97
  97.1 10.7 %collective-permute-start.40 = (f32[10,8,128]{2,1,0:T(8,128)}, f32[10,8,128]{2,1,0:T(8,128)}, u32[]{:S(2)}, u32[]{:S(2)}) collective-permute-start(f32[10,8,128]{2,1,0:T(8,128)} %get-tuple-element.177), channel_id=1, source_target_pairs={{960,961},{961,962},{962,963},{963,964},{964,965},{965,966},{966,9... | collective-permute-start | bytes 122888 | tf_op jit(solution)/shard_map/cond/branch_3_fun/ppermute | solution.py:97
  103.2 8.1 %collective-permute-start.41 = (f32[10,8,128]{2,1,0:T(8,128)}, f32[10,8,128]{2,1,0:T(8,128)}, u32[]{:S(2)}, u32[]{:S(2)}) collective-permute-start(f32[10,8,128]{2,1,0:T(8,128)} %get-tuple-element.177), channel_id=1, source_target_pairs={{960,962},{961,963},{962,964},{963,965},{964,966},{965,967},{966,9... | collective-permute-start | bytes 122888 | tf_op jit(solution)/shard_map/cond/branch_3_fun/ppermute | solution.py:97
  112.4 0.7 copy-start.9
  118.9 0.6 copy-start.1
  118.9 0.8 copy-start.8

commit v5 on v4

--- a/solution.py
+++ b/solution.py
@@ -216,11 +216,6 @@
     ocean_land_mask,
     fold_partner_column,
 ):
-    ocean = regroup_local(ocean_blocks, block_map)
-    ocean_temp = ocean[:, 0, :]
-    ocean_salt = ocean[:, 1, :]
-    ocean_current_east = ocean[:, 2, :]
-    ocean_current_north = ocean[:, 3, :]
     hsum = jnp.sum(area * thickness, axis=0)
     conc = jnp.sum(area, axis=0)
     strength = PSTAR * hsum * jnp.exp(-CSTAR * (1.0 - conc))
@@ -241,7 +236,7 @@
             stress,
             strength[None],
             ice_mass_per_area[None],
-            wind + DRAG * jnp.stack([ocean_current_east, ocean_current_north]),
+            wind,
             velocity_mask[None],
         ],
         axis=0,
@@ -249,7 +244,27 @@
     signs = jnp.array(
         [-1.0, -1.0, 1.0, 1.0, 1.0, 1.0, 1.0, -1.0, -1.0, 1.0], jnp.float32
     ).reshape(-1, 1, 1)
-    ext = exchange(stack, width, signs, fold_start, fold_rest)
+    ext_early = exchange(stack, width, signs, fold_start, fold_rest)
+    ocean = regroup_local(ocean_blocks, block_map)
+    ocean_temp = ocean[:, 0, :]
+    ocean_salt = ocean[:, 1, :]
+    ocean_current_east = ocean[:, 2, :]
+    ocean_current_north = ocean[:, 3, :]
+    current_ext = exchange(
+        jnp.stack([ocean_current_east, ocean_current_north]),
+        width,
+        -jnp.ones((2, 1, 1), jnp.float32),
+        fold_start,
+        fold_rest,
+    )
+    ext = jnp.concatenate(
+        [
+            ext_early[:7],
+            ext_early[7:9] + DRAG * current_ext,
+            ext_early[9:10],
+        ],
+        axis=0,
+    )
     grid_row = lax.axis_index("gy") * rows + jnp.arange(-width, rows + width, dtype=jnp.int32)
     true_row = jnp.where(grid_row > total_rows - 1, 2 * total_rows - 1 - grid_row, grid_row)
     coriolis_ext = (FCOR * (true_row.astype(jnp.float32) + 0.5) / float(total_rows))[:, None]

time: 121 us -> 162 us (1.34)
  the two profiles are of different devices: /device:TPU:63 before, /device:TPU:31 now
where the time goes in v5:
time: 162 us; the launch traced here: 161 us
  starting transfers between devices  112 us (69%)
  waiting for transfers between devices  24.2 us (15%)
  local copies, waits for them, and re-layouts  11.6 us (7%)
  other arithmetic  9.48 us (6%)
  between operations  3.08 us (2%)
    ppermute x6, starting transfers between devices, run(): lax.ppermute(y, both, on_top(lambda e, t=t: e + bb + t))  41.7 us
    all_to_all x1, starting transfers between devices, regroup_local(): lax.all_to_all(packed, 'gx', split_axis=0, concat_axis=0, tiled=True)  30 us
    ppermute x6, waiting for transfers between devices, run(): lax.ppermute(y, both, on_top(lambda e, t=t: e + bb + t))  18.6 us
    ppermute x2, starting transfers between devices, run(): mirrored = lax.ppermute(top, both, on_top(lambda e: low * aa - e))  15.5 us
    ppermute x2, starting transfers between devices, run(): west = lax.ppermute(west_in, 'gx', shift_pairs(nx, 1, True))  9.86 us
    ppermute x2, starting transfers between devices, run(): north = lax.ppermute(north_in, 'gy', shift_pairs(ny, -1, False))  7.28 us
    ppermute x2, waiting for transfers between devices, run(): east = lax.ppermute(east_in, 'gx', shift_pairs(nx, -1, True))  5.26 us
    unnamed x29, local copies, waits for them, and re-layouts  4.98 us
  transfers between devices with their start and end apart: 17, of which 6 were waited for; matrix products, arithmetic and copies ran while one was open for 4% of the time, Pallas kernels for 0%

profile of v5, /device:TPU:31, one launch (start us, length us, event | category | flops | bytes accessed | tf_op | source)
XLA Modules:
  0.0 161.3 jit_solution(7792361794153262312)
XLA Ops:
  0.6 0.5 broadcast.423
  1.3 0.7 reduce.3
  2.6 1.0 reshape.177
  3.5 0.4 fusion.149
  4.0 1.0 copy.190
  5.0 30.0 %all-to-all-start = ((f32[64,1,1026]{2,1,0:T(1,128)}), f32[64,1,1026]{2,1,0:T(1,128)S(1)}, u32[]{:S(2)}, u32[]{:S(2)}) async-start(f32[64,1,1026]{2,1,0:T(1,128)} %copy.190), calls=%async_computation | async-start | bytes 589824 | tf_op jit(solution)/shard_map/all_to_all | solution.py:48
  35.0 1.2 slice.561
  39.2 0.9 copy-done.2
  40.2 0.7 copy-done.3
  41.1 0.7 copy-done.7
  41.8 23.8 %conditional.4 = (f32[10,8,128]{2,1,0:T(8,128)}, f32[10,64,8]{2,1,0:T(8,128)S(1)}, f32[10,64,8]{2,1,0:T(8,128)S(1)}) conditional(s32[]{:T(128)} %clamp.9, (f32[10,64,128]{2,1,0:T(8,128)S(1)}, f32[10,64,128]{2,1,0:T(8,128)S(1)}, f32[10,64,128]{2,1,0:T(8,128)S(1)}) %tuple.200, (f32[10,64,128]{2,1,0:T(8,128)S(1)}, ...), branch_computations={%region_2.3_spmd, %region_3.4_spmd, %region_4.5_spmd, %region_5.6_... | conditional | bytes 614544 | solution.py:83
  41.8 12.0 %collective-permute-start.9 = (f32[10,8,128]{2,1,0:T(8,128)S(1)}, f32[10,8,128]{2,1,0:T(8,128)}, u32[]{:S(2)}, u32[]{:S(2)}) collective-permute-start(f32[10,8,128]{2,1,0:T(8,128)S(1)} %slice.724), channel_id=1, source_target_pairs={{960,984},{961,983},{962,982},{963,981},{964,980},{965,979},{966,9... | collective-permute-start | bytes 122888 | tf_op jit(solution)/shard_map/cond/branch_3_fun/ppermute | solution.py:76
  54.1 5.2 %collective-permute-start.10 = (f32[10,64,8]{1,2,0:T(8,128)S(1)}, f32[10,64,8]{1,2,0:T(8,128)S(1)}, u32[]{:S(2)}, u32[]{:S(2)}) collective-permute-start(f32[10,64,8]{1,2,0:T(8,128)S(1)} %copy.174), channel_id=1, source_target_pairs={{0,1},{1,2},{2,3},{3,4},{4,5},{5,6},{6,7},{7,8},{8,9},{9,10},{10,1... | collective-permute-start | bytes 61448 | tf_op jit(solution)/shard_map/cond/branch_3_fun/ppermute | solution.py:77
  59.4 2.2 %collective-permute-start.11 = (f32[10,64,8]{1,2,0:T(8,128)S(1)}, f32[10,64,8]{1,2,0:T(8,128)S(1)}, u32[]{:S(2)}, u32[]{:S(2)}) collective-permute-start(f32[10,64,8]{1,2,0:T(8,128)S(1)} %copy.175), channel_id=1, source_target_pairs={{0,63},{1,0},{2,1},{3,2},{4,3},{5,4},{6,5},{7,6},{8,7},{9,8},{10,9... | collective-permute-start | bytes 61448 | tf_op jit(solution)/shard_map/cond/branch_3_fun/ppermute | solution.py:78
  61.8 3.7 %collective-permute-done.11 = f32[10,64,8]{1,2,0:T(8,128)S(1)} collective-permute-done((f32[10,64,8]{1,2,0:T(8,128)S(1)}, f32[10,64,8]{1,2,0:T(8,128)S(1)}, u32[]{:S(2)}, u32[]{:S(2)}) %collective-permute-start.11) | collective-permute-done | bytes 20512 | tf_op jit(solution)/shard_map/cond/branch_3_fun/ppermute | solution.py:78
  65.8 37.6 %conditional.5 = (f32[10,8,128]{2,1,0:T(8,128)}, f32[10,8,128]{2,1,0:T(8,128)}, f32[10,8,128]{2,1,0:T(8,128)}, f32[10,8,144]{2,1,0:T(8,128)}, f32[10,8,144]{2,1,0:T(8,128)}) conditional(s32[]{:T(128)} %clamp.8, (f32[10,8,128]{2,1,0:T(8,128)}, f32[10,8,144]{2,1,0:T(8,128)S(1)}, ...), branch_computations={%region_10.11_spmd, %region_11.12_spmd, %region_12.13_spmd, %regio... | conditional | bytes 860400 | solution.py:105
  65.8 1.3 collective-permute-start.82
  67.1 3.7 %collective-permute-start.83 = (f32[10,8,144]{2,1,0:T(8,128)S(1)}, f32[10,8,144]{2,1,0:T(8,128)}, u32[]{:S(2)}, u32[]{:S(2)}) collective-permute-start(f32[10,8,144]{2,1,0:T(8,128)S(1)} %get-tuple-element.347), channel_id=1, source_target_pairs={{64,0},{128,64},{192,128},{256,192},{320,256},{384,320},{448,384},... | collective-permute-start | bytes 138248 | tf_op jit(solution)/shard_map/cond/branch_11_fun/ppermute | solution.py:100
  70.8 10.9 %collective-permute-start.79 = (f32[10,8,128]{2,1,0:T(8,128)}, f32[10,8,128]{2,1,0:T(8,128)}, u32[]{:S(2)}, u32[]{:S(2)}) collective-permute-start(f32[10,8,128]{2,1,0:T(8,128)} %get-tuple-element.345), channel_id=1, source_target_pairs={{960,964},{961,965},{962,966},{963,967},{964,968},{965,969},{966,9... | collective-permute-start | bytes 122888 | tf_op jit(solution)/shard_map/cond/branch_11_fun/ppermute | solution.py:97
  81.6 8.7 %collective-permute-start.80 = (f32[10,8,128]{2,1,0:T(8,128)}, f32[10,8,128]{2,1,0:T(8,128)}, u32[]{:S(2)}, u32[]{:S(2)}) collective-permute-start(f32[10,8,128]{2,1,0:T(8,128)} %get-tuple-element.345), channel_id=1, source_target_pairs={{960,965},{961,966},{962,967},{963,968},{964,969},{965,970},{966,9... | collective-permute-start | bytes 122888 | tf_op jit(solution)/shard_map/cond/branch_11_fun/ppermute | solution.py:97
  90.3 4.9 %collective-permute-start.81 = (f32[10,8,128]{2,1,0:T(8,128)}, f32[10,8,128]{2,1,0:T(8,128)}, u32[]{:S(2)}, u32[]{:S(2)}) collective-permute-start(f32[10,8,128]{2,1,0:T(8,128)} %get-tuple-element.345), channel_id=1, source_target_pairs={{960,966},{961,967},{962,968},{963,969},{964,970},{965,971},{966,9... | collective-permute-start | bytes 122888 | tf_op jit(solution)/shard_map/cond/branch_11_fun/ppermute | solution.py:97
  95.3 8.1 %collective-permute-done.81 = f32[10,8,128]{2,1,0:T(8,128)} collective-permute-done((f32[10,8,128]{2,1,0:T(8,128)}, f32[10,8,128]{2,1,0:T(8,128)}, u32[]{:S(2)}, u32[]{:S(2)}) %collective-permute-start.81) | collective-permute-done | bytes 40992 | tf_op jit(solution)/shard_map/cond/branch_11_fun/ppermute | solution.py:97
  103.3 0.9 fusion.1
  104.5 0.7 copy-done.9
  105.2 1.2 pad_maximum_fusion
  107.4 0.3 fusion.138
  107.8 13.3 %conditional.6 = (f32[2,8,128]{2,1,0:T(8,128)}, f32[2,64,8]{2,1,0:T(8,128)S(1)}, f32[2,64,8]{2,1,0:T(8,128)S(1)}) conditional(s32[]{:T(128)} %clamp.9, (f32[2,64,128]{2,1,0:T(8,128)S(1)}, f32[2,64,128]{2,1,0:T(8,128)S(1)}, f32[2,64,128]{2,1,0:T(8,128)S(1)}) %tuple.202, (f32[2,64,128]{2,1,0:T(8,128)S(1)}, ...), branch_computations={%region_27.28_spmd, %region_28.29_spmd, %region_29.30_spmd, %regio... | conditional | bytes 123024 | solution.py:83
  107.8 3.6 %collective-permute-start.113 = (f32[2,8,128]{2,1,0:T(8,128)S(1)}, f32[2,8,128]{2,1,0:T(8,128)}, u32[]{:S(2)}, u32[]{:S(2)}) collective-permute-start(f32[2,8,128]{2,1,0:T(8,128)S(1)} %slice.748), channel_id=1, source_target_pairs={{960,984},{961,983},{962,982},{963,981},{964,980},{965,979},{966,9... | collective-permute-start | bytes 24584 | tf_op jit(solution)/shard_map/cond/branch_3_fun/ppermute | solution.py:76
  111.5 4.7 %collective-permute-start.114 = (f32[2,64,8]{1,2,0:T(8,128)S(1)}, f32[2,64,8]{1,2,0:T(8,128)S(1)}, u32[]{:S(2)}, u32[]{:S(2)}) collective-permute-start(f32[2,64,8]{1,2,0:T(8,128)S(1)} %copy.198), channel_id=1, source_target_pairs={{0,1},{1,2},{2,3},{3,4},{4,5},{5,6},{6,7},{7,8},{8,9},{9,10},{10,1... | collective-permute-start | bytes 12296 | tf_op jit(solution)/shard_map/cond/branch_3_fun/ppermute | solution.py:77
  116.3 2.7 %collective-permute-start.115 = (f32[2,64,8]{1,2,0:T(8,128)S(1)}, f32[2,64,8]{1,2,0:T(8,128)S(1)}, u32[]{:S(2)}, u32[]{:S(2)}) collective-permute-start(f32[2,64,8]{1,2,0:T(8,128)S(1)} %copy.199), channel_id=1, source_target_pairs={{0,63},{1,0},{2,1},{3,2},{4,3},{5,4},{6,5},{7,6},{8,7},{9,8},{10,9... | collective-permute-start | bytes 12296 | tf_op jit(solution)/shard_map/cond/branch_3_fun/ppermute | solution.py:78
  119.1 1.6 collective-permute-done.115
  121.1 32.8 %conditional.7 = (f32[2,8,128]{2,1,0:T(8,128)}, f32[2,8,128]{2,1,0:T(8,128)}, f32[2,8,128]{2,1,0:T(8,128)}, f32[2,8,144]{2,1,0:T(8,128)}, f32[2,8,144]{2,1,0:T(8,128)}) conditional(s32[]{:T(128)} %clamp.8, (f32[2,8,128]{2,1,0:T(8,128)}, f32[2,8,144]{2,1,0:T(8,128)S(1)}, f32[2,8,144]{2,1,0:T(8,128)S(1)}) %tuple.203, ...), branch_computations={%region_35.36_spmd, %region_36.37_spmd, %region_37.38_spmd, %regio... | conditional | bytes 172272 | solution.py:105
  121.1 1.3 collective-permute-start.186
  122.4 3.6 %collective-permute-start.187 = (f32[2,8,144]{2,1,0:T(8,128)S(1)}, f32[2,8,144]{2,1,0:T(8,128)}, u32[]{:S(2)}, u32[]{:S(2)}) collective-permute-start(f32[2,8,144]{2,1,0:T(8,128)S(1)} %get-tuple-element.419), channel_id=1, source_target_pairs={{64,0},{128,64},{192,128},{256,192},{320,256},{384,320},{448,384},... | collective-permute-start | bytes 27656 | tf_op jit(solution)/shard_map/cond/branch_11_fun/ppermute | solution.py:100
  126.1 13.4 %collective-permute-start.183 = (f32[2,8,128]{2,1,0:T(8,128)}, f32[2,8,128]{2,1,0:T(8,128)}, u32[]{:S(2)}, u32[]{:S(2)}) collective-permute-start(f32[2,8,128]{2,1,0:T(8,128)} %get-tuple-element.417), channel_id=1, source_target_pairs={{960,964},{961,965},{962,966},{963,967},{964,968},{965,969},{966,9... | collective-permute-start | bytes 24584 | tf_op jit(solution)/shard_map/cond/branch_11_fun/ppermute | solution.py:97
  139.4 1.9 %collective-permute-start.184 = (f32[2,8,128]{2,1,0:T(8,128)}, f32[2,8,128]{2,1,0:T(8,128)}, u32[]{:S(2)}, u32[]{:S(2)}) collective-permute-start(f32[2,8,128]{2,1,0:T(8,128)} %get-tuple-element.417), channel_id=1, source_target_pairs={{960,965},{961,966},{962,967},{963,968},{964,969},{965,970},{966,9... | collective-permute-start | bytes 24584 | tf_op jit(solution)/shard_map/cond/branch_11_fun/ppermute | solution.py:97
  141.4 1.9 %collective-permute-start.185 = (f32[2,8,128]{2,1,0:T(8,128)}, f32[2,8,128]{2,1,0:T(8,128)}, u32[]{:S(2)}, u32[]{:S(2)}) collective-permute-start(f32[2,8,128]{2,1,0:T(8,128)} %get-tuple-element.417), channel_id=1, source_target_pairs={{960,966},{961,967},{962,968},{963,969},{964,970},{965,971},{966,9... | collective-permute-start | bytes 24584 | tf_op jit(solution)/shard_map/cond/branch_11_fun/ppermute | solution.py:97
  143.3 7.8 %collective-permute-done.184 = f32[2,8,128]{2,1,0:T(8,128)} collective-permute-done((f32[2,8,128]{2,1,0:T(8,128)}, f32[2,8,128]{2,1,0:T(8,128)}, u32[]{:S(2)}, u32[]{:S(2)}) %collective-permute-start.184) | collective-permute-done | bytes 8224 | tf_op jit(solution)/shard_map/cond/branch_11_fun/ppermute | solution.py:97
  151.1 2.8 %collective-permute-done.185 = f32[2,8,128]{2,1,0:T(8,128)} collective-permute-done((f32[2,8,128]{2,1,0:T(8,128)}, f32[2,8,128]{2,1,0:T(8,128)}, u32[]{:S(2)}, u32[]{:S(2)}) %collective-permute-start.185) | collective-permute-done | bytes 8224 | tf_op jit(solution)/shard_map/cond/branch_11_fun/ppermute | solution.py:97
  153.9 0.8 fusion.141
  155.0 0.8 slice_add_fusion
  155.8 0.3 fusion.30
  156.2 0.3 fusion.14
  156.8 0.3 fusion.105
  157.8 0.3 fusion.74
  158.7 0.7 slice.901
  159.8 0.6 copy-done.1
  160.5 0.7 maximum_multiply_fusion
  (113 shorter events, 7.0 us)
Async XLA Ops:
  0.6 0.7 copy-start.10
  5.0 34.2 %copy-start.5 = (f32[2,64,128]{2,1,0:T(8,128)S(1)}, f32[2,64,128]{2,1,0:T(8,128)}, u32[]{:S(2)}) copy-start(f32[2,64,128]{2,1,0:T(8,128)} %param.62) | copy-start | bytes 196612
  5.0 102.1 %all-to-all-start = ((f32[64,1,1026]{2,1,0:T(1,128)}), f32[64,1,1026]{2,1,0:T(1,128)S(1)}, u32[]{:S(2)}, u32[]{:S(2)}) async-start(f32[64,1,1026]{2,1,0:T(1,128)} %copy.190), calls=%async_computation | async-start | bytes 589824 | tf_op jit(solution)/shard_map/all_to_all | solution.py:48
  38.2 1.0 copy-start.4
  39.1 0.9 copy-start.2
  39.2 1.0 copy-start
  40.2 0.8 copy-start.3
  40.2 0.8 copy-start.6
  41.1 0.8 copy-start.7
  41.8 23.8 %collective-permute-start.9 = (f32[10,8,128]{2,1,0:T(8,128)S(1)}, f32[10,8,128]{2,1,0:T(8,128)}, u32[]{:S(2)}, u32[]{:S(2)}) collective-permute-start(f32[10,8,128]{2,1,0:T(8,128)S(1)} %slice.724), channel_id=1, source_target_pairs={{960,984},{961,983},{962,982},{963,981},{964,980},{965,979},{966,9... | collective-permute-start | bytes 122888 | tf_op jit(solution)/shard_map/cond/branch_3_fun/ppermute | solution.py:76
  54.1 7.5 %collective-permute-start.10 = (f32[10,64,8]{1,2,0:T(8,128)S(1)}, f32[10,64,8]{1,2,0:T(8,128)S(1)}, u32[]{:S(2)}, u32[]{:S(2)}) collective-permute-start(f32[10,64,8]{1,2,0:T(8,128)S(1)} %copy.174), channel_id=1, source_target_pairs={{0,1},{1,2},{2,3},{3,4},{4,5},{5,6},{6,7},{7,8},{8,9},{9,10},{10,1... | collective-permute-start | bytes 61448 | tf_op jit(solution)/shard_map/cond/branch_3_fun/ppermute | solution.py:77
  59.4 6.1 %collective-permute-start.11 = (f32[10,64,8]{1,2,0:T(8,128)S(1)}, f32[10,64,8]{1,2,0:T(8,128)S(1)}, u32[]{:S(2)}, u32[]{:S(2)}) collective-permute-start(f32[10,64,8]{1,2,0:T(8,128)S(1)} %copy.175), channel_id=1, source_target_pairs={{0,63},{1,0},{2,1},{3,2},{4,3},{5,4},{6,5},{7,6},{8,7},{9,8},{10,9... | collective-permute-start | bytes 61448 | tf_op jit(solution)/shard_map/cond/branch_3_fun/ppermute | solution.py:78
  65.8 37.5 %collective-permute-start.82 = (f32[10,8,144]{2,1,0:T(8,128)S(1)}, f32[10,8,144]{2,1,0:T(8,128)}, u32[]{:S(2)}, u32[]{:S(2)}) collective-permute-start(f32[10,8,144]{2,1,0:T(8,128)S(1)} %get-tuple-element.346), channel_id=1, source_target_pairs={{0,64},{64,128},{128,192},{192,256},{256,320},{320,384},{384,448},... | collective-permute-start | bytes 138248 | tf_op jit(solution)/shard_map/cond/branch_11_fun/ppermute | solution.py:99
  67.1 36.2 %collective-permute-start.83 = (f32[10,8,144]{2,1,0:T(8,128)S(1)}, f32[10,8,144]{2,1,0:T(8,128)}, u32[]{:S(2)}, u32[]{:S(2)}) collective-permute-start(f32[10,8,144]{2,1,0:T(8,128)S(1)} %get-tuple-element.347), channel_id=1, source_target_pairs={{64,0},{128,64},{192,128},{256,192},{320,256},{384,320},{448,384},... | collective-permute-start | bytes 138248 | tf_op jit(solution)/shard_map/cond/branch_11_fun/ppermute | solution.py:100
  70.8 24.5 %collective-permute-start.79 = (f32[10,8,128]{2,1,0:T(8,128)}, f32[10,8,128]{2,1,0:T(8,128)}, u32[]{:S(2)}, u32[]{:S(2)}) collective-permute-start(f32[10,8,128]{2,1,0:T(8,128)} %get-tuple-element.345), channel_id=1, source_target_pairs={{960,964},{961,965},{962,966},{963,967},{964,968},{965,969},{966,9... | collective-permute-start | bytes 122888 | tf_op jit(solution)/shard_map/cond/branch_11_fun/ppermute | solution.py:97
  81.6 13.6 %collective-permute-start.80 = (f32[10,8,128]{2,1,0:T(8,128)}, f32[10,8,128]{2,1,0:T(8,128)}, u32[]{:S(2)}, u32[]{:S(2)}) collective-permute-start(f32[10,8,128]{2,1,0:T(8,128)} %get-tuple-element.345), channel_id=1, source_target_pairs={{960,965},{961,966},{962,967},{963,968},{964,969},{965,970},{966,9... | collective-permute-start | bytes 122888 | tf_op jit(solution)/shard_map/cond/branch_11_fun/ppermute | solution.py:97
  90.3 13.0 %collective-permute-start.81 = (f32[10,8,128]{2,1,0:T(8,128)}, f32[10,8,128]{2,1,0:T(8,128)}, u32[]{:S(2)}, u32[]{:S(2)}) collective-permute-start(f32[10,8,128]{2,1,0:T(8,128)} %get-tuple-element.345), channel_id=1, source_target_pairs={{960,966},{961,967},{962,968},{963,969},{964,970},{965,971},{966,9... | collective-permute-start | bytes 122888 | tf_op jit(solution)/shard_map/cond/branch_11_fun/ppermute | solution.py:97
  104.5 0.7 copy-start.9
  107.8 13.2 %collective-permute-start.113 = (f32[2,8,128]{2,1,0:T(8,128)S(1)}, f32[2,8,128]{2,1,0:T(8,128)}, u32[]{:S(2)}, u32[]{:S(2)}) collective-permute-start(f32[2,8,128]{2,1,0:T(8,128)S(1)} %slice.748), channel_id=1, source_target_pairs={{960,984},{961,983},{962,982},{963,981},{964,980},{965,979},{966,9... | collective-permute-start | bytes 24584 | tf_op jit(solution)/shard_map/cond/branch_3_fun/ppermute | solution.py:76
  111.5 7.5 %collective-permute-start.114 = (f32[2,64,8]{1,2,0:T(8,128)S(1)}, f32[2,64,8]{1,2,0:T(8,128)S(1)}, u32[]{:S(2)}, u32[]{:S(2)}) collective-permute-start(f32[2,64,8]{1,2,0:T(8,128)S(1)} %copy.198), channel_id=1, source_target_pairs={{0,1},{1,2},{2,3},{3,4},{4,5},{5,6},{6,7},{7,8},{8,9},{9,10},{10,1... | collective-permute-start | bytes 12296 | tf_op jit(solution)/shard_map/cond/branch_3_fun/ppermute | solution.py:77
  116.3 4.4 %collective-permute-start.115 = (f32[2,64,8]{1,2,0:T(8,128)S(1)}, f32[2,64,8]{1,2,0:T(8,128)S(1)}, u32[]{:S(2)}, u32[]{:S(2)}) collective-permute-start(f32[2,64,8]{1,2,0:T(8,128)S(1)} %copy.199), channel_id=1, source_target_pairs={{0,63},{1,0},{2,1},{3,2},{4,3},{5,4},{6,5},{7,6},{8,7},{9,8},{10,9... | collective-permute-start | bytes 12296 | tf_op jit(solution)/shard_map/cond/branch_3_fun/ppermute | solution.py:78
  121.1 32.8 %collective-permute-start.186 = (f32[2,8,144]{2,1,0:T(8,128)S(1)}, f32[2,8,144]{2,1,0:T(8,128)}, u32[]{:S(2)}, u32[]{:S(2)}) collective-permute-start(f32[2,8,144]{2,1,0:T(8,128)S(1)} %get-tuple-element.418), channel_id=1, source_target_pairs={{0,64},{64,128},{128,192},{192,256},{256,320},{320,384},{384,448},... | collective-permute-start | bytes 27656 | tf_op jit(solution)/shard_map/cond/branch_11_fun/ppermute | solution.py:99
  122.4 31.5 %collective-permute-start.187 = (f32[2,8,144]{2,1,0:T(8,128)S(1)}, f32[2,8,144]{2,1,0:T(8,128)}, u32[]{:S(2)}, u32[]{:S(2)}) collective-permute-start(f32[2,8,144]{2,1,0:T(8,128)S(1)} %get-tuple-element.419), channel_id=1, source_target_pairs={{64,0},{128,64},{192,128},{256,192},{320,256},{384,320},{448,384},... | collective-permute-start | bytes 27656 | tf_op jit(solution)/shard_map/cond/branch_11_fun/ppermute | solution.py:100
  126.1 17.2 %collective-permute-start.183 = (f32[2,8,128]{2,1,0:T(8,128)}, f32[2,8,128]{2,1,0:T(8,128)}, u32[]{:S(2)}, u32[]{:S(2)}) collective-permute-start(f32[2,8,128]{2,1,0:T(8,128)} %get-tuple-element.417), channel_id=1, source_target_pairs={{960,964},{961,965},{962,966},{963,967},{964,968},{965,969},{966,9... | collective-permute-start | bytes 24584 | tf_op jit(solution)/shard_map/cond/branch_11_fun/ppermute | solution.py:97
  139.4 11.6 %collective-permute-start.184 = (f32[2,8,128]{2,1,0:T(8,128)}, f32[2,8,128]{2,1,0:T(8,128)}, u32[]{:S(2)}, u32[]{:S(2)}) collective-permute-start(f32[2,8,128]{2,1,0:T(8,128)} %get-tuple-element.417), channel_id=1, source_target_pairs={{960,965},{961,966},{962,967},{963,968},{964,969},{965,970},{966,9... | collective-permute-start | bytes 24584 | tf_op jit(solution)/shard_map/cond/branch_11_fun/ppermute | solution.py:97
  141.4 12.5 %collective-permute-start.185 = (f32[2,8,128]{2,1,0:T(8,128)}, f32[2,8,128]{2,1,0:T(8,128)}, u32[]{:S(2)}, u32[]{:S(2)}) collective-permute-start(f32[2,8,128]{2,1,0:T(8,128)} %get-tuple-element.417), channel_id=1, source_target_pairs={{960,966},{961,967},{962,968},{963,969},{964,970},{965,971},{966,9... | collective-permute-start | bytes 24584 | tf_op jit(solution)/shard_map/cond/branch_11_fun/ppermute | solution.py:97
  159.7 0.6 copy-start.1
  159.7 0.8 copy-start.8

commit v6 on v4

--- a/solution.py
+++ b/solution.py
@@ -62,7 +62,7 @@
     nx = lax.axis_size("gx")
     w = width
     cols = stack.shape[-1]
-    low = 8 if nx % 8 == 0 else 1
+    low = 4 if nx % 4 == 0 else 1
     a = fold_start // low
     b = fold_start % low
     top_row = (ny - 1) * nx

time: 121 us -> 124 us (1.025)
  the two profiles are of different devices: /device:TPU:63 before, /device:TPU:61 now
where the time goes in v6:
time: 124 us; the launch traced here: 123 us
  starting transfers between devices  63.4 us (51%)
  waiting for transfers between devices  36.7 us (30%)
  local copies, waits for them, and re-layouts  11.4 us (9%)
  other arithmetic  7.66 us (6%)
  between operations  3.04 us (2%)
    all_to_all x1, waiting for transfers between devices, regroup_local(): lax.all_to_all(packed, 'gx', split_axis=0, concat_axis=0, tiled=True)  34.1 us
    all_to_all x1, starting transfers between devices, regroup_local(): lax.all_to_all(packed, 'gx', split_axis=0, concat_axis=0, tiled=True)  29.1 us
    ppermute x3, starting transfers between devices, run(): lax.ppermute(y, both, on_top(lambda e, t=t: e + bb + t))  17.5 us
    ppermute x1, starting transfers between devices, run(): mirrored = lax.ppermute(top, both, on_top(lambda e: low * aa - e))  5.69 us
    unnamed x27, local copies, waits for them, and re-layouts  5.12 us
    ppermute x1, starting transfers between devices, run(): north = lax.ppermute(north_in, 'gy', shift_pairs(ny, -1, False))  4.58 us
    ppermute x1, starting transfers between devices, run(): east = lax.ppermute(east_in, 'gx', shift_pairs(nx, -1, True))  3.36 us
  transfers between devices with their start and end apart: 9, of which 3 were waited for; matrix products, arithmetic and copies ran while one was open for 2% of the time, Pallas kernels for 0%

profile of v6, /device:TPU:61, one launch (start us, length us, event | category | flops | bytes accessed | tf_op | source)
XLA Modules:
  0.0 123.2 jit_solution(17892324216848915569)
XLA Ops:
  0.6 0.5 broadcast.423
  1.3 0.7 reduce.3
  2.6 1.0 reshape.177
  3.5 0.4 fusion.147
  4.0 1.0 copy.164
  5.0 29.1 %all-to-all-start = ((f32[64,1,1026]{2,1,0:T(1,128)}), f32[64,1,1026]{2,1,0:T(1,128)S(1)}, u32[]{:S(2)}, u32[]{:S(2)}) async-start(f32[64,1,1026]{2,1,0:T(1,128)} %copy.164), calls=%async_computation | async-start | bytes 589824 | tf_op jit(solution)/shard_map/all_to_all | solution.py:48
  34.1 1.2 slice.555
  38.2 0.3 copy-done.3
  38.5 0.5 copy-done.4
  39.1 0.3 copy-done.2
  39.6 34.1 %all-to-all-done = f32[64,1,1026]{2,1,0:T(1,128)S(1)} async-done(((f32[64,1,1026]{2,1,0:T(1,128)}), f32[64,1,1026]{2,1,0:T(1,128)S(1)}, u32[]{:S(2)}, u32[]{:S(2)}) %all-to-all-start) | async-done | bytes 262688 | tf_op jit(solution)/shard_map/all_to_all | solution.py:48
  73.9 0.1 eq.47
  74.1 0.3 fusion.138
  74.4 0.8 copy-done.6
  75.2 0.7 copy-done.7
  76.0 13.0 %conditional.2 = (f32[10,8,128]{2,1,0:T(8,128)}, f32[10,64,8]{2,1,0:T(8,128)S(1)}, f32[10,64,8]{2,1,0:T(8,128)S(1)}) conditional(s32[]{:T(128)} %clamp.7, (f32[10,64,128]{2,1,0:T(8,128)S(1)}, f32[10,64,128]{2,1,0:T(8,128)S(1)}, f32[10,64,128]{2,1,0:T(8,128)S(1)}) %tuple.104, (f32[10,64,128]{2,1,0:T(8,128)S(1)}, ...), branch_computations={%region_3.4_spmd, %region_4.5_spmd, %region_5.6_spmd, %region_6.7_... | conditional | bytes 614544 | solution.py:83
  76.0 5.7 %collective-permute-start.27 = (f32[10,8,128]{2,1,0:T(8,128)S(1)}, f32[10,8,128]{2,1,0:T(8,128)}, u32[]{:S(2)}, u32[]{:S(2)}) collective-permute-start(f32[10,8,128]{2,1,0:T(8,128)S(1)} %slice.718), channel_id=1, source_target_pairs={{960,996},{961,995},{962,994},{963,993},{964,992},{965,991},{966,9... | collective-permute-start | bytes 122888 | tf_op jit(solution)/shard_map/cond/branch_9_fun/ppermute | solution.py:76
  81.7 0.1 slice.734
  81.9 1.9 %collective-permute-start.28 = (f32[10,64,8]{1,2,0:T(8,128)S(1)}, f32[10,64,8]{1,2,0:T(8,128)S(1)}, u32[]{:S(2)}, u32[]{:S(2)}) collective-permute-start(f32[10,64,8]{1,2,0:T(8,128)S(1)} %copy.184), channel_id=1, source_target_pairs={{0,1},{1,2},{2,3},{3,4},{4,5},{5,6},{6,7},{7,8},{8,9},{9,10},{10,1... | collective-permute-start | bytes 61448 | tf_op jit(solution)/shard_map/cond/branch_9_fun/ppermute | solution.py:77
  84.0 3.4 %collective-permute-start.29 = (f32[10,64,8]{1,2,0:T(8,128)S(1)}, f32[10,64,8]{1,2,0:T(8,128)S(1)}, u32[]{:S(2)}, u32[]{:S(2)}) collective-permute-start(f32[10,64,8]{1,2,0:T(8,128)S(1)} %copy.185), channel_id=1, source_target_pairs={{0,63},{1,0},{2,1},{3,2},{4,3},{5,4},{6,5},{7,6},{8,7},{9,8},{10,9... | collective-permute-start | bytes 61448 | tf_op jit(solution)/shard_map/cond/branch_9_fun/ppermute | solution.py:78
  87.5 1.2 collective-permute-done.29
  89.1 25.0 %conditional.3 = (f32[10,8,128]{2,1,0:T(8,128)}, f32[10,8,128]{2,1,0:T(8,128)}, f32[10,8,128]{2,1,0:T(8,128)}, f32[10,8,144]{2,1,0:T(8,128)}, f32[10,8,144]{2,1,0:T(8,128)}) conditional(s32[]{:T(128)} %clamp.6, (f32[10,8,128]{2,1,0:T(8,128)}, f32[10,8,144]{2,1,0:T(8,128)S(1)}, ...), branch_computations={%region_19.20_spmd, %region_20.21_spmd, %region_21.22_spmd, %regio... | conditional | bytes 860400 | solution.py:105
  89.3 1.3 %collective-permute-start.76 = (f32[10,8,144]{2,1,0:T(8,128)S(1)}, f32[10,8,144]{2,1,0:T(8,128)}, u32[]{:S(2)}, u32[]{:S(2)}) collective-permute-start(f32[10,8,144]{2,1,0:T(8,128)S(1)} %get-tuple-element.208), channel_id=1, source_target_pairs={{0,64},{64,128},{128,192},{192,256},{256,320},{320,384},{384,448},... | collective-permute-start | bytes 138248 | tf_op jit(solution)/shard_map/cond/branch_5_fun/ppermute | solution.py:99
  90.6 4.6 %collective-permute-start.77 = (f32[10,8,144]{2,1,0:T(8,128)S(1)}, f32[10,8,144]{2,1,0:T(8,128)}, u32[]{:S(2)}, u32[]{:S(2)}) collective-permute-start(f32[10,8,144]{2,1,0:T(8,128)S(1)} %get-tuple-element.209), channel_id=1, source_target_pairs={{64,0},{128,64},{192,128},{256,192},{320,256},{384,320},{448,384},... | collective-permute-start | bytes 138248 | tf_op jit(solution)/shard_map/cond/branch_5_fun/ppermute | solution.py:100
  95.1 3.6 %collective-permute-start.73 = (f32[10,8,128]{2,1,0:T(8,128)}, f32[10,8,128]{2,1,0:T(8,128)}, u32[]{:S(2)}, u32[]{:S(2)}) collective-permute-start(f32[10,8,128]{2,1,0:T(8,128)} %get-tuple-element.207), channel_id=1, source_target_pairs={{960,961},{961,962},{962,963},{963,964},{964,965},{965,966},{966,9... | collective-permute-start | bytes 122888 | tf_op jit(solution)/shard_map/cond/branch_5_fun/ppermute | solution.py:97
  98.8 3.6 %collective-permute-start.74 = (f32[10,8,128]{2,1,0:T(8,128)}, f32[10,8,128]{2,1,0:T(8,128)}, u32[]{:S(2)}, u32[]{:S(2)}) collective-permute-start(f32[10,8,128]{2,1,0:T(8,128)} %get-tuple-element.207), channel_id=1, source_target_pairs={{960,962},{961,963},{962,964},{963,965},{964,966},{965,967},{966,9... | collective-permute-start | bytes 122888 | tf_op jit(solution)/shard_map/cond/branch_5_fun/ppermute | solution.py:97
  102.4 10.3 %collective-permute-start.75 = (f32[10,8,128]{2,1,0:T(8,128)}, f32[10,8,128]{2,1,0:T(8,128)}, u32[]{:S(2)}, u32[]{:S(2)}) collective-permute-start(f32[10,8,128]{2,1,0:T(8,128)} %get-tuple-element.207), channel_id=1, source_target_pairs={{960,963},{961,964},{962,965},{963,966},{964,967},{965,968},{966,9... | collective-permute-start | bytes 122888 | tf_op jit(solution)/shard_map/cond/branch_5_fun/ppermute | solution.py:97
  112.7 1.4 %collective-permute-done.75 = f32[10,8,128]{2,1,0:T(8,128)} collective-permute-done((f32[10,8,128]{2,1,0:T(8,128)}, f32[10,8,128]{2,1,0:T(8,128)}, u32[]{:S(2)}, u32[]{:S(2)}) %collective-permute-start.75) | collective-permute-done | bytes 40992 | tf_op jit(solution)/shard_map/cond/branch_5_fun/ppermute | solution.py:97
  114.1 0.9 fusion.1
  115.0 0.2 reverse
  115.2 0.7 copy-done.9
  116.0 1.2 pad_maximum_fusion
  117.2 0.2 fusion.45
  117.5 0.2 fusion.38
  117.8 0.3 fusion.30
  118.2 0.2 fusion.14
  118.5 0.2 fusion.7
  118.8 0.3 fusion.105
  119.2 0.2 fusion.89
  119.4 0.2 fusion.82
  119.7 0.3 fusion.74
  120.2 0.2 fusion.58
  120.4 0.2 fusion.51
  120.7 0.7 slice.888
  121.4 0.2 fusion.133
  121.7 0.6 copy-done.1
  122.3 0.2 copy-done.8
  122.5 0.7 maximum_multiply_fusion
  (83 shorter events, 3.7 us)
Async XLA Ops:
  0.6 0.7 copy-start.10
  5.0 68.7 %all-to-all-start = ((f32[64,1,1026]{2,1,0:T(1,128)}), f32[64,1,1026]{2,1,0:T(1,128)S(1)}, u32[]{:S(2)}, u32[]{:S(2)}) async-start(f32[64,1,1026]{2,1,0:T(1,128)} %copy.164), calls=%async_computation | async-start | bytes 589824 | tf_op jit(solution)/shard_map/all_to_all | solution.py:48
  37.2 1.3 %copy-start.5 = (f32[2,64,128]{2,1,0:T(8,128)S(1)}, f32[2,64,128]{2,1,0:T(8,128)}, u32[]{:S(2)}) copy-start(f32[2,64,128]{2,1,0:T(8,128)} %param.38) | copy-start | bytes 196612
  37.7 0.8 copy-start.3
  38.2 0.9 copy-start.4
  38.5 0.9 copy-start.2
  38.5 1.0 copy-start
  74.3 0.8 copy-start.6
  75.2 0.8 copy-start.7
  76.0 12.9 %collective-permute-start.27 = (f32[10,8,128]{2,1,0:T(8,128)S(1)}, f32[10,8,128]{2,1,0:T(8,128)}, u32[]{:S(2)}, u32[]{:S(2)}) collective-permute-start(f32[10,8,128]{2,1,0:T(8,128)S(1)} %slice.718), channel_id=1, source_target_pairs={{960,996},{961,995},{962,994},{963,993},{964,992},{965,991},{966,9... | collective-permute-start | bytes 122888 | tf_op jit(solution)/shard_map/cond/branch_9_fun/ppermute | solution.py:76
  81.9 5.4 %collective-permute-start.28 = (f32[10,64,8]{1,2,0:T(8,128)S(1)}, f32[10,64,8]{1,2,0:T(8,128)S(1)}, u32[]{:S(2)}, u32[]{:S(2)}) collective-permute-start(f32[10,64,8]{1,2,0:T(8,128)S(1)} %copy.184), channel_id=1, source_target_pairs={{0,1},{1,2},{2,3},{3,4},{4,5},{5,6},{6,7},{7,8},{8,9},{9,10},{10,1... | collective-permute-start | bytes 61448 | tf_op jit(solution)/shard_map/cond/branch_9_fun/ppermute | solution.py:77
  84.0 4.7 %collective-permute-start.29 = (f32[10,64,8]{1,2,0:T(8,128)S(1)}, f32[10,64,8]{1,2,0:T(8,128)S(1)}, u32[]{:S(2)}, u32[]{:S(2)}) collective-permute-start(f32[10,64,8]{1,2,0:T(8,128)S(1)} %copy.185), channel_id=1, source_target_pairs={{0,63},{1,0},{2,1},{3,2},{4,3},{5,4},{6,5},{7,6},{8,7},{9,8},{10,9... | collective-permute-start | bytes 61448 | tf_op jit(solution)/shard_map/cond/branch_9_fun/ppermute | solution.py:78
  89.3 24.8 %collective-permute-start.76 = (f32[10,8,144]{2,1,0:T(8,128)S(1)}, f32[10,8,144]{2,1,0:T(8,128)}, u32[]{:S(2)}, u32[]{:S(2)}) collective-permute-start(f32[10,8,144]{2,1,0:T(8,128)S(1)} %get-tuple-element.208), channel_id=1, source_target_pairs={{0,64},{64,128},{128,192},{192,256},{256,320},{320,384},{384,448},... | collective-permute-start | bytes 138248 | tf_op jit(solution)/shard_map/cond/branch_5_fun/ppermute | solution.py:99
  90.6 23.5 %collective-permute-start.77 = (f32[10,8,144]{2,1,0:T(8,128)S(1)}, f32[10,8,144]{2,1,0:T(8,128)}, u32[]{:S(2)}, u32[]{:S(2)}) collective-permute-start(f32[10,8,144]{2,1,0:T(8,128)S(1)} %get-tuple-element.209), channel_id=1, source_target_pairs={{64,0},{128,64},{192,128},{256,192},{320,256},{384,320},{448,384},... | collective-permute-start | bytes 138248 | tf_op jit(solution)/shard_map/cond/branch_5_fun/ppermute | solution.py:100
  95.1 17.5 %collective-permute-start.73 = (f32[10,8,128]{2,1,0:T(8,128)}, f32[10,8,128]{2,1,0:T(8,128)}, u32[]{:S(2)}, u32[]{:S(2)}) collective-permute-start(f32[10,8,128]{2,1,0:T(8,128)} %get-tuple-element.207), channel_id=1, source_target_pairs={{960,961},{961,962},{962,963},{963,964},{964,965},{965,966},{966,9... | collective-permute-start | bytes 122888 | tf_op jit(solution)/shard_map/cond/branch_5_fun/ppermute | solution.py:97
  98.8 13.9 %collective-permute-start.74 = (f32[10,8,128]{2,1,0:T(8,128)}, f32[10,8,128]{2,1,0:T(8,128)}, u32[]{:S(2)}, u32[]{:S(2)}) collective-permute-start(f32[10,8,128]{2,1,0:T(8,128)} %get-tuple-element.207), channel_id=1, source_target_pairs={{960,962},{961,963},{962,964},{963,965},{964,966},{965,967},{966,9... | collective-permute-start | bytes 122888 | tf_op jit(solution)/shard_map/cond/branch_5_fun/ppermute | solution.py:97
  102.4 11.7 %collective-permute-start.75 = (f32[10,8,128]{2,1,0:T(8,128)}, f32[10,8,128]{2,1,0:T(8,128)}, u32[]{:S(2)}, u32[]{:S(2)}) collective-permute-start(f32[10,8,128]{2,1,0:T(8,128)} %get-tuple-element.207), channel_id=1, source_target_pairs={{960,963},{961,964},{962,965},{963,966},{964,967},{965,968},{966,9... | collective-permute-start | bytes 122888 | tf_op jit(solution)/shard_map/cond/branch_5_fun/ppermute | solution.py:97
  115.2 0.7 copy-start.9
  121.7 0.6 copy-start.1
  121.7 0.8 copy-start.8

commit v7 on v6

--- a/solution.py
+++ b/solution.py
@@ -88,14 +88,15 @@
         stack[:, :, :w],
     )
     wide = jnp.concatenate([west, stack, east], axis=2)
-    spans = ((-2, -1, 0), (-1, 0, 1))
-    span = jnp.where(fold_rest < w - 1, 0, 1)
+    spans = ((-2, -1, 0), (-1, 0), (-1, 0, 1))
+    span = jnp.where(fold_rest < w - 1, 0, jnp.where(fold_rest > cols - 1 - w, 2, 1))
 
     def stage_two(bb, ts):
         def run(y, south_in, north_in):
             parts = [
                 lax.ppermute(y, both, on_top(lambda e, t=t: e + bb + t)) for t in ts
             ]
+            parts += [jnp.zeros_like(y)] * (3 - len(ts))
             south = lax.ppermute(south_in, "gy", shift_pairs(ny, 1, False))
             north = lax.ppermute(north_in, "gy", shift_pairs(ny, -1, False))
             return tuple(parts), south, north

time: 124 us -> 122 us (0.984)
  the two profiles are of different devices: /device:TPU:61 before, /device:TPU:125 now
where the time goes in v7:
time: 122 us; the launch traced here: 123 us
  starting transfers between devices  50.4 us (41%)
  waiting for transfers between devices  49.2 us (40%)
  local copies, waits for them, and re-layouts  12.1 us (10%)
  other arithmetic  7.65 us (6%)
  between operations  3.03 us (2%)
    all_to_all x1, waiting for transfers between devices, regroup_local(): lax.all_to_all(packed, 'gx', split_axis=0, concat_axis=0, tiled=True)  36.1 us
    all_to_all x1, starting transfers between devices, regroup_local(): lax.all_to_all(packed, 'gx', split_axis=0, concat_axis=0, tiled=True)  28.2 us
    ppermute x2, starting transfers between devices, run(): lax.ppermute(y, both, on_top(lambda e, t=t: e + bb + t))  5.79 us
    ppermute x1, starting transfers between devices, run(): mirrored = lax.ppermute(top, both, on_top(lambda e: low * aa - e))  5.62 us
    ppermute x1, waiting for transfers between devices, run(): mirrored = lax.ppermute(top, both, on_top(lambda e: low * aa - e))  5.26 us
    unnamed x27, local copies, waits for them, and re-layouts  5.19 us
    ppermute x2, waiting for transfers between devices, run(): lax.ppermute(y, both, on_top(lambda e, t=t: e + bb + t))  4.02 us
    ppermute x1, starting transfers between devices, run(): west = lax.ppermute(west_in, 'gx', shift_pairs(nx, 1, True))  3.93 us
  transfers between devices with their start and end apart: 8, of which 4 were waited for; matrix products, arithmetic and copies ran while one was open for 2% of the time, Pallas kernels for 0%

profile of v7, /device:TPU:125, one launch (start us, length us, event | category | flops | bytes accessed | tf_op | source)
XLA Modules:
  0.0 123.4 jit_solution(511835412879557683)
XLA Ops:
  0.6 0.5 broadcast.435
  1.3 0.7 reduce.3
  2.6 1.0 reshape.177
  3.5 0.4 fusion.147
  4.0 1.0 copy.164
  5.0 28.2 %all-to-all-start = ((f32[64,1,1026]{2,1,0:T(1,128)}), f32[64,1,1026]{2,1,0:T(1,128)S(1)}, u32[]{:S(2)}, u32[]{:S(2)}) async-start(f32[64,1,1026]{2,1,0:T(1,128)} %copy.164), calls=%async_computation | async-start | bytes 589824 | tf_op jit(solution)/shard_map/all_to_all | solution.py:48
  33.1 1.2 slice.555
  37.3 0.4 copy-done.3
  37.7 0.5 copy-done.4
  38.2 0.4 copy-done.2
  38.7 36.1 %all-to-all-done = f32[64,1,1026]{2,1,0:T(1,128)S(1)} async-done(((f32[64,1,1026]{2,1,0:T(1,128)}), f32[64,1,1026]{2,1,0:T(1,128)S(1)}, u32[]{:S(2)}, u32[]{:S(2)}) %all-to-all-start) | async-done | bytes 262688 | tf_op jit(solution)/shard_map/all_to_all | solution.py:48
  75.0 0.1 eq.47
  75.2 0.3 fusion.138
  75.5 0.8 copy-done.6
  76.3 0.7 copy-done.7
  77.1 21.3 %conditional.2 = (f32[10,8,128]{2,1,0:T(8,128)}, f32[10,64,8]{2,1,0:T(8,128)S(1)}, f32[10,64,8]{2,1,0:T(8,128)S(1)}) conditional(s32[]{:T(128)} %clamp.7, (f32[10,64,128]{2,1,0:T(8,128)S(1)}, f32[10,64,128]{2,1,0:T(8,128)S(1)}, f32[10,64,128]{2,1,0:T(8,128)S(1)}) %tuple.120, (f32[10,64,128]{2,1,0:T(8,128)S(1)}, ...), branch_computations={%region_3.4_spmd, %region_4.5_spmd, %region_5.6_spmd, %region_6.7_... | conditional | bytes 614544 | solution.py:83
  77.1 5.6 %collective-permute-start.42 = (f32[10,8,128]{2,1,0:T(8,128)S(1)}, f32[10,8,128]{2,1,0:T(8,128)}, u32[]{:S(2)}, u32[]{:S(2)}) collective-permute-start(f32[10,8,128]{2,1,0:T(8,128)S(1)} %slice.723), channel_id=1, source_target_pairs={{960,1016},{961,1015},{962,1014},{963,1013},{964,1012},{965,1011},... | collective-permute-start | bytes 122888 | tf_op jit(solution)/shard_map/cond/branch_14_fun/ppermute | solution.py:76
  83.0 3.9 %collective-permute-start.43 = (f32[10,64,8]{1,2,0:T(8,128)S(1)}, f32[10,64,8]{1,2,0:T(8,128)S(1)}, u32[]{:S(2)}, u32[]{:S(2)}) collective-permute-start(f32[10,64,8]{1,2,0:T(8,128)S(1)} %copy.194), channel_id=1, source_target_pairs={{0,1},{1,2},{2,3},{3,4},{4,5},{5,6},{6,7},{7,8},{8,9},{9,10},{10,1... | collective-permute-start | bytes 61448 | tf_op jit(solution)/shard_map/cond/branch_14_fun/ppermute | solution.py:77
  87.1 1.9 %collective-permute-start.44 = (f32[10,64,8]{1,2,0:T(8,128)S(1)}, f32[10,64,8]{1,2,0:T(8,128)S(1)}, u32[]{:S(2)}, u32[]{:S(2)}) collective-permute-start(f32[10,64,8]{1,2,0:T(8,128)S(1)} %copy.195), channel_id=1, source_target_pairs={{0,63},{1,0},{2,1},{3,2},{4,3},{5,4},{6,5},{7,6},{8,7},{9,8},{10,9... | collective-permute-start | bytes 61448 | tf_op jit(solution)/shard_map/cond/branch_14_fun/ppermute | solution.py:78
  89.1 3.9 %collective-permute-done.44 = f32[10,64,8]{1,2,0:T(8,128)S(1)} collective-permute-done((f32[10,64,8]{1,2,0:T(8,128)S(1)}, f32[10,64,8]{1,2,0:T(8,128)S(1)}, u32[]{:S(2)}, u32[]{:S(2)}) %collective-permute-start.44) | collective-permute-done | bytes 20512 | tf_op jit(solution)/shard_map/cond/branch_14_fun/ppermute | solution.py:78
  93.2 5.3 %collective-permute-done.42 = f32[10,8,128]{2,1,0:T(8,128)} collective-permute-done((f32[10,8,128]{2,1,0:T(8,128)S(1)}, f32[10,8,128]{2,1,0:T(8,128)}, u32[]{:S(2)}, u32[]{:S(2)}) %collective-permute-start.42) | collective-permute-done | bytes 40992 | tf_op jit(solution)/shard_map/cond/branch_14_fun/ppermute | solution.py:76
  98.6 15.7 %conditional.3 = (f32[10,8,128]{2,1,0:T(8,128)}, f32[10,8,128]{2,1,0:T(8,128)}, f32[10,8,128]{2,1,0:T(8,128)}, f32[10,8,144]{2,1,0:T(8,128)}, f32[10,8,144]{2,1,0:T(8,128)}) conditional(s32[]{:T(128)} %clamp.6, (f32[10,8,128]{2,1,0:T(8,128)}, f32[10,8,144]{2,1,0:T(8,128)S(1)}, ...), branch_computations={%region_19.20_spmd, %region_20.21_spmd, %region_21.22_spmd, %regio... | conditional | bytes 860400 | solution.py:106
  98.8 1.3 %collective-permute-start.83 = (f32[10,8,144]{2,1,0:T(8,128)S(1)}, f32[10,8,144]{2,1,0:T(8,128)}, u32[]{:S(2)}, u32[]{:S(2)}) collective-permute-start(f32[10,8,144]{2,1,0:T(8,128)S(1)} %get-tuple-element.238), channel_id=1, source_target_pairs={{0,64},{64,128},{128,192},{192,256},{256,320},{320,384},{384,448},... | collective-permute-start | bytes 138248 | tf_op jit(solution)/shard_map/cond/branch_7_fun/ppermute | solution.py:100
  100.1 3.7 %collective-permute-start.84 = (f32[10,8,144]{2,1,0:T(8,128)S(1)}, f32[10,8,144]{2,1,0:T(8,128)}, u32[]{:S(2)}, u32[]{:S(2)}) collective-permute-start(f32[10,8,144]{2,1,0:T(8,128)S(1)} %get-tuple-element.239), channel_id=1, source_target_pairs={{64,0},{128,64},{192,128},{256,192},{320,256},{384,320},{448,384},... | collective-permute-start | bytes 138248 | tf_op jit(solution)/shard_map/cond/branch_7_fun/ppermute | solution.py:101
  103.8 3.9 %collective-permute-start.81 = (f32[10,8,128]{2,1,0:T(8,128)}, f32[10,8,128]{2,1,0:T(8,128)}, u32[]{:S(2)}, u32[]{:S(2)}) collective-permute-start(f32[10,8,128]{2,1,0:T(8,128)} %get-tuple-element.237), channel_id=1, source_target_pairs={{960,961},{961,962},{962,963},{963,964},{964,965},{965,966},{966,9... | collective-permute-start | bytes 122888 | tf_op jit(solution)/shard_map/cond/branch_7_fun/ppermute | solution.py:97
  107.6 1.9 %collective-permute-start.82 = (f32[10,8,128]{2,1,0:T(8,128)}, f32[10,8,128]{2,1,0:T(8,128)}, u32[]{:S(2)}, u32[]{:S(2)}) collective-permute-start(f32[10,8,128]{2,1,0:T(8,128)} %get-tuple-element.237), channel_id=1, source_target_pairs={{960,962},{961,963},{962,964},{963,965},{964,966},{965,967},{966,9... | collective-permute-start | bytes 122888 | tf_op jit(solution)/shard_map/cond/branch_7_fun/ppermute | solution.py:97
  109.6 4.0 %collective-permute-done.82 = f32[10,8,128]{2,1,0:T(8,128)} collective-permute-done((f32[10,8,128]{2,1,0:T(8,128)}, f32[10,8,128]{2,1,0:T(8,128)}, u32[]{:S(2)}, u32[]{:S(2)}) %collective-permute-start.82) | collective-permute-done | bytes 40992 | tf_op jit(solution)/shard_map/cond/branch_7_fun/ppermute | solution.py:97
  113.6 0.6 broadcast.247
  114.2 0.9 fusion.1
  115.2 0.2 reverse
  115.3 0.7 copy-done.9
  116.1 1.2 pad_maximum_fusion
  117.4 0.2 fusion.45
  117.6 0.2 fusion.38
  117.9 0.3 fusion.30
  118.4 0.2 fusion.14
  118.6 0.2 fusion.7
  118.9 0.3 fusion.105
  119.4 0.2 fusion.89
  119.6 0.2 fusion.82
  119.9 0.3 fusion.74
  120.3 0.2 fusion.58
  120.6 0.2 fusion.51
  120.9 0.7 slice.888
  121.6 0.2 fusion.133
  121.9 0.6 copy-done.1
  122.5 0.2 copy-done.8
  122.6 0.7 maximum_multiply_fusion
  (82 shorter events, 3.8 us)
Async XLA Ops:
  0.6 0.7 copy-start.10
  5.0 69.8 %all-to-all-start = ((f32[64,1,1026]{2,1,0:T(1,128)}), f32[64,1,1026]{2,1,0:T(1,128)S(1)}, u32[]{:S(2)}, u32[]{:S(2)}) async-start(f32[64,1,1026]{2,1,0:T(1,128)} %copy.164), calls=%async_computation | async-start | bytes 589824 | tf_op jit(solution)/shard_map/all_to_all | solution.py:48
  36.3 1.4 %copy-start.5 = (f32[2,64,128]{2,1,0:T(8,128)S(1)}, f32[2,64,128]{2,1,0:T(8,128)}, u32[]{:S(2)}) copy-start(f32[2,64,128]{2,1,0:T(8,128)} %param.42) | copy-start | bytes 196612
  36.9 0.8 copy-start.3
  37.3 0.9 copy-start.4
  37.7 0.9 copy-start.2
  37.7 1.0 copy-start
  75.5 0.8 copy-start.6
  76.3 0.8 copy-start.7
  77.1 21.3 %collective-permute-start.42 = (f32[10,8,128]{2,1,0:T(8,128)S(1)}, f32[10,8,128]{2,1,0:T(8,128)}, u32[]{:S(2)}, u32[]{:S(2)}) collective-permute-start(f32[10,8,128]{2,1,0:T(8,128)S(1)} %slice.723), channel_id=1, source_target_pairs={{960,1016},{961,1015},{962,1014},{963,1013},{964,1012},{965,1011},... | collective-permute-start | bytes 122888 | tf_op jit(solution)/shard_map/cond/branch_14_fun/ppermute | solution.py:76
  83.0 6.0 %collective-permute-start.43 = (f32[10,64,8]{1,2,0:T(8,128)S(1)}, f32[10,64,8]{1,2,0:T(8,128)S(1)}, u32[]{:S(2)}, u32[]{:S(2)}) collective-permute-start(f32[10,64,8]{1,2,0:T(8,128)S(1)} %copy.194), channel_id=1, source_target_pairs={{0,1},{1,2},{2,3},{3,4},{4,5},{5,6},{6,7},{7,8},{8,9},{9,10},{10,1... | collective-permute-start | bytes 61448 | tf_op jit(solution)/shard_map/cond/branch_14_fun/ppermute | solution.py:77
  87.1 6.0 %collective-permute-start.44 = (f32[10,64,8]{1,2,0:T(8,128)S(1)}, f32[10,64,8]{1,2,0:T(8,128)S(1)}, u32[]{:S(2)}, u32[]{:S(2)}) collective-permute-start(f32[10,64,8]{1,2,0:T(8,128)S(1)} %copy.195), channel_id=1, source_target_pairs={{0,63},{1,0},{2,1},{3,2},{4,3},{5,4},{6,5},{7,6},{8,7},{9,8},{10,9... | collective-permute-start | bytes 61448 | tf_op jit(solution)/shard_map/cond/branch_14_fun/ppermute | solution.py:78
  98.8 14.8 %collective-permute-start.83 = (f32[10,8,144]{2,1,0:T(8,128)S(1)}, f32[10,8,144]{2,1,0:T(8,128)}, u32[]{:S(2)}, u32[]{:S(2)}) collective-permute-start(f32[10,8,144]{2,1,0:T(8,128)S(1)} %get-tuple-element.238), channel_id=1, source_target_pairs={{0,64},{64,128},{128,192},{192,256},{256,320},{320,384},{384,448},... | collective-permute-start | bytes 138248 | tf_op jit(solution)/shard_map/cond/branch_7_fun/ppermute | solution.py:100
  100.1 13.5 %collective-permute-start.84 = (f32[10,8,144]{2,1,0:T(8,128)S(1)}, f32[10,8,144]{2,1,0:T(8,128)}, u32[]{:S(2)}, u32[]{:S(2)}) collective-permute-start(f32[10,8,144]{2,1,0:T(8,128)S(1)} %get-tuple-element.239), channel_id=1, source_target_pairs={{64,0},{128,64},{192,128},{256,192},{320,256},{384,320},{448,384},... | collective-permute-start | bytes 138248 | tf_op jit(solution)/shard_map/cond/branch_7_fun/ppermute | solution.py:101
  103.8 5.8 %collective-permute-start.81 = (f32[10,8,128]{2,1,0:T(8,128)}, f32[10,8,128]{2,1,0:T(8,128)}, u32[]{:S(2)}, u32[]{:S(2)}) collective-permute-start(f32[10,8,128]{2,1,0:T(8,128)} %get-tuple-element.237), channel_id=1, source_target_pairs={{960,961},{961,962},{962,963},{963,964},{964,965},{965,966},{966,9... | collective-permute-start | bytes 122888 | tf_op jit(solution)/shard_map/cond/branch_7_fun/ppermute | solution.py:97
  107.6 6.0 %collective-permute-start.82 = (f32[10,8,128]{2,1,0:T(8,128)}, f32[10,8,128]{2,1,0:T(8,128)}, u32[]{:S(2)}, u32[]{:S(2)}) collective-permute-start(f32[10,8,128]{2,1,0:T(8,128)} %get-tuple-element.237), channel_id=1, source_target_pairs={{960,962},{961,963},{962,964},{963,965},{964,966},{965,967},{966,9... | collective-permute-start | bytes 122888 | tf_op jit(solution)/shard_map/cond/branch_7_fun/ppermute | solution.py:97
  115.3 0.7 copy-start.9
  121.8 0.6 copy-start.1
  121.8 0.8 copy-start.8

commit v8 on v7

--- a/solution.py
+++ b/solution.py
@@ -27,7 +27,7 @@
     return pairs
 
 
-def regroup_local(ocean_blocks, block_map):
+def regroup_local(ocean_blocks, block_map, width):
     rows, fields, cols = ocean_blocks.shape
     peers = lax.axis_size("gx")
     group = max(2, rows // peers)
@@ -35,29 +35,50 @@
     target = block_map[:, 0]
     dest_dev = target[::group] // rows
     dest_row = (target % rows).reshape(count, group)
-    chosen = dest_dev[None, :] == jnp.arange(peers, dtype=jnp.int32)[:, None]
-    blocks = ocean_blocks.reshape(count, group * fields * cols)
-    outgoing = jnp.dot(
-        chosen.astype(jnp.float32),
-        blocks,
-        precision=lax.Precision.HIGHEST,
-        preferred_element_type=jnp.float32,
-    )
-    labels = jnp.sum(jnp.where(chosen[:, :, None], dest_row[None, :, :] + 1, 0), axis=1) - 1
-    packed = jnp.concatenate([outgoing, labels.astype(jnp.float32)], axis=1)
-    arrived = lax.all_to_all(packed, "gx", split_axis=0, concat_axis=0, tiled=True)
-    flat = arrived[:, : group * fields * cols].reshape(peers * group, fields * cols)
-    arrived_rows = arrived[:, group * fields * cols :].astype(jnp.int32)
-    picks = (
-        arrived_rows.reshape(-1)[None, :] == jnp.arange(rows, dtype=jnp.int32)[:, None]
-    ).astype(jnp.float32)
-    local = jnp.dot(
-        picks, flat, precision=lax.Precision.HIGHEST, preferred_element_type=jnp.float32
-    )
-    return local.reshape(rows, fields, cols)
-
-
-def exchange(stack, width, signs, fold_start, fold_rest):
+    devices = jnp.arange(peers, dtype=jnp.int32)
+    blocks = ocean_blocks.reshape(count, group, fields, cols)
+    currents = blocks[:, :, 2:4, :]
+
+    def pack(dest, payload):
+        chosen = dest[None, :] == devices[:, None]
+        out = jnp.dot(
+            chosen.astype(jnp.float32),
+            payload.reshape(count, -1),
+            precision=lax.Precision.HIGHEST,
+            preferred_element_type=jnp.float32,
+        )
+        labels = jnp.sum(jnp.where(chosen[:, :, None], dest_row[None, :, :] + 1, 0), axis=1) - 1
+        return out, labels.astype(jnp.float32)
+
+    main, main_rows = pack(dest_dev, blocks)
+    west, west_rows = pack((dest_dev + 1) % peers, currents[..., cols - width :])
+    east, east_rows = pack((dest_dev - 1) % peers, currents[..., :width])
+    pieces = [main, west, east, main_rows, west_rows, east_rows]
+    arrived = lax.all_to_all(
+        jnp.concatenate(pieces, axis=1), "gx", split_axis=0, concat_axis=0, tiled=True
+    )
+    bounds = [0]
+    for piece in pieces:
+        bounds.append(bounds[-1] + piece.shape[1])
+    part = [arrived[:, bounds[i] : bounds[i + 1]] for i in range(len(pieces))]
+
+    def unpack(data, labels):
+        flat = data.reshape(peers * group, -1)
+        picks = (
+            labels.astype(jnp.int32).reshape(-1)[None, :]
+            == jnp.arange(rows, dtype=jnp.int32)[:, None]
+        ).astype(jnp.float32)
+        return jnp.dot(
+            picks, flat, precision=lax.Precision.HIGHEST, preferred_element_type=jnp.float32
+        )
+
+    local = unpack(part[0], part[3]).reshape(rows, fields, cols)
+    west_rim = unpack(part[1], part[4]).reshape(rows, 2, width).transpose(1, 0, 2)
+    east_rim = unpack(part[2], part[5]).reshape(rows, 2, width).transpose(1, 0, 2)
+    return local, west_rim, east_rim
+
+
+def exchange(stack, west, east, width, signs, fold_start, fold_rest):
     ny = lax.axis_size("gy")
     nx = lax.axis_size("gx")
     w = width
@@ -72,21 +93,9 @@
         return [(top_row + e, top_row + target(e) % nx) for e in range(nx)]
 
     def stage_one(aa):
-        def run(top, west_in, east_in):
-            mirrored = lax.ppermute(top, both, on_top(lambda e: low * aa - e))
-            west = lax.ppermute(west_in, "gx", shift_pairs(nx, 1, True))
-            east = lax.ppermute(east_in, "gx", shift_pairs(nx, -1, True))
-            return mirrored, west, east
-
-        return run
-
-    mirrored, west, east = lax.switch(
-        a,
-        [stage_one(aa) for aa in range(nx // low)],
-        stack[:, -w:, :],
-        stack[:, :, -w:],
-        stack[:, :, :w],
-    )
+        return lambda top: lax.ppermute(top, both, on_top(lambda e: low * aa - e))
+
+    mirrored = lax.switch(a, [stage_one(aa) for aa in range(nx // low)], stack[:, -w:, :])
     wide = jnp.concatenate([west, stack, east], axis=2)
     spans = ((-2, -1, 0), (-1, 0), (-1, 0, 1))
     span = jnp.where(fold_rest < w - 1, 0, jnp.where(fold_rest > cols - 1 - w, 2, 1))
@@ -217,11 +226,6 @@
     ocean_land_mask,
     fold_partner_column,
 ):
-    ocean = regroup_local(ocean_blocks, block_map)
-    ocean_temp = ocean[:, 0, :]
-    ocean_salt = ocean[:, 1, :]
-    ocean_current_east = ocean[:, 2, :]
-    ocean_current_north = ocean[:, 3, :]
     hsum = jnp.sum(area * thickness, axis=0)
     conc = jnp.sum(area, axis=0)
     strength = PSTAR * hsum * jnp.exp(-CSTAR * (1.0 - conc))
@@ -236,21 +240,38 @@
     fold_rest = fold_col % cols
 
     width = 2 * ITERS
-    stack = jnp.concatenate(
-        [
-            velocity,
-            stress,
-            strength[None],
-            ice_mass_per_area[None],
-            wind + DRAG * jnp.stack([ocean_current_east, ocean_current_north]),
-            velocity_mask[None],
-        ],
+    nx = lax.axis_size("gx")
+    early = jnp.concatenate(
+        [velocity, stress, strength[None], ice_mass_per_area[None], wind, velocity_mask[None]],
         axis=0,
     )
+    west_early = lax.ppermute(early[:, :, -width:], "gx", shift_pairs(nx, 1, True))
+    east_early = lax.ppermute(early[:, :, :width], "gx", shift_pairs(nx, -1, True))
+    ocean, current_west, current_east = regroup_local(ocean_blocks, block_map, width)
+    ocean_temp = ocean[:, 0, :]
+    ocean_salt = ocean[:, 1, :]
+    ocean_current_east = ocean[:, 2, :]
+    ocean_current_north = ocean[:, 3, :]
+    currents = jnp.stack([ocean_current_east, ocean_current_north])
+
+    def with_forcing(fields, current):
+        return jnp.concatenate(
+            [fields[:7], fields[7:9] + DRAG * current, fields[9:10]], axis=0
+        )
+
+    stack = with_forcing(early, currents)
     signs = jnp.array(
         [-1.0, -1.0, 1.0, 1.0, 1.0, 1.0, 1.0, -1.0, -1.0, 1.0], jnp.float32
     ).reshape(-1, 1, 1)
-    ext = exchange(stack, width, signs, fold_start, fold_rest)
+    ext = exchange(
+        stack,
+        with_forcing(west_early, current_west),
+        with_forcing(east_early, current_east),
+        width,
+        signs,
+        fold_start,
+        fold_rest,
+    )
     grid_row = lax.axis_index("gy") * rows + jnp.arange(-width, rows + width, dtype=jnp.int32)
     true_row = jnp.where(grid_row > total_rows - 1, 2 * total_rows - 1 - grid_row, grid_row)
     coriolis_ext = (FCOR * (true_row.astype(jnp.float32) + 0.5) / float(total_rows))[:, None]

time: 122 us -> 129 us (1.057)
  the two profiles are of different devices: /device:TPU:125 before, /device:TPU:31 now
where the time goes in v8:
time: 129 us; the launch traced here: 128 us
  starting transfers between devices  52.9 us (41%)
  waiting for transfers between devices  48.6 us (38%)
  local copies, waits for them, and re-layouts  13.7 us (11%)
  other arithmetic  7.93 us (6%)
  between operations  3.33 us (3%)
  matrix products  1.48 us (1%)
    all_to_all x1, waiting for transfers between devices, regroup_local(): lax.all_to_all(jnp.concatenate(pieces, axis=1), 'gx', split_axis=0, conca...  30.9 us
    all_to_all x1, starting transfers between devices, regroup_local(): lax.all_to_all(jnp.concatenate(pieces, axis=1), 'gx', split_axis=0, conca...  30 us
    ppermute x2, waiting for transfers between devices, run(): lax.ppermute(y, both, on_top(lambda e, t=t: e + bb + t))  12.4 us
    ppermute x1, starting transfers between devices, stage_one(): return lambda top: lax.ppermute(top, both, on_top(lambda e: low * aa - e))  8.28 us
    unnamed x38, local copies, waits for them, and re-layouts  6.49 us
    ppermute x1, waiting for transfers between devices, stage_one(): return lambda top: lax.ppermute(top, both, on_top(lambda e: low * aa - e))  5.28 us
    ppermute x2, starting transfers between devices, run(): lax.ppermute(y, both, on_top(lambda e, t=t: e + bb + t))  4.34 us
    ppermute x1, starting transfers between devices, run(): north = lax.ppermute(north_in, 'gy', shift_pairs(ny, -1, False))  3.66 us
  transfers between devices with their start and end apart: 8, of which 3 were waited for; matrix products, arithmetic and copies ran while one was open for 3% of the time, Pallas kernels for 0%

profile of v8, /device:TPU:31, one launch (start us, length us, event | category | flops | bytes accessed | tf_op | source)
XLA Modules:
  0.0 128.0 jit_solution(3859443638347418619)
XLA Ops:
  0.6 1.0 copy.80
  1.7 0.5 broadcast.479
  2.4 0.7 reduce.3
  4.2 0.3 fusion.147
  4.5 0.3 fusion.149
  4.8 0.4 fusion.169
  5.3 1.0 copy.91
  6.4 30.0 %all-to-all-start = ((f32[64,1,1094]{2,1,0:T(1,128)}), f32[64,1,1094]{2,1,0:T(1,128)S(1)}, u32[]{:S(2)}, u32[]{:S(2)}) async-start(f32[64,1,1094]{2,1,0:T(1,128)} %copy.91), calls=%async_computation | async-start | bytes 589824 | tf_op jit(solution)/shard_map/all_to_all | solution.py:57
  36.4 1.2 slice.644
  40.7 0.7 copy-done.3
  41.6 0.7 copy-done.5
  42.4 0.8 copy-done.2
  43.6 30.9 %all-to-all-done = f32[64,1,1094]{2,1,0:T(1,128)S(1)} async-done(((f32[64,1,1094]{2,1,0:T(1,128)}), f32[64,1,1094]{2,1,0:T(1,128)S(1)}, u32[]{:S(2)}, u32[]{:S(2)}) %all-to-all-start) | async-done | bytes 280096 | tf_op jit(solution)/shard_map/all_to_all | solution.py:57
  75.1 0.3 fusion.138
  75.4 0.7 copy-done.9
  76.3 1.9 %collective-permute-start.73 = (f32[10,64,8]{1,2,0:T(8,128)S(1)}, f32[10,64,8]{1,2,0:T(8,128)S(1)}, u32[]{:S(2)}, u32[]{:S(2)}) collective-permute-start(f32[10,64,8]{1,2,0:T(8,128)S(1)} %get-tuple-element.195), channel_id=1, source_target_pairs={{0,63},{1,0},{2,1},{3,2},{4,3},{5,4},{6,5},{7,6},{8,7},{9,8},{10,9... | collective-permute-start | bytes 61448 | tf_op jit(solution)/shard_map/ppermute | solution.py:249
  78.5 0.2 eq.124
  78.8 3.4 %collective-permute-start.72 = (f32[10,64,8]{1,2,0:T(8,128)S(1)}, f32[10,64,8]{1,2,0:T(8,128)S(1)}, u32[]{:S(2)}, u32[]{:S(2)}) collective-permute-start(f32[10,64,8]{1,2,0:T(8,128)S(1)} %get-tuple-element.194), channel_id=1, source_target_pairs={{0,1},{1,2},{2,3},{3,4},{4,5},{5,6},{6,7},{7,8},{8,9},{9,10},{10,1... | collective-permute-start | bytes 61448 | tf_op jit(solution)/shard_map/ppermute | solution.py:248
  82.2 13.6 %conditional.2 = (f32[10,8,128]{2,1,0:T(8,128)}) conditional(s32[]{:T(128)} %clamp.7, f32[10,8,128]{2,1,0:T(8,128)S(1)} %slice.816, f32[10,8,128]{2,1,0:T(8,128)S(1)} %slice.816, f32[10,8,128]{2,1,0:T(8,128)S(1)} %slice.816, f32[10,8,128]{2,1,0:T(8,128)S(1)} %slice.816, f32[10,8,128]{2,1,0:T(8,128)S(1)} %slice.816, ...), branch_computations={%region_5.6_spmd, %region_6.7_spmd, %region_7.8_spmd, %region_8.9_... | conditional | bytes 163888 | solution.py:98
  82.2 8.3 %collective-permute-start.2 = (f32[10,8,128]{2,1,0:T(8,128)S(1)}, f32[10,8,128]{2,1,0:T(8,128)}, u32[]{:S(2)}, u32[]{:S(2)}) collective-permute-start(f32[10,8,128]{2,1,0:T(8,128)S(1)} %param.2), channel_id=1, source_target_pairs={{960,968},{961,967},{962,966},{963,965},{964,964},{965,963},{966,9... | collective-permute-start | bytes 122888 | tf_op jit(solution)/shard_map/cond/branch_2_fun/ppermute | solution.py:96
  90.5 5.3 %collective-permute-done.2 = f32[10,8,128]{2,1,0:T(8,128)} collective-permute-done((f32[10,8,128]{2,1,0:T(8,128)S(1)}, f32[10,8,128]{2,1,0:T(8,128)}, u32[]{:S(2)}, u32[]{:S(2)}) %collective-permute-start.2) | collective-permute-done | bytes 40992 | tf_op jit(solution)/shard_map/cond/branch_2_fun/ppermute | solution.py:96
  96.0 0.1 copy.102
  96.6 22.4 %conditional.3 = (f32[10,8,128]{2,1,0:T(8,128)}, f32[10,8,128]{2,1,0:T(8,128)}, f32[10,8,128]{2,1,0:T(8,128)}, f32[10,8,144]{2,1,0:T(8,128)}, f32[10,8,144]{2,1,0:T(8,128)}) conditional(s32[]{:T(128)} %clamp.6, (f32[10,8,128]{2,1,0:T(8,128)}, f32[10,8,144]{2,1,0:T(8,128)S(1)}, ...), branch_computations={%region_21.22_spmd, %region_22.23_spmd, %region_23.24_spmd, %regio... | conditional | bytes 860400 | solution.py:115
  96.7 1.3 %collective-permute-start.65 = (f32[10,8,144]{2,1,0:T(8,128)S(1)}, f32[10,8,144]{2,1,0:T(8,128)}, u32[]{:S(2)}, u32[]{:S(2)}) collective-permute-start(f32[10,8,144]{2,1,0:T(8,128)S(1)} %get-tuple-element.136), channel_id=1, source_target_pairs={{0,64},{64,128},{128,192},{192,256},{256,320},{320,384},{384,448},... | collective-permute-start | bytes 138248 | tf_op jit(solution)/shard_map/cond/branch_10_fun/ppermute | solution.py:109
  98.0 3.7 %collective-permute-start.66 = (f32[10,8,144]{2,1,0:T(8,128)S(1)}, f32[10,8,144]{2,1,0:T(8,128)}, u32[]{:S(2)}, u32[]{:S(2)}) collective-permute-start(f32[10,8,144]{2,1,0:T(8,128)S(1)} %get-tuple-element.137), channel_id=1, source_target_pairs={{64,0},{128,64},{192,128},{256,192},{320,256},{384,320},{448,384},... | collective-permute-start | bytes 138248 | tf_op jit(solution)/shard_map/cond/branch_10_fun/ppermute | solution.py:110
  101.6 2.4 %collective-permute-start.64 = (f32[10,8,128]{2,1,0:T(8,128)}, f32[10,8,128]{2,1,0:T(8,128)}, u32[]{:S(2)}, u32[]{:S(2)}) collective-permute-start(f32[10,8,128]{2,1,0:T(8,128)} %get-tuple-element.135), channel_id=1, source_target_pairs={{960,963},{961,964},{962,965},{963,966},{964,967},{965,968},{966,9... | collective-permute-start | bytes 122888 | tf_op jit(solution)/shard_map/cond/branch_10_fun/ppermute | solution.py:106
  104.0 1.9 %collective-permute-start.63 = (f32[10,8,128]{2,1,0:T(8,128)}, f32[10,8,128]{2,1,0:T(8,128)}, u32[]{:S(2)}, u32[]{:S(2)}) collective-permute-start(f32[10,8,128]{2,1,0:T(8,128)} %get-tuple-element.135), channel_id=1, source_target_pairs={{960,962},{961,963},{962,964},{963,965},{964,966},{965,967},{966,9... | collective-permute-start | bytes 122888 | tf_op jit(solution)/shard_map/cond/branch_10_fun/ppermute | solution.py:106
  106.0 12.4 %collective-permute-done.64 = f32[10,8,128]{2,1,0:T(8,128)} collective-permute-done((f32[10,8,128]{2,1,0:T(8,128)}, f32[10,8,128]{2,1,0:T(8,128)}, u32[]{:S(2)}, u32[]{:S(2)}) %collective-permute-start.64) | collective-permute-done | bytes 40992 | tf_op jit(solution)/shard_map/cond/branch_10_fun/ppermute | solution.py:106
  118.4 0.6 broadcast.284
  119.0 0.9 fusion.1
  119.9 0.2 reverse
  120.1 0.7 copy-done.10
  120.9 1.2 pad_maximum_fusion
  122.1 0.2 fusion.45
  122.4 0.2 fusion.38
  122.7 0.3 fusion.30
  123.2 0.2 fusion.14
  123.4 0.2 fusion.7
  123.7 0.3 fusion.105
  124.1 0.2 fusion.89
  124.4 0.2 fusion.82
  124.7 0.3 fusion.74
  125.1 0.2 fusion.58
  125.3 0.2 fusion.51
  125.6 0.7 slice.956
  126.4 0.2 fusion.133
  126.7 0.6 copy-done.4
  127.3 0.7 maximum_multiply_fusion
  (122 shorter events, 5.7 us)
Async XLA Ops:
  0.6 1.0 copy-start.1
  1.7 0.7 copy-start.11
  6.4 34.2 %copy-start.7 = (s32[64,128]{1,0:T(8,128)S(1)}, s32[64,128]{1,0:T(8,128)}, u32[]{:S(2)}) copy-start(s32[64,128]{1,0:T(8,128)} %param.49) | copy-start | bytes 98308
  6.4 34.2 %copy-start.6 = (f32[5,64,128]{2,1,0:T(8,128)S(1)}, f32[5,64,128]{2,1,0:T(8,128)}, u32[]{:S(2)}) copy-start(f32[5,64,128]{2,1,0:T(8,128)} %param.45) | copy-start | bytes 491524
  6.4 68.1 %all-to-all-start = ((f32[64,1,1094]{2,1,0:T(1,128)}), f32[64,1,1094]{2,1,0:T(1,128)S(1)}, u32[]{:S(2)}, u32[]{:S(2)}) async-start(f32[64,1,1094]{2,1,0:T(1,128)} %copy.91), calls=%async_computation | async-start | bytes 589824 | tf_op jit(solution)/shard_map/all_to_all | solution.py:57
  36.4 4.2 %copy-start = (f32[5,64,128]{2,1,0:T(8,128)S(1)}, f32[5,64,128]{2,1,0:T(8,128)}, u32[]{:S(2)}) copy-start(f32[5,64,128]{2,1,0:T(8,128)} %param.44) | copy-start | bytes 491524
  40.6 0.8 copy-start.3
  41.5 0.8 copy-start.5
  42.3 0.9 copy-start.2
  75.4 0.8 copy-start.9
  76.2 2.0 %copy-start.8 = (f32[64,128]{1,0:T(8,128)S(1)}, f32[64,128]{1,0:T(8,128)}, u32[]{:S(2)}) copy-start(f32[64,128]{1,0:T(8,128)} %param.47) | copy-start | bytes 98308
  76.3 19.5 %collective-permute-start.73 = (f32[10,64,8]{1,2,0:T(8,128)S(1)}, f32[10,64,8]{1,2,0:T(8,128)S(1)}, u32[]{:S(2)}, u32[]{:S(2)}) collective-permute-start(f32[10,64,8]{1,2,0:T(8,128)S(1)} %get-tuple-element.195), channel_id=1, source_target_pairs={{0,63},{1,0},{2,1},{3,2},{4,3},{5,4},{6,5},{7,6},{8,7},{9,8},{10,9... | collective-permute-start | bytes 61448 | tf_op jit(solution)/shard_map/ppermute | solution.py:249
  78.8 17.3 %collective-permute-start.72 = (f32[10,64,8]{1,2,0:T(8,128)S(1)}, f32[10,64,8]{1,2,0:T(8,128)S(1)}, u32[]{:S(2)}, u32[]{:S(2)}) collective-permute-start(f32[10,64,8]{1,2,0:T(8,128)S(1)} %get-tuple-element.194), channel_id=1, source_target_pairs={{0,1},{1,2},{2,3},{3,4},{4,5},{5,6},{6,7},{7,8},{8,9},{9,10},{10,1... | collective-permute-start | bytes 61448 | tf_op jit(solution)/shard_map/ppermute | solution.py:248
  82.2 13.6 %collective-permute-start.2 = (f32[10,8,128]{2,1,0:T(8,128)S(1)}, f32[10,8,128]{2,1,0:T(8,128)}, u32[]{:S(2)}, u32[]{:S(2)}) collective-permute-start(f32[10,8,128]{2,1,0:T(8,128)S(1)} %param.2), channel_id=1, source_target_pairs={{960,968},{961,967},{962,966},{963,965},{964,964},{965,963},{966,9... | collective-permute-start | bytes 122888 | tf_op jit(solution)/shard_map/cond/branch_2_fun/ppermute | solution.py:96
  96.7 21.7 %collective-permute-start.65 = (f32[10,8,144]{2,1,0:T(8,128)S(1)}, f32[10,8,144]{2,1,0:T(8,128)}, u32[]{:S(2)}, u32[]{:S(2)}) collective-permute-start(f32[10,8,144]{2,1,0:T(8,128)S(1)} %get-tuple-element.136), channel_id=1, source_target_pairs={{0,64},{64,128},{128,192},{192,256},{256,320},{320,384},{384,448},... | collective-permute-start | bytes 138248 | tf_op jit(solution)/shard_map/cond/branch_10_fun/ppermute | solution.py:109
  98.0 20.4 %collective-permute-start.66 = (f32[10,8,144]{2,1,0:T(8,128)S(1)}, f32[10,8,144]{2,1,0:T(8,128)}, u32[]{:S(2)}, u32[]{:S(2)}) collective-permute-start(f32[10,8,144]{2,1,0:T(8,128)S(1)} %get-tuple-element.137), channel_id=1, source_target_pairs={{64,0},{128,64},{192,128},{256,192},{320,256},{384,320},{448,384},... | collective-permute-start | bytes 138248 | tf_op jit(solution)/shard_map/cond/branch_10_fun/ppermute | solution.py:110
  101.6 16.8 %collective-permute-start.64 = (f32[10,8,128]{2,1,0:T(8,128)}, f32[10,8,128]{2,1,0:T(8,128)}, u32[]{:S(2)}, u32[]{:S(2)}) collective-permute-start(f32[10,8,128]{2,1,0:T(8,128)} %get-tuple-element.135), channel_id=1, source_target_pairs={{960,963},{961,964},{962,965},{963,966},{964,967},{965,968},{966,9... | collective-permute-start | bytes 122888 | tf_op jit(solution)/shard_map/cond/branch_10_fun/ppermute | solution.py:106
  104.0 14.3 %collective-permute-start.63 = (f32[10,8,128]{2,1,0:T(8,128)}, f32[10,8,128]{2,1,0:T(8,128)}, u32[]{:S(2)}, u32[]{:S(2)}) collective-permute-start(f32[10,8,128]{2,1,0:T(8,128)} %get-tuple-element.135), channel_id=1, source_target_pairs={{960,962},{961,963},{962,964},{963,965},{964,966},{965,967},{966,9... | collective-permute-start | bytes 122888 | tf_op jit(solution)/shard_map/cond/branch_10_fun/ppermute | solution.py:106
  120.1 0.7 copy-start.10
  126.6 0.6 copy-start.4

commit v9 on v7

--- a/solution.py
+++ b/solution.py
@@ -93,12 +93,12 @@
 
     def stage_two(bb, ts):
         def run(y, south_in, north_in):
+            south = lax.ppermute(south_in, "gy", shift_pairs(ny, 1, False))
+            north = lax.ppermute(north_in, "gy", shift_pairs(ny, -1, False))
             parts = [
                 lax.ppermute(y, both, on_top(lambda e, t=t: e + bb + t)) for t in ts
             ]
             parts += [jnp.zeros_like(y)] * (3 - len(ts))
-            south = lax.ppermute(south_in, "gy", shift_pairs(ny, 1, False))
-            north = lax.ppermute(north_in, "gy", shift_pairs(ny, -1, False))
             return tuple(parts), south, north
 
         return run

time: 122 us -> 121 us (level)
  the two profiles are of different devices: /device:TPU:125 before, /device:TPU:159 now
where the time goes in v9:
time: 121 us; the launch traced here: 120 us
  starting transfers between devices  51.1 us (42%)
  waiting for transfers between devices  45.3 us (37%)
  local copies, waits for them, and re-layouts  12.1 us (10%)
  other arithmetic  7.65 us (6%)
  between operations  3.03 us (3%)
    all_to_all x1, waiting for transfers between devices, regroup_local(): lax.all_to_all(packed, 'gx', split_axis=0, concat_axis=0, tiled=True)  32.6 us
    all_to_all x1, starting transfers between devices, regroup_local(): lax.all_to_all(packed, 'gx', split_axis=0, concat_axis=0, tiled=True)  28.1 us
    ppermute x1, starting transfers between devices, run(): mirrored = lax.ppermute(top, both, on_top(lambda e: low * aa - e))  7.64 us
    ppermute x1, waiting for transfers between devices, run(): mirrored = lax.ppermute(top, both, on_top(lambda e: low * aa - e))  7.39 us
    unnamed x27, local copies, waits for them, and re-layouts  5.19 us
    ppermute x1, starting transfers between devices, run(): east = lax.ppermute(east_in, 'gx', shift_pairs(nx, -1, True))  4.57 us
    ppermute x2, waiting for transfers between devices, run(): lax.ppermute(y, both, on_top(lambda e, t=t: e + bb + t))  4.34 us
    ppermute x2, starting transfers between devices, run(): lax.ppermute(y, both, on_top(lambda e, t=t: e + bb + t))  3.94 us
  transfers between devices with their start and end apart: 8, of which 4 were waited for; matrix products, arithmetic and copies ran while one was open for 2% of the time, Pallas kernels for 0%

profile of v9, /device:TPU:159, one launch (start us, length us, event | category | flops | bytes accessed | tf_op | source)
XLA Modules:
  0.0 120.0 jit_solution(511835412879557683)
XLA Ops:
  0.6 0.5 broadcast.435
  1.3 0.7 reduce.3
  2.6 1.0 reshape.177
  3.5 0.4 fusion.147
  4.0 1.0 copy.164
  5.0 28.1 %all-to-all-start = ((f32[64,1,1026]{2,1,0:T(1,128)}), f32[64,1,1026]{2,1,0:T(1,128)S(1)}, u32[]{:S(2)}, u32[]{:S(2)}) async-start(f32[64,1,1026]{2,1,0:T(1,128)} %copy.164), calls=%async_computation | async-start | bytes 589824 | tf_op jit(solution)/shard_map/all_to_all | solution.py:48
  33.1 1.2 slice.555
  37.2 0.4 copy-done.3
  37.6 0.5 copy-done.4
  38.1 0.4 copy-done.2
  38.7 32.6 %all-to-all-done = f32[64,1,1026]{2,1,0:T(1,128)S(1)} async-done(((f32[64,1,1026]{2,1,0:T(1,128)}), f32[64,1,1026]{2,1,0:T(1,128)S(1)}, u32[]{:S(2)}, u32[]{:S(2)}) %all-to-all-start) | async-done | bytes 262688 | tf_op jit(solution)/shard_map/all_to_all | solution.py:48
  71.7 0.3 fusion.138
  72.0 0.8 copy-done.6
  72.9 0.7 copy-done.7
  73.6 23.2 %conditional.2 = (f32[10,8,128]{2,1,0:T(8,128)}, f32[10,64,8]{2,1,0:T(8,128)S(1)}, f32[10,64,8]{2,1,0:T(8,128)S(1)}) conditional(s32[]{:T(128)} %clamp.7, (f32[10,64,128]{2,1,0:T(8,128)S(1)}, f32[10,64,128]{2,1,0:T(8,128)S(1)}, f32[10,64,128]{2,1,0:T(8,128)S(1)}) %tuple.120, (f32[10,64,128]{2,1,0:T(8,128)S(1)}, ...), branch_computations={%region_3.4_spmd, %region_4.5_spmd, %region_5.6_spmd, %region_6.7_... | conditional | bytes 614544 | solution.py:83
  73.6 7.6 %collective-permute-start.18 = (f32[10,8,128]{2,1,0:T(8,128)S(1)}, f32[10,8,128]{2,1,0:T(8,128)}, u32[]{:S(2)}, u32[]{:S(2)}) collective-permute-start(f32[10,8,128]{2,1,0:T(8,128)S(1)} %slice.715), channel_id=1, source_target_pairs={{960,984},{961,983},{962,982},{963,981},{964,980},{965,979},{966,9... | collective-permute-start | bytes 122888 | tf_op jit(solution)/shard_map/cond/branch_6_fun/ppermute | solution.py:76
  81.3 0.1 slice.731
  81.5 1.9 %collective-permute-start.19 = (f32[10,64,8]{1,2,0:T(8,128)S(1)}, f32[10,64,8]{1,2,0:T(8,128)S(1)}, u32[]{:S(2)}, u32[]{:S(2)}) collective-permute-start(f32[10,64,8]{1,2,0:T(8,128)S(1)} %copy.178), channel_id=1, source_target_pairs={{0,1},{1,2},{2,3},{3,4},{4,5},{5,6},{6,7},{7,8},{8,9},{9,10},{10,1... | collective-permute-start | bytes 61448 | tf_op jit(solution)/shard_map/cond/branch_6_fun/ppermute | solution.py:77
  83.6 4.6 %collective-permute-start.20 = (f32[10,64,8]{1,2,0:T(8,128)S(1)}, f32[10,64,8]{1,2,0:T(8,128)S(1)}, u32[]{:S(2)}, u32[]{:S(2)}) collective-permute-start(f32[10,64,8]{1,2,0:T(8,128)S(1)} %copy.179), channel_id=1, source_target_pairs={{0,63},{1,0},{2,1},{3,2},{4,3},{5,4},{6,5},{7,6},{8,7},{9,8},{10,9... | collective-permute-start | bytes 61448 | tf_op jit(solution)/shard_map/cond/branch_6_fun/ppermute | solution.py:78
  88.3 0.9 collective-permute-done.20
  89.4 7.4 %collective-permute-done.18 = f32[10,8,128]{2,1,0:T(8,128)} collective-permute-done((f32[10,8,128]{2,1,0:T(8,128)S(1)}, f32[10,8,128]{2,1,0:T(8,128)}, u32[]{:S(2)}, u32[]{:S(2)}) %collective-permute-start.18) | collective-permute-done | bytes 40992 | tf_op jit(solution)/shard_map/cond/branch_6_fun/ppermute | solution.py:76
  96.9 13.9 %conditional.3 = (f32[10,8,128]{2,1,0:T(8,128)}, f32[10,8,128]{2,1,0:T(8,128)}, f32[10,8,128]{2,1,0:T(8,128)}, f32[10,8,144]{2,1,0:T(8,128)}, f32[10,8,144]{2,1,0:T(8,128)}) conditional(s32[]{:T(128)} %clamp.6, (f32[10,8,128]{2,1,0:T(8,128)}, f32[10,8,144]{2,1,0:T(8,128)S(1)}, ...), branch_computations={%region_19.20_spmd, %region_20.21_spmd, %region_21.22_spmd, %regio... | conditional | bytes 860400 | solution.py:106
  97.0 1.3 %collective-permute-start.69 = (f32[10,8,144]{2,1,0:T(8,128)S(1)}, f32[10,8,144]{2,1,0:T(8,128)}, u32[]{:S(2)}, u32[]{:S(2)}) collective-permute-start(f32[10,8,144]{2,1,0:T(8,128)S(1)} %get-tuple-element.229), channel_id=1, source_target_pairs={{0,64},{64,128},{128,192},{192,256},{256,320},{320,384},{384,448},... | collective-permute-start | bytes 138248 | tf_op jit(solution)/shard_map/cond/branch_4_fun/ppermute | solution.py:96
  98.3 3.7 %collective-permute-start.70 = (f32[10,8,144]{2,1,0:T(8,128)S(1)}, f32[10,8,144]{2,1,0:T(8,128)}, u32[]{:S(2)}, u32[]{:S(2)}) collective-permute-start(f32[10,8,144]{2,1,0:T(8,128)S(1)} %get-tuple-element.230), channel_id=1, source_target_pairs={{64,0},{128,64},{192,128},{256,192},{320,256},{384,320},{448,384},... | collective-permute-start | bytes 138248 | tf_op jit(solution)/shard_map/cond/branch_4_fun/ppermute | solution.py:97
  101.9 2.0 %collective-permute-start.67 = (f32[10,8,128]{2,1,0:T(8,128)}, f32[10,8,128]{2,1,0:T(8,128)}, u32[]{:S(2)}, u32[]{:S(2)}) collective-permute-start(f32[10,8,128]{2,1,0:T(8,128)} %get-tuple-element.228), channel_id=1, source_target_pairs={{960,960},{961,961},{962,962},{963,963},{964,964},{965,965},{966,9... | collective-permute-start | bytes 122888 | tf_op jit(solution)/shard_map/cond/branch_4_fun/ppermute | solution.py:99
  104.0 1.9 %collective-permute-start.68 = (f32[10,8,128]{2,1,0:T(8,128)}, f32[10,8,128]{2,1,0:T(8,128)}, u32[]{:S(2)}, u32[]{:S(2)}) collective-permute-start(f32[10,8,128]{2,1,0:T(8,128)} %get-tuple-element.228), channel_id=1, source_target_pairs={{960,961},{961,962},{962,963},{963,964},{964,965},{965,966},{966,9... | collective-permute-start | bytes 122888 | tf_op jit(solution)/shard_map/cond/branch_4_fun/ppermute | solution.py:99
  105.9 4.3 %collective-permute-done.68 = f32[10,8,128]{2,1,0:T(8,128)} collective-permute-done((f32[10,8,128]{2,1,0:T(8,128)}, f32[10,8,128]{2,1,0:T(8,128)}, u32[]{:S(2)}, u32[]{:S(2)}) %collective-permute-start.68) | collective-permute-done | bytes 40992 | tf_op jit(solution)/shard_map/cond/branch_4_fun/ppermute | solution.py:99
  110.2 0.6 broadcast.246
  110.9 0.9 fusion.1
  111.8 0.2 reverse
  112.0 0.7 copy-done.9
  112.8 1.2 %pad_maximum_fusion = f32[10,80,144]{2,1,0:T(8,128)S(1)} fusion(f32[10,8,144]{2,1,0:T(8,128)S(1)} %multiply_select_fusion, f32[10,64,8]{2,1,0:T(8,128)S(1)} %get-tuple-element.512, f32[10,64,128]{2,1,0:T(8,128)S(1)} %bitcast_dynamic-update-slice_fusion, f32[10,64,8]{2,1,0:T(8,128)S(1)} %get-tuple-element.511, f32[10,8,144]{2,1,0:T(8,128)} %get-tuple-element.266), kind=kLoop, calls=%fused_computation | loop fusion | flops 460800 | bytes 921600 | tf_op jit(solution)/shard_map/concatenate | solution.py:119
  114.0 0.2 fusion.45
  114.3 0.2 fusion.38
  114.6 0.3 fusion.30
  115.0 0.2 fusion.14
  115.3 0.2 fusion.7
  115.6 0.3 fusion.105
  116.0 0.2 fusion.89
  116.2 0.2 fusion.82
  116.5 0.3 fusion.74
  117.0 0.2 fusion.58
  117.2 0.2 fusion.51
  117.5 0.7 slice.888
  118.2 0.2 fusion.133
  118.5 0.6 copy-done.1
  119.1 0.2 copy-done.8
  119.3 0.7 maximum_multiply_fusion
  (82 shorter events, 3.8 us)
Async XLA Ops:
  0.6 0.7 copy-start.10
  5.0 66.3 %all-to-all-start = ((f32[64,1,1026]{2,1,0:T(1,128)}), f32[64,1,1026]{2,1,0:T(1,128)S(1)}, u32[]{:S(2)}, u32[]{:S(2)}) async-start(f32[64,1,1026]{2,1,0:T(1,128)} %copy.164), calls=%async_computation | async-start | bytes 589824 | tf_op jit(solution)/shard_map/all_to_all | solution.py:48
  36.2 1.4 %copy-start.5 = (f32[2,64,128]{2,1,0:T(8,128)S(1)}, f32[2,64,128]{2,1,0:T(8,128)}, u32[]{:S(2)}) copy-start(f32[2,64,128]{2,1,0:T(8,128)} %param.42) | copy-start | bytes 196612
  36.8 0.8 copy-start.3
  37.2 0.9 copy-start.4
  37.6 0.9 copy-start.2
  37.6 1.0 copy-start
  72.0 0.8 copy-start.6
  72.8 0.8 copy-start.7
  73.6 23.2 %collective-permute-start.18 = (f32[10,8,128]{2,1,0:T(8,128)S(1)}, f32[10,8,128]{2,1,0:T(8,128)}, u32[]{:S(2)}, u32[]{:S(2)}) collective-permute-start(f32[10,8,128]{2,1,0:T(8,128)S(1)} %slice.715), channel_id=1, source_target_pairs={{960,984},{961,983},{962,982},{963,981},{964,980},{965,979},{966,9... | collective-permute-start | bytes 122888 | tf_op jit(solution)/shard_map/cond/branch_6_fun/ppermute | solution.py:76
  81.5 6.6 %collective-permute-start.19 = (f32[10,64,8]{1,2,0:T(8,128)S(1)}, f32[10,64,8]{1,2,0:T(8,128)S(1)}, u32[]{:S(2)}, u32[]{:S(2)}) collective-permute-start(f32[10,64,8]{1,2,0:T(8,128)S(1)} %copy.178), channel_id=1, source_target_pairs={{0,1},{1,2},{2,3},{3,4},{4,5},{5,6},{6,7},{7,8},{8,9},{9,10},{10,1... | collective-permute-start | bytes 61448 | tf_op jit(solution)/shard_map/cond/branch_6_fun/ppermute | solution.py:77
  83.6 5.7 %collective-permute-start.20 = (f32[10,64,8]{1,2,0:T(8,128)S(1)}, f32[10,64,8]{1,2,0:T(8,128)S(1)}, u32[]{:S(2)}, u32[]{:S(2)}) collective-permute-start(f32[10,64,8]{1,2,0:T(8,128)S(1)} %copy.179), channel_id=1, source_target_pairs={{0,63},{1,0},{2,1},{3,2},{4,3},{5,4},{6,5},{7,6},{8,7},{9,8},{10,9... | collective-permute-start | bytes 61448 | tf_op jit(solution)/shard_map/cond/branch_6_fun/ppermute | solution.py:78
  97.0 13.3 %collective-permute-start.69 = (f32[10,8,144]{2,1,0:T(8,128)S(1)}, f32[10,8,144]{2,1,0:T(8,128)}, u32[]{:S(2)}, u32[]{:S(2)}) collective-permute-start(f32[10,8,144]{2,1,0:T(8,128)S(1)} %get-tuple-element.229), channel_id=1, source_target_pairs={{0,64},{64,128},{128,192},{192,256},{256,320},{320,384},{384,448},... | collective-permute-start | bytes 138248 | tf_op jit(solution)/shard_map/cond/branch_4_fun/ppermute | solution.py:96
  98.3 12.0 %collective-permute-start.70 = (f32[10,8,144]{2,1,0:T(8,128)S(1)}, f32[10,8,144]{2,1,0:T(8,128)}, u32[]{:S(2)}, u32[]{:S(2)}) collective-permute-start(f32[10,8,144]{2,1,0:T(8,128)S(1)} %get-tuple-element.230), channel_id=1, source_target_pairs={{64,0},{128,64},{192,128},{256,192},{320,256},{384,320},{448,384},... | collective-permute-start | bytes 138248 | tf_op jit(solution)/shard_map/cond/branch_4_fun/ppermute | solution.py:97
  101.9 4.0 %collective-permute-start.67 = (f32[10,8,128]{2,1,0:T(8,128)}, f32[10,8,128]{2,1,0:T(8,128)}, u32[]{:S(2)}, u32[]{:S(2)}) collective-permute-start(f32[10,8,128]{2,1,0:T(8,128)} %get-tuple-element.228), channel_id=1, source_target_pairs={{960,960},{961,961},{962,962},{963,963},{964,964},{965,965},{966,9... | collective-permute-start | bytes 122888 | tf_op jit(solution)/shard_map/cond/branch_4_fun/ppermute | solution.py:99
  104.0 6.3 %collective-permute-start.68 = (f32[10,8,128]{2,1,0:T(8,128)}, f32[10,8,128]{2,1,0:T(8,128)}, u32[]{:S(2)}, u32[]{:S(2)}) collective-permute-start(f32[10,8,128]{2,1,0:T(8,128)} %get-tuple-element.228), channel_id=1, source_target_pairs={{960,961},{961,962},{962,963},{963,964},{964,965},{965,966},{966,9... | collective-permute-start | bytes 122888 | tf_op jit(solution)/shard_map/cond/branch_4_fun/ppermute | solution.py:99
  112.0 0.7 copy-start.9
  118.5 0.6 copy-start.1
  118.5 0.8 copy-start.8

commit v10 on v7

--- a/solution.py
+++ b/solution.py
@@ -36,24 +36,23 @@
     dest_dev = target[::group] // rows
     dest_row = (target % rows).reshape(count, group)
     chosen = dest_dev[None, :] == jnp.arange(peers, dtype=jnp.int32)[:, None]
-    blocks = ocean_blocks.reshape(count, group * fields * cols)
-    outgoing = jnp.dot(
-        chosen.astype(jnp.float32),
-        blocks,
-        precision=lax.Precision.HIGHEST,
-        preferred_element_type=jnp.float32,
-    )
+    source = jnp.sum(jnp.where(chosen, jnp.arange(count, dtype=jnp.int32)[None, :] + 1, 0), axis=1) - 1
+    source = jnp.where(source < 0, count, source)
+    blocks = jnp.concatenate(
+        [ocean_blocks.reshape(count, group * fields * cols), jnp.zeros((1, group * fields * cols), jnp.float32)],
+        axis=0,
+    )
+    outgoing = jnp.take(blocks, source, axis=0)
     labels = jnp.sum(jnp.where(chosen[:, :, None], dest_row[None, :, :] + 1, 0), axis=1) - 1
     packed = jnp.concatenate([outgoing, labels.astype(jnp.float32)], axis=1)
     arrived = lax.all_to_all(packed, "gx", split_axis=0, concat_axis=0, tiled=True)
     flat = arrived[:, : group * fields * cols].reshape(peers * group, fields * cols)
-    arrived_rows = arrived[:, group * fields * cols :].astype(jnp.int32)
-    picks = (
-        arrived_rows.reshape(-1)[None, :] == jnp.arange(rows, dtype=jnp.int32)[:, None]
-    ).astype(jnp.float32)
-    local = jnp.dot(
-        picks, flat, precision=lax.Precision.HIGHEST, preferred_element_type=jnp.float32
-    )
+    arrived_rows = arrived[:, group * fields * cols :].astype(jnp.int32).reshape(-1)
+    hits = arrived_rows[None, :] == jnp.arange(rows, dtype=jnp.int32)[:, None]
+    where_from = jnp.sum(
+        jnp.where(hits, jnp.arange(peers * group, dtype=jnp.int32)[None, :], 0), axis=1
+    )
+    local = jnp.take(flat, where_from, axis=0)
     return local.reshape(rows, fields, cols)
 
 

time: 122 us -> 123 us (level)
  the two profiles are of different devices: /device:TPU:125 before, /device:TPU:95 now
where the time goes in v10:
time: 123 us; the launch traced here: 122 us
  starting transfers between devices  59.9 us (49%)
  waiting for transfers between devices  37 us (30%)
  local copies, waits for them, and re-layouts  13.8 us (11%)
  other arithmetic  8.07 us (7%)
  between operations  3.09 us (3%)
    all_to_all x1, waiting for transfers between devices, regroup_local(): lax.all_to_all(packed, 'gx', split_axis=0, concat_axis=0, tiled=True)  34.2 us
    all_to_all x1, starting transfers between devices, regroup_local(): lax.all_to_all(packed, 'gx', split_axis=0, concat_axis=0, tiled=True)  29.1 us
    ppermute x2, starting transfers between devices, run(): lax.ppermute(y, both, on_top(lambda e, t=t: e + bb + t))  14.7 us
    ppermute x1, starting transfers between devices, run(): north = lax.ppermute(north_in, 'gy', shift_pairs(ny, -1, False))  6.04 us
    unnamed x27, local copies, waits for them, and re-layouts  5.7 us
    ppermute x1, starting transfers between devices, run(): west = lax.ppermute(west_in, 'gx', shift_pairs(nx, 1, True))  4.31 us
    ppermute x1, starting transfers between devices, run(): east = lax.ppermute(east_in, 'gx', shift_pairs(nx, -1, True))  3.09 us
  transfers between devices with their start and end apart: 8, of which 3 were waited for; matrix products, arithmetic and copies ran while one was open for 2% of the time, Pallas kernels for 0%

profile of v10, /device:TPU:95, one launch (start us, length us, event | category | flops | bytes accessed | tf_op | source)
XLA Modules:
  0.0 122.3 jit_solution(888532933598462188)
XLA Ops:
  0.6 0.6 copy-done.10
  1.6 0.5 broadcast.539
  2.1 0.7 reduce.3
  3.2 1.0 reshape.233
  4.2 0.7 gather_fusion
  5.0 1.0 copy.164
  6.1 29.1 %all-to-all-start = ((f32[64,1,1026]{2,1,0:T(1,128)}), f32[64,1,1026]{2,1,0:T(1,128)S(1)}, u32[]{:S(2)}, u32[]{:S(2)}) async-start(f32[64,1,1026]{2,1,0:T(1,128)} %copy.164), calls=%async_computation | async-start | bytes 589824 | tf_op jit(solution)/shard_map/all_to_all | solution.py:48
  35.2 1.2 slice.555
  39.3 0.4 copy-done.3
  39.7 0.2 copy-done.4
  39.9 0.7 copy-done.2
  40.8 34.2 %all-to-all-done = f32[64,1,1026]{2,1,0:T(1,128)S(1)} async-done(((f32[64,1,1026]{2,1,0:T(1,128)}), f32[64,1,1026]{2,1,0:T(1,128)S(1)}, u32[]{:S(2)}, u32[]{:S(2)}) %all-to-all-start) | async-done | bytes 262688 | tf_op jit(solution)/shard_map/all_to_all | solution.py:48
  75.3 0.7 gather_fusion.1
  76.1 0.8 copy-done.6
  76.9 0.7 copy-done.7
  77.7 10.9 %conditional.2 = (f32[10,8,128]{2,1,0:T(8,128)}, f32[10,64,8]{2,1,0:T(8,128)S(1)}, f32[10,64,8]{2,1,0:T(8,128)S(1)}) conditional(s32[]{:T(128)} %clamp.7, (f32[10,64,128]{2,1,0:T(8,128)S(1)}, f32[10,64,128]{2,1,0:T(8,128)S(1)}, f32[10,64,128]{2,1,0:T(8,128)S(1)}) %tuple.120, (f32[10,64,128]{2,1,0:T(8,128)S(1)}, ...), branch_computations={%region_5.6_spmd, %region_6.7_spmd, %region_7.8_spmd, %region_8.9_... | conditional | bytes 614544 | solution.py:82
  77.7 1.3 %collective-permute-start.3 = (f32[10,8,128]{2,1,0:T(8,128)S(1)}, f32[10,8,128]{2,1,0:T(8,128)}, u32[]{:S(2)}, u32[]{:S(2)}) collective-permute-start(f32[10,8,128]{2,1,0:T(8,128)S(1)} %slice.710), channel_id=1, source_target_pairs={{960,964},{961,963},{962,962},{963,961},{964,960},{965,1023},{966,... | collective-permute-start | bytes 122888 | tf_op jit(solution)/shard_map/cond/branch_1_fun/ppermute | solution.py:75
  79.3 4.3 %collective-permute-start.4 = (f32[10,64,8]{1,2,0:T(8,128)S(1)}, f32[10,64,8]{1,2,0:T(8,128)S(1)}, u32[]{:S(2)}, u32[]{:S(2)}) collective-permute-start(f32[10,64,8]{1,2,0:T(8,128)S(1)} %copy.168), channel_id=1, source_target_pairs={{0,1},{1,2},{2,3},{3,4},{4,5},{5,6},{6,7},{7,8},{8,9},{9,10},{10,1... | collective-permute-start | bytes 61448 | tf_op jit(solution)/shard_map/cond/branch_1_fun/ppermute | solution.py:76
  83.7 3.1 %collective-permute-start.5 = (f32[10,64,8]{1,2,0:T(8,128)S(1)}, f32[10,64,8]{1,2,0:T(8,128)S(1)}, u32[]{:S(2)}, u32[]{:S(2)}) collective-permute-start(f32[10,64,8]{1,2,0:T(8,128)S(1)} %copy.169), channel_id=1, source_target_pairs={{0,63},{1,0},{2,1},{3,2},{4,3},{5,4},{6,5},{7,6},{8,7},{9,8},{10,9... | collective-permute-start | bytes 61448 | tf_op jit(solution)/shard_map/cond/branch_1_fun/ppermute | solution.py:77
  86.8 0.1 copy.201
  87.0 1.5 %collective-permute-done.5 = f32[10,64,8]{1,2,0:T(8,128)S(1)} collective-permute-done((f32[10,64,8]{1,2,0:T(8,128)S(1)}, f32[10,64,8]{1,2,0:T(8,128)S(1)}, u32[]{:S(2)}, u32[]{:S(2)}) %collective-permute-start.5) | collective-permute-done | bytes 20512 | tf_op jit(solution)/shard_map/cond/branch_1_fun/ppermute | solution.py:77
  88.8 24.3 %conditional.3 = (f32[10,8,128]{2,1,0:T(8,128)}, f32[10,8,128]{2,1,0:T(8,128)}, f32[10,8,128]{2,1,0:T(8,128)}, f32[10,8,144]{2,1,0:T(8,128)}, f32[10,8,144]{2,1,0:T(8,128)}) conditional(s32[]{:T(128)} %clamp.6, (f32[10,8,128]{2,1,0:T(8,128)}, f32[10,8,144]{2,1,0:T(8,128)S(1)}, ...), branch_computations={%region_21.22_spmd, %region_22.23_spmd, %region_23.24_spmd, %regio... | conditional | bytes 860400 | solution.py:105
  89.0 1.3 %collective-permute-start.97 = (f32[10,8,144]{2,1,0:T(8,128)S(1)}, f32[10,8,144]{2,1,0:T(8,128)}, u32[]{:S(2)}, u32[]{:S(2)}) collective-permute-start(f32[10,8,144]{2,1,0:T(8,128)S(1)} %get-tuple-element.247), channel_id=1, source_target_pairs={{0,64},{64,128},{128,192},{192,256},{256,320},{320,384},{384,448},... | collective-permute-start | bytes 138248 | tf_op jit(solution)/shard_map/cond/branch_10_fun/ppermute | solution.py:99
  90.3 6.0 %collective-permute-start.98 = (f32[10,8,144]{2,1,0:T(8,128)S(1)}, f32[10,8,144]{2,1,0:T(8,128)}, u32[]{:S(2)}, u32[]{:S(2)}) collective-permute-start(f32[10,8,144]{2,1,0:T(8,128)S(1)} %get-tuple-element.248), channel_id=1, source_target_pairs={{64,0},{128,64},{192,128},{256,192},{320,256},{384,320},{448,384},... | collective-permute-start | bytes 138248 | tf_op jit(solution)/shard_map/cond/branch_10_fun/ppermute | solution.py:100
  96.3 2.7 %collective-permute-start.95 = (f32[10,8,128]{2,1,0:T(8,128)}, f32[10,8,128]{2,1,0:T(8,128)}, u32[]{:S(2)}, u32[]{:S(2)}) collective-permute-start(f32[10,8,128]{2,1,0:T(8,128)} %get-tuple-element.246), channel_id=1, source_target_pairs={{960,962},{961,963},{962,964},{963,965},{964,966},{965,967},{966,9... | collective-permute-start | bytes 122888 | tf_op jit(solution)/shard_map/cond/branch_10_fun/ppermute | solution.py:96
  99.1 12.0 %collective-permute-start.96 = (f32[10,8,128]{2,1,0:T(8,128)}, f32[10,8,128]{2,1,0:T(8,128)}, u32[]{:S(2)}, u32[]{:S(2)}) collective-permute-start(f32[10,8,128]{2,1,0:T(8,128)} %get-tuple-element.246), channel_id=1, source_target_pairs={{960,963},{961,964},{962,965},{963,966},{964,967},{965,968},{966,9... | collective-permute-start | bytes 122888 | tf_op jit(solution)/shard_map/cond/branch_10_fun/ppermute | solution.py:96
  111.1 1.4 %collective-permute-done.96 = f32[10,8,128]{2,1,0:T(8,128)} collective-permute-done((f32[10,8,128]{2,1,0:T(8,128)}, f32[10,8,128]{2,1,0:T(8,128)}, u32[]{:S(2)}, u32[]{:S(2)}) %collective-permute-start.96) | collective-permute-done | bytes 40992 | tf_op jit(solution)/shard_map/cond/branch_10_fun/ppermute | solution.py:96
  112.5 0.6 broadcast.338
  113.1 0.9 fusion.1
  114.0 0.2 reverse
  114.2 0.7 copy-done.9
  115.0 1.2 pad_maximum_fusion
  116.2 0.2 fusion.45
  116.5 0.2 fusion.38
  116.8 0.3 fusion.30
  117.3 0.2 fusion.14
  117.5 0.2 fusion.7
  117.8 0.3 fusion.105
  118.2 0.2 fusion.89
  118.5 0.2 fusion.82
  118.8 0.3 fusion.74
  119.2 0.2 fusion.58
  119.4 0.2 fusion.51
  119.7 0.7 slice.892
  120.5 0.2 fusion.133
  120.8 0.6 copy-done.1
  121.4 0.2 copy-done.8
  121.5 0.7 maximum_multiply_fusion
  (92 shorter events, 4.0 us)
Async XLA Ops:
  0.6 0.7 copy-start.10
  6.1 33.7 %copy-start.5 = (f32[2,64,128]{2,1,0:T(8,128)S(1)}, f32[2,64,128]{2,1,0:T(8,128)}, u32[]{:S(2)}) copy-start(f32[2,64,128]{2,1,0:T(8,128)} %param.42) | copy-start | bytes 196612
  6.1 68.9 %all-to-all-start = ((f32[64,1,1026]{2,1,0:T(1,128)}), f32[64,1,1026]{2,1,0:T(1,128)S(1)}, u32[]{:S(2)}, u32[]{:S(2)}) async-start(f32[64,1,1026]{2,1,0:T(1,128)} %copy.164), calls=%async_computation | async-start | bytes 589824 | tf_op jit(solution)/shard_map/all_to_all | solution.py:48
  38.9 0.8 copy-start.3
  39.0 0.9 copy-start.4
  39.7 0.9 copy-start.2
  39.7 1.0 copy-start
  76.1 0.8 copy-start.6
  76.9 0.8 copy-start.7
  77.7 10.9 %collective-permute-start.3 = (f32[10,8,128]{2,1,0:T(8,128)S(1)}, f32[10,8,128]{2,1,0:T(8,128)}, u32[]{:S(2)}, u32[]{:S(2)}) collective-permute-start(f32[10,8,128]{2,1,0:T(8,128)S(1)} %slice.710), channel_id=1, source_target_pairs={{960,964},{961,963},{962,962},{963,961},{964,960},{965,1023},{966,... | collective-permute-start | bytes 122888 | tf_op jit(solution)/shard_map/cond/branch_1_fun/ppermute | solution.py:75
  79.3 7.5 %collective-permute-start.4 = (f32[10,64,8]{1,2,0:T(8,128)S(1)}, f32[10,64,8]{1,2,0:T(8,128)S(1)}, u32[]{:S(2)}, u32[]{:S(2)}) collective-permute-start(f32[10,64,8]{1,2,0:T(8,128)S(1)} %copy.168), channel_id=1, source_target_pairs={{0,1},{1,2},{2,3},{3,4},{4,5},{5,6},{6,7},{7,8},{8,9},{9,10},{10,1... | collective-permute-start | bytes 61448 | tf_op jit(solution)/shard_map/cond/branch_1_fun/ppermute | solution.py:76
  83.7 4.7 %collective-permute-start.5 = (f32[10,64,8]{1,2,0:T(8,128)S(1)}, f32[10,64,8]{1,2,0:T(8,128)S(1)}, u32[]{:S(2)}, u32[]{:S(2)}) collective-permute-start(f32[10,64,8]{1,2,0:T(8,128)S(1)} %copy.169), channel_id=1, source_target_pairs={{0,63},{1,0},{2,1},{3,2},{4,3},{5,4},{6,5},{7,6},{8,7},{9,8},{10,9... | collective-permute-start | bytes 61448 | tf_op jit(solution)/shard_map/cond/branch_1_fun/ppermute | solution.py:77
  89.0 23.5 %collective-permute-start.97 = (f32[10,8,144]{2,1,0:T(8,128)S(1)}, f32[10,8,144]{2,1,0:T(8,128)}, u32[]{:S(2)}, u32[]{:S(2)}) collective-permute-start(f32[10,8,144]{2,1,0:T(8,128)S(1)} %get-tuple-element.247), channel_id=1, source_target_pairs={{0,64},{64,128},{128,192},{192,256},{256,320},{320,384},{384,448},... | collective-permute-start | bytes 138248 | tf_op jit(solution)/shard_map/cond/branch_10_fun/ppermute | solution.py:99
  90.3 22.2 %collective-permute-start.98 = (f32[10,8,144]{2,1,0:T(8,128)S(1)}, f32[10,8,144]{2,1,0:T(8,128)}, u32[]{:S(2)}, u32[]{:S(2)}) collective-permute-start(f32[10,8,144]{2,1,0:T(8,128)S(1)} %get-tuple-element.248), channel_id=1, source_target_pairs={{64,0},{128,64},{192,128},{256,192},{320,256},{384,320},{448,384},... | collective-permute-start | bytes 138248 | tf_op jit(solution)/shard_map/cond/branch_10_fun/ppermute | solution.py:100
  96.3 14.8 %collective-permute-start.95 = (f32[10,8,128]{2,1,0:T(8,128)}, f32[10,8,128]{2,1,0:T(8,128)}, u32[]{:S(2)}, u32[]{:S(2)}) collective-permute-start(f32[10,8,128]{2,1,0:T(8,128)} %get-tuple-element.246), channel_id=1, source_target_pairs={{960,962},{961,963},{962,964},{963,965},{964,966},{965,967},{966,9... | collective-permute-start | bytes 122888 | tf_op jit(solution)/shard_map/cond/branch_10_fun/ppermute | solution.py:96
  99.1 13.4 %collective-permute-start.96 = (f32[10,8,128]{2,1,0:T(8,128)}, f32[10,8,128]{2,1,0:T(8,128)}, u32[]{:S(2)}, u32[]{:S(2)}) collective-permute-start(f32[10,8,128]{2,1,0:T(8,128)} %get-tuple-element.246), channel_id=1, source_target_pairs={{960,963},{961,964},{962,965},{963,966},{964,967},{965,968},{966,9... | collective-permute-start | bytes 122888 | tf_op jit(solution)/shard_map/cond/branch_10_fun/ppermute | solution.py:96
  114.2 0.7 copy-start.9
  120.7 0.6 copy-start.1
  120.7 0.8 copy-start.8

commit v11 on v7

--- a/solution.py
+++ b/solution.py
@@ -48,12 +48,11 @@
     arrived = lax.all_to_all(packed, "gx", split_axis=0, concat_axis=0, tiled=True)
     flat = arrived[:, : group * fields * cols].reshape(peers * group, fields * cols)
     arrived_rows = arrived[:, group * fields * cols :].astype(jnp.int32)
-    picks = (
-        arrived_rows.reshape(-1)[None, :] == jnp.arange(rows, dtype=jnp.int32)[:, None]
-    ).astype(jnp.float32)
-    local = jnp.dot(
-        picks, flat, precision=lax.Precision.HIGHEST, preferred_element_type=jnp.float32
-    )
+    hits = arrived_rows.reshape(-1)[None, :] == jnp.arange(rows, dtype=jnp.int32)[:, None]
+    where_from = jnp.sum(
+        jnp.where(hits, jnp.arange(peers * group, dtype=jnp.int32)[None, :], 0), axis=1
+    )
+    local = jnp.take(flat, where_from, axis=0)
     return local.reshape(rows, fields, cols)
 
 

time: 122 us -> 124 us (1.016)
  the two profiles are of different devices: /device:TPU:125 before, /device:TPU:31 now
where the time goes in v11:
time: 124 us; the launch traced here: 123 us
  starting transfers between devices  60.7 us (49%)
  waiting for transfers between devices  38.7 us (31%)
  local copies, waits for them, and re-layouts  12 us (10%)
  other arithmetic  7.87 us (6%)
  between operations  3.06 us (2%)
    all_to_all x1, waiting for transfers between devices, regroup_local(): lax.all_to_all(packed, 'gx', split_axis=0, concat_axis=0, tiled=True)  32.5 us
    all_to_all x1, starting transfers between devices, regroup_local(): lax.all_to_all(packed, 'gx', split_axis=0, concat_axis=0, tiled=True)  29.9 us
    ppermute x3, starting transfers between devices, run(): lax.ppermute(y, both, on_top(lambda e, t=t: e + bb + t))  9.71 us
    ppermute x1, starting transfers between devices, run(): mirrored = lax.ppermute(top, both, on_top(lambda e: low * aa - e))  8.74 us
    ppermute x3, waiting for transfers between devices, run(): lax.ppermute(y, both, on_top(lambda e, t=t: e + bb + t))  5.23 us
    unnamed x27, local copies, waits for them, and re-layouts  5.19 us
    ppermute x1, starting transfers between devices, run(): east = lax.ppermute(east_in, 'gx', shift_pairs(nx, -1, True))  3.98 us
    ppermute x1, starting transfers between devices, run(): north = lax.ppermute(north_in, 'gy', shift_pairs(ny, -1, False))  3.66 us
  transfers between devices with their start and end apart: 9, of which 3 were waited for; matrix products, arithmetic and copies ran while one was open for 2% of the time, Pallas kernels for 0%

profile of v11, /device:TPU:31, one launch (start us, length us, event | category | flops | bytes accessed | tf_op | source)
XLA Modules:
  0.0 122.8 jit_solution(4574627094156612869)
XLA Ops:
  0.6 0.5 broadcast.469
  1.3 0.7 reduce.3
  2.6 1.0 reshape.199
  3.5 0.4 fusion.144
  4.0 1.0 copy.164
  5.0 29.9 %all-to-all-start = ((f32[64,1,1026]{2,1,0:T(1,128)}), f32[64,1,1026]{2,1,0:T(1,128)S(1)}, u32[]{:S(2)}, u32[]{:S(2)}) async-start(f32[64,1,1026]{2,1,0:T(1,128)} %copy.164), calls=%async_computation | async-start | bytes 589824 | tf_op jit(solution)/shard_map/all_to_all | solution.py:48
  34.9 1.2 slice.555
  39.0 0.4 copy-done.3
  39.5 0.5 copy-done.4
  39.9 0.4 copy-done.2
  40.5 32.5 %all-to-all-done = f32[64,1,1026]{2,1,0:T(1,128)S(1)} async-done(((f32[64,1,1026]{2,1,0:T(1,128)}), f32[64,1,1026]{2,1,0:T(1,128)S(1)}, u32[]{:S(2)}, u32[]{:S(2)}) %all-to-all-start) | async-done | bytes 262688 | tf_op jit(solution)/shard_map/all_to_all | solution.py:48
  73.4 0.7 gather_fusion
  74.2 0.8 copy-done.6
  75.0 0.7 copy-done.7
  75.8 17.8 %conditional.2 = (f32[10,8,128]{2,1,0:T(8,128)}, f32[10,64,8]{2,1,0:T(8,128)S(1)}, f32[10,64,8]{2,1,0:T(8,128)S(1)}) conditional(s32[]{:T(128)} %clamp.7, (f32[10,64,128]{2,1,0:T(8,128)S(1)}, f32[10,64,128]{2,1,0:T(8,128)S(1)}, f32[10,64,128]{2,1,0:T(8,128)S(1)}) %tuple.120, (f32[10,64,128]{2,1,0:T(8,128)S(1)}, ...), branch_computations={%region_4.5_spmd, %region_5.6_spmd, %region_6.7_spmd, %region_7.8_... | conditional | bytes 614544 | solution.py:82
  75.8 8.7 %collective-permute-start.45 = (f32[10,8,128]{2,1,0:T(8,128)S(1)}, f32[10,8,128]{2,1,0:T(8,128)}, u32[]{:S(2)}, u32[]{:S(2)}) collective-permute-start(f32[10,8,128]{2,1,0:T(8,128)S(1)} %slice.724), channel_id=1, source_target_pairs={{960,1020},{961,1019},{962,1018},{963,1017},{964,1016},{965,1015},... | collective-permute-start | bytes 122888 | tf_op jit(solution)/shard_map/cond/branch_15_fun/ppermute | solution.py:75
  84.5 0.1 slice.740
  84.8 3.4 %collective-permute-start.46 = (f32[10,64,8]{1,2,0:T(8,128)S(1)}, f32[10,64,8]{1,2,0:T(8,128)S(1)}, u32[]{:S(2)}, u32[]{:S(2)}) collective-permute-start(f32[10,64,8]{1,2,0:T(8,128)S(1)} %copy.196), channel_id=1, source_target_pairs={{0,1},{1,2},{2,3},{3,4},{4,5},{5,6},{6,7},{7,8},{8,9},{9,10},{10,1... | collective-permute-start | bytes 61448 | tf_op jit(solution)/shard_map/cond/branch_15_fun/ppermute | solution.py:76
  88.4 4.0 %collective-permute-start.47 = (f32[10,64,8]{1,2,0:T(8,128)S(1)}, f32[10,64,8]{1,2,0:T(8,128)S(1)}, u32[]{:S(2)}, u32[]{:S(2)}) collective-permute-start(f32[10,64,8]{1,2,0:T(8,128)S(1)} %copy.197), channel_id=1, source_target_pairs={{0,63},{1,0},{2,1},{3,2},{4,3},{5,4},{6,5},{7,6},{8,7},{9,8},{10,9... | collective-permute-start | bytes 61448 | tf_op jit(solution)/shard_map/cond/branch_15_fun/ppermute | solution.py:77
  92.3 0.1 copy.215
  92.5 0.9 collective-permute-done.47
  93.7 20.0 %conditional.3 = (f32[10,8,128]{2,1,0:T(8,128)}, f32[10,8,128]{2,1,0:T(8,128)}, f32[10,8,128]{2,1,0:T(8,128)}, f32[10,8,144]{2,1,0:T(8,128)}, f32[10,8,144]{2,1,0:T(8,128)}) conditional(s32[]{:T(128)} %clamp.6, (f32[10,8,128]{2,1,0:T(8,128)}, f32[10,8,144]{2,1,0:T(8,128)S(1)}, ...), branch_computations={%region_20.21_spmd, %region_21.22_spmd, %region_22.23_spmd, %regio... | conditional | bytes 860400 | solution.py:105
  93.7 1.3 %collective-permute-start.65 = (f32[10,8,144]{2,1,0:T(8,128)S(1)}, f32[10,8,144]{2,1,0:T(8,128)}, u32[]{:S(2)}, u32[]{:S(2)}) collective-permute-start(f32[10,8,144]{2,1,0:T(8,128)S(1)} %get-tuple-element.226), channel_id=1, source_target_pairs={{0,64},{64,128},{128,192},{192,256},{256,320},{320,384},{384,448},... | collective-permute-start | bytes 138248 | tf_op jit(solution)/shard_map/cond/branch_3_fun/ppermute | solution.py:99
  95.0 3.7 %collective-permute-start.66 = (f32[10,8,144]{2,1,0:T(8,128)S(1)}, f32[10,8,144]{2,1,0:T(8,128)}, u32[]{:S(2)}, u32[]{:S(2)}) collective-permute-start(f32[10,8,144]{2,1,0:T(8,128)S(1)} %get-tuple-element.227), channel_id=1, source_target_pairs={{64,0},{128,64},{192,128},{256,192},{320,256},{384,320},{448,384},... | collective-permute-start | bytes 138248 | tf_op jit(solution)/shard_map/cond/branch_3_fun/ppermute | solution.py:100
  98.7 5.8 %collective-permute-start.62 = (f32[10,8,128]{2,1,0:T(8,128)}, f32[10,8,128]{2,1,0:T(8,128)}, u32[]{:S(2)}, u32[]{:S(2)}) collective-permute-start(f32[10,8,128]{2,1,0:T(8,128)} %get-tuple-element.225), channel_id=1, source_target_pairs={{960,1023},{961,960},{962,961},{963,962},{964,963},{965,964},{966,... | collective-permute-start | bytes 122888 | tf_op jit(solution)/shard_map/cond/branch_3_fun/ppermute | solution.py:96
  104.5 2.0 %collective-permute-start.63 = (f32[10,8,128]{2,1,0:T(8,128)}, f32[10,8,128]{2,1,0:T(8,128)}, u32[]{:S(2)}, u32[]{:S(2)}) collective-permute-start(f32[10,8,128]{2,1,0:T(8,128)} %get-tuple-element.225), channel_id=1, source_target_pairs={{960,960},{961,961},{962,962},{963,963},{964,964},{965,965},{966,9... | collective-permute-start | bytes 122888 | tf_op jit(solution)/shard_map/cond/branch_3_fun/ppermute | solution.py:96
  106.5 1.9 %collective-permute-start.64 = (f32[10,8,128]{2,1,0:T(8,128)}, f32[10,8,128]{2,1,0:T(8,128)}, u32[]{:S(2)}, u32[]{:S(2)}) collective-permute-start(f32[10,8,128]{2,1,0:T(8,128)} %get-tuple-element.225), channel_id=1, source_target_pairs={{960,961},{961,962},{962,963},{963,964},{964,965},{965,966},{966,9... | collective-permute-start | bytes 122888 | tf_op jit(solution)/shard_map/cond/branch_3_fun/ppermute | solution.py:96
  108.5 5.2 %collective-permute-done.64 = f32[10,8,128]{2,1,0:T(8,128)} collective-permute-done((f32[10,8,128]{2,1,0:T(8,128)}, f32[10,8,128]{2,1,0:T(8,128)}, u32[]{:S(2)}, u32[]{:S(2)}) %collective-permute-start.64) | collective-permute-done | bytes 40992 | tf_op jit(solution)/shard_map/cond/branch_3_fun/ppermute | solution.py:96
  113.7 0.9 fusion.1
  114.6 0.2 reverse
  114.8 0.7 copy-done.9
  115.6 1.2 pad_maximum_fusion
  116.8 0.2 fusion.45
  117.1 0.2 fusion.38
  117.4 0.3 fusion.30
  117.9 0.2 fusion.14
  118.1 0.2 fusion.7
  118.4 0.3 fusion.105
  118.8 0.2 fusion.89
  119.1 0.2 fusion.82
  119.4 0.3 fusion.74
  119.8 0.2 fusion.58
  120.0 0.2 fusion.51
  120.3 0.7 slice.890
  121.1 0.2 fusion.133
  121.4 0.6 copy-done.1
  121.9 0.2 copy-done.8
  122.1 0.7 maximum_multiply_fusion
  (87 shorter events, 3.8 us)
Async XLA Ops:
  0.6 0.7 copy-start.10
  5.0 68.0 %all-to-all-start = ((f32[64,1,1026]{2,1,0:T(1,128)}), f32[64,1,1026]{2,1,0:T(1,128)S(1)}, u32[]{:S(2)}, u32[]{:S(2)}) async-start(f32[64,1,1026]{2,1,0:T(1,128)} %copy.164), calls=%async_computation | async-start | bytes 589824 | tf_op jit(solution)/shard_map/all_to_all | solution.py:48
  38.0 1.4 %copy-start.5 = (f32[2,64,128]{2,1,0:T(8,128)S(1)}, f32[2,64,128]{2,1,0:T(8,128)}, u32[]{:S(2)}) copy-start(f32[2,64,128]{2,1,0:T(8,128)} %param.42) | copy-start | bytes 196612
  38.7 0.8 copy-start.3
  39.0 0.9 copy-start.4
  39.4 0.9 copy-start.2
  39.4 1.0 copy-start
  74.2 0.8 copy-start.6
  75.0 0.8 copy-start.7
  75.8 17.8 %collective-permute-start.45 = (f32[10,8,128]{2,1,0:T(8,128)S(1)}, f32[10,8,128]{2,1,0:T(8,128)}, u32[]{:S(2)}, u32[]{:S(2)}) collective-permute-start(f32[10,8,128]{2,1,0:T(8,128)S(1)} %slice.724), channel_id=1, source_target_pairs={{960,1020},{961,1019},{962,1018},{963,1017},{964,1016},{965,1015},... | collective-permute-start | bytes 122888 | tf_op jit(solution)/shard_map/cond/branch_15_fun/ppermute | solution.py:75
  84.8 7.5 %collective-permute-start.46 = (f32[10,64,8]{1,2,0:T(8,128)S(1)}, f32[10,64,8]{1,2,0:T(8,128)S(1)}, u32[]{:S(2)}, u32[]{:S(2)}) collective-permute-start(f32[10,64,8]{1,2,0:T(8,128)S(1)} %copy.196), channel_id=1, source_target_pairs={{0,1},{1,2},{2,3},{3,4},{4,5},{5,6},{6,7},{7,8},{8,9},{9,10},{10,1... | collective-permute-start | bytes 61448 | tf_op jit(solution)/shard_map/cond/branch_15_fun/ppermute | solution.py:76
  88.4 5.1 %collective-permute-start.47 = (f32[10,64,8]{1,2,0:T(8,128)S(1)}, f32[10,64,8]{1,2,0:T(8,128)S(1)}, u32[]{:S(2)}, u32[]{:S(2)}) collective-permute-start(f32[10,64,8]{1,2,0:T(8,128)S(1)} %copy.197), channel_id=1, source_target_pairs={{0,63},{1,0},{2,1},{3,2},{4,3},{5,4},{6,5},{7,6},{8,7},{9,8},{10,9... | collective-permute-start | bytes 61448 | tf_op jit(solution)/shard_map/cond/branch_15_fun/ppermute | solution.py:77
  93.7 19.9 %collective-permute-start.65 = (f32[10,8,144]{2,1,0:T(8,128)S(1)}, f32[10,8,144]{2,1,0:T(8,128)}, u32[]{:S(2)}, u32[]{:S(2)}) collective-permute-start(f32[10,8,144]{2,1,0:T(8,128)S(1)} %get-tuple-element.226), channel_id=1, source_target_pairs={{0,64},{64,128},{128,192},{192,256},{256,320},{320,384},{384,448},... | collective-permute-start | bytes 138248 | tf_op jit(solution)/shard_map/cond/branch_3_fun/ppermute | solution.py:99
  95.0 18.6 %collective-permute-start.66 = (f32[10,8,144]{2,1,0:T(8,128)S(1)}, f32[10,8,144]{2,1,0:T(8,128)}, u32[]{:S(2)}, u32[]{:S(2)}) collective-permute-start(f32[10,8,144]{2,1,0:T(8,128)S(1)} %get-tuple-element.227), channel_id=1, source_target_pairs={{64,0},{128,64},{192,128},{256,192},{320,256},{384,320},{448,384},... | collective-permute-start | bytes 138248 | tf_op jit(solution)/shard_map/cond/branch_3_fun/ppermute | solution.py:100
  98.7 9.7 %collective-permute-start.62 = (f32[10,8,128]{2,1,0:T(8,128)}, f32[10,8,128]{2,1,0:T(8,128)}, u32[]{:S(2)}, u32[]{:S(2)}) collective-permute-start(f32[10,8,128]{2,1,0:T(8,128)} %get-tuple-element.225), channel_id=1, source_target_pairs={{960,1023},{961,960},{962,961},{963,962},{964,963},{965,964},{966,... | collective-permute-start | bytes 122888 | tf_op jit(solution)/shard_map/cond/branch_3_fun/ppermute | solution.py:96
  104.5 4.0 %collective-permute-start.63 = (f32[10,8,128]{2,1,0:T(8,128)}, f32[10,8,128]{2,1,0:T(8,128)}, u32[]{:S(2)}, u32[]{:S(2)}) collective-permute-start(f32[10,8,128]{2,1,0:T(8,128)} %get-tuple-element.225), channel_id=1, source_target_pairs={{960,960},{961,961},{962,962},{963,963},{964,964},{965,965},{966,9... | collective-permute-start | bytes 122888 | tf_op jit(solution)/shard_map/cond/branch_3_fun/ppermute | solution.py:96
  106.5 7.2 %collective-permute-start.64 = (f32[10,8,128]{2,1,0:T(8,128)}, f32[10,8,128]{2,1,0:T(8,128)}, u32[]{:S(2)}, u32[]{:S(2)}) collective-permute-start(f32[10,8,128]{2,1,0:T(8,128)} %get-tuple-element.225), channel_id=1, source_target_pairs={{960,961},{961,962},{962,963},{963,964},{964,965},{965,966},{966,9... | collective-permute-start | bytes 122888 | tf_op jit(solution)/shard_map/cond/branch_3_fun/ppermute | solution.py:96
  114.8 0.7 copy-start.9
  121.3 0.6 copy-start.1
  121.3 0.8 copy-start.8

commit v12 on v7

--- a/solution.py
+++ b/solution.py
@@ -83,7 +83,7 @@
     mirrored, west, east = lax.switch(
         a,
         [stage_one(aa) for aa in range(nx // low)],
-        stack[:, -w:, :],
+        stack[:, -w:, :] * signs,
         stack[:, :, -w:],
         stack[:, :, :w],
     )
@@ -114,7 +114,7 @@
     lowest = jnp.where(span == 0, 2, 1)
     first = lowest * cols + fold_rest - (cols - 1) - w
     window = lax.dynamic_slice_in_dim(strip, first, cols + 2 * w, axis=2)
-    folded = jnp.flip(window, axis=(1, 2)) * signs
+    folded = jnp.flip(window, axis=(1, 2))
     north = jnp.where(lax.axis_index("gy") == ny - 1, folded, north)
     return jnp.concatenate([south, wide, north], axis=1)
 

time: 122 us -> 126 us (1.033)
  the two profiles are of different devices: /device:TPU:125 before, /device:TPU:61 now
where the time goes in v12:
time: 126 us; the launch traced here: 125 us
  starting transfers between devices  63.9 us (51%)
  waiting for transfers between devices  37.3 us (30%)
  local copies, waits for them, and re-layouts  12.1 us (10%)
  other arithmetic  7.73 us (6%)
  between operations  3.04 us (2%)
    all_to_all x1, waiting for transfers between devices, regroup_local(): lax.all_to_all(packed, 'gx', split_axis=0, concat_axis=0, tiled=True)  34 us
    all_to_all x1, starting transfers between devices, regroup_local(): lax.all_to_all(packed, 'gx', split_axis=0, concat_axis=0, tiled=True)  29.1 us
    ppermute x2, starting transfers between devices, run(): lax.ppermute(y, both, on_top(lambda e, t=t: e + bb + t))  17.1 us
    ppermute x1, starting transfers between devices, run(): mirrored = lax.ppermute(top, both, on_top(lambda e: low * aa - e))  7.51 us
    unnamed x25, local copies, waits for them, and re-layouts  4.53 us
    ppermute x1, starting transfers between devices, run(): north = lax.ppermute(north_in, 'gy', shift_pairs(ny, -1, False))  3.68 us
    ppermute x1, starting transfers between devices, run(): east = lax.ppermute(east_in, 'gx', shift_pairs(nx, -1, True))  2.74 us
    ppermute x1, starting transfers between devices, run(): west = lax.ppermute(west_in, 'gx', shift_pairs(nx, 1, True))  2.55 us
  transfers between devices with their start and end apart: 8, of which 3 were waited for; matrix products, arithmetic and copies ran while one was open for 2% of the time, Pallas kernels for 0%

profile of v12, /device:TPU:61, one launch (start us, length us, event | category | flops | bytes accessed | tf_op | source)
XLA Modules:
  0.0 125.0 jit_solution(9203054277554267394)
XLA Ops:
  0.6 0.5 broadcast.435
  1.3 0.7 reduce.3
  2.6 1.0 reshape.177
  3.5 0.4 fusion.147
  4.0 1.0 copy.164
  5.0 29.1 %all-to-all-start = ((f32[64,1,1026]{2,1,0:T(1,128)}), f32[64,1,1026]{2,1,0:T(1,128)S(1)}, u32[]{:S(2)}, u32[]{:S(2)}) async-start(f32[64,1,1026]{2,1,0:T(1,128)} %copy.164), calls=%async_computation | async-start | bytes 589824 | tf_op jit(solution)/shard_map/all_to_all | solution.py:48
  34.1 1.2 slice.555
  38.2 0.4 copy-done.3
  38.6 0.5 copy-done.4
  39.1 0.4 copy-done.2
  39.7 34.0 %all-to-all-done = f32[64,1,1026]{2,1,0:T(1,128)S(1)} async-done(((f32[64,1,1026]{2,1,0:T(1,128)}), f32[64,1,1026]{2,1,0:T(1,128)S(1)}, u32[]{:S(2)}, u32[]{:S(2)}) %all-to-all-start) | async-done | bytes 262688 | tf_op jit(solution)/shard_map/all_to_all | solution.py:48
  73.9 0.1 eq.47
  74.1 0.3 fusion.138
  74.4 0.8 copy-done.6
  75.2 0.7 copy-done.7
  76.0 16.1 %conditional.2 = (f32[10,8,128]{2,1,0:T(8,128)}, f32[10,64,8]{2,1,0:T(8,128)S(1)}, f32[10,64,8]{2,1,0:T(8,128)S(1)}) conditional(s32[]{:T(128)} %clamp.7, (f32[10,64,128]{2,1,0:T(8,128)S(1)}, f32[10,64,128]{2,1,0:T(8,128)S(1)}, f32[10,64,128]{2,1,0:T(8,128)S(1)}, ()) %tuple.120, (f32[10,64,128]{2,1,0:T(8,128)S(1)}, ...), branch_computations={%region_3.4_spmd, %region_4.5_spmd, %region_5.6_spmd, %region_6.7_... | conditional | flops 10240 | bytes 614772 | solution.py:83
  76.0 0.6 copy-done.23
  76.7 7.5 %collective-permute-start.101 = (f32[10,8,128]{2,1,0:T(8,128)S(1)}, f32[10,8,128]{2,1,0:T(8,128)}, u32[]{:S(2)}, u32[]{:S(2)}) collective-permute-start(f32[10,8,128]{2,1,0:T(8,128)S(1)} %slice_multiply_fusion.15), channel_id=1, source_target_pairs={{960,1020},{961,1019},{962,1018},{963,1017},{964,1016},{965,1015},... | collective-permute-start | bytes 122888 | tf_op jit(solution)/shard_map/cond/branch_15_fun/ppermute | solution.py:76
  84.5 2.5 %collective-permute-start.102 = (f32[10,64,8]{1,2,0:T(8,128)S(1)}, f32[10,64,8]{1,2,0:T(8,128)S(1)}, u32[]{:S(2)}, u32[]{:S(2)}) collective-permute-start(f32[10,64,8]{1,2,0:T(8,128)S(1)} %copy.196), channel_id=1, source_target_pairs={{0,1},{1,2},{2,3},{3,4},{4,5},{5,6},{6,7},{7,8},{8,9},{9,10},{10,1... | collective-permute-start | bytes 61448 | tf_op jit(solution)/shard_map/cond/branch_15_fun/ppermute | solution.py:77
  87.2 2.7 %collective-permute-start.103 = (f32[10,64,8]{1,2,0:T(8,128)S(1)}, f32[10,64,8]{1,2,0:T(8,128)S(1)}, u32[]{:S(2)}, u32[]{:S(2)}) collective-permute-start(f32[10,64,8]{1,2,0:T(8,128)S(1)} %copy.197), channel_id=1, source_target_pairs={{0,63},{1,0},{2,1},{3,2},{4,3},{5,4},{6,5},{7,6},{8,7},{9,8},{10,9... | collective-permute-start | bytes 61448 | tf_op jit(solution)/shard_map/cond/branch_15_fun/ppermute | solution.py:78
  89.9 0.1 copy.215
  90.1 1.8 %collective-permute-done.103 = f32[10,64,8]{1,2,0:T(8,128)S(1)} collective-permute-done((f32[10,64,8]{1,2,0:T(8,128)S(1)}, f32[10,64,8]{1,2,0:T(8,128)S(1)}, u32[]{:S(2)}, u32[]{:S(2)}) %collective-permute-start.103) | collective-permute-done | bytes 20512 | tf_op jit(solution)/shard_map/cond/branch_15_fun/ppermute | solution.py:78
  92.2 24.4 %conditional.3 = (f32[10,8,128]{2,1,0:T(8,128)}, f32[10,8,128]{2,1,0:T(8,128)}, f32[10,8,128]{2,1,0:T(8,128)}, f32[10,8,144]{2,1,0:T(8,128)}, f32[10,8,144]{2,1,0:T(8,128)}) conditional(s32[]{:T(128)} %clamp.6, (f32[10,8,128]{2,1,0:T(8,128)}, f32[10,8,144]{2,1,0:T(8,128)S(1)}, ...), branch_computations={%region_19.20_spmd, %region_20.21_spmd, %region_21.22_spmd, %regio... | conditional | bytes 860400 | solution.py:106
  92.4 1.3 %collective-permute-start.49 = (f32[10,8,144]{2,1,0:T(8,128)S(1)}, f32[10,8,144]{2,1,0:T(8,128)}, u32[]{:S(2)}, u32[]{:S(2)}) collective-permute-start(f32[10,8,144]{2,1,0:T(8,128)S(1)} %get-tuple-element.247), channel_id=1, source_target_pairs={{0,64},{64,128},{128,192},{192,256},{256,320},{320,384},{384,448},... | collective-permute-start | bytes 138248 | tf_op jit(solution)/shard_map/cond/branch_10_fun/ppermute | solution.py:100
  93.7 3.7 %collective-permute-start.50 = (f32[10,8,144]{2,1,0:T(8,128)S(1)}, f32[10,8,144]{2,1,0:T(8,128)}, u32[]{:S(2)}, u32[]{:S(2)}) collective-permute-start(f32[10,8,144]{2,1,0:T(8,128)S(1)} %get-tuple-element.248), channel_id=1, source_target_pairs={{64,0},{128,64},{192,128},{256,192},{320,256},{384,320},{448,384},... | collective-permute-start | bytes 138248 | tf_op jit(solution)/shard_map/cond/branch_10_fun/ppermute | solution.py:101
  97.4 7.2 %collective-permute-start.47 = (f32[10,8,128]{2,1,0:T(8,128)}, f32[10,8,128]{2,1,0:T(8,128)}, u32[]{:S(2)}, u32[]{:S(2)}) collective-permute-start(f32[10,8,128]{2,1,0:T(8,128)} %get-tuple-element.246), channel_id=1, source_target_pairs={{960,962},{961,963},{962,964},{963,965},{964,966},{965,967},{966,9... | collective-permute-start | bytes 122888 | tf_op jit(solution)/shard_map/cond/branch_10_fun/ppermute | solution.py:97
  104.6 9.9 %collective-permute-start.48 = (f32[10,8,128]{2,1,0:T(8,128)}, f32[10,8,128]{2,1,0:T(8,128)}, u32[]{:S(2)}, u32[]{:S(2)}) collective-permute-start(f32[10,8,128]{2,1,0:T(8,128)} %get-tuple-element.246), channel_id=1, source_target_pairs={{960,963},{961,964},{962,965},{963,966},{964,967},{965,968},{966,9... | collective-permute-start | bytes 122888 | tf_op jit(solution)/shard_map/cond/branch_10_fun/ppermute | solution.py:97
  114.6 1.4 %collective-permute-done.48 = f32[10,8,128]{2,1,0:T(8,128)} collective-permute-done((f32[10,8,128]{2,1,0:T(8,128)}, f32[10,8,128]{2,1,0:T(8,128)}, u32[]{:S(2)}, u32[]{:S(2)}) %collective-permute-start.48) | collective-permute-done | bytes 40992 | tf_op jit(solution)/shard_map/cond/branch_10_fun/ppermute | solution.py:97
  115.9 0.6 broadcast.248
  116.6 0.9 fusion.1
  117.5 0.2 reverse
  117.8 1.2 pad_maximum_fusion
  119.0 0.2 fusion.45
  119.3 0.2 fusion.38
  119.6 0.3 fusion.30
  120.1 0.2 fusion.14
  120.3 0.2 fusion.7
  120.6 0.3 fusion.105
  121.0 0.2 fusion.89
  121.3 0.2 fusion.82
  121.6 0.3 fusion.74
  122.0 0.2 fusion.58
  122.2 0.2 fusion.51
  122.5 0.7 slice.888
  123.3 0.2 fusion.133
  123.6 0.6 copy-done.1
  124.1 0.2 copy-done.8
  124.3 0.7 maximum_multiply_fusion
  (82 shorter events, 3.8 us)
Async XLA Ops:
  0.6 0.7 copy-start.25
  5.0 68.7 %all-to-all-start = ((f32[64,1,1026]{2,1,0:T(1,128)}), f32[64,1,1026]{2,1,0:T(1,128)S(1)}, u32[]{:S(2)}, u32[]{:S(2)}) async-start(f32[64,1,1026]{2,1,0:T(1,128)} %copy.164), calls=%async_computation | async-start | bytes 589824 | tf_op jit(solution)/shard_map/all_to_all | solution.py:48
  37.2 1.4 %copy-start.5 = (f32[2,64,128]{2,1,0:T(8,128)S(1)}, f32[2,64,128]{2,1,0:T(8,128)}, u32[]{:S(2)}) copy-start(f32[2,64,128]{2,1,0:T(8,128)} %param.42) | copy-start | bytes 196612
  37.8 0.8 copy-start.3
  38.2 0.9 copy-start.4
  38.6 0.9 copy-start.2
  38.6 1.0 copy-start
  74.4 0.8 copy-start.6
  75.2 0.8 copy-start.7
  76.0 0.7 copy-start.23
  76.7 15.4 %collective-permute-start.101 = (f32[10,8,128]{2,1,0:T(8,128)S(1)}, f32[10,8,128]{2,1,0:T(8,128)}, u32[]{:S(2)}, u32[]{:S(2)}) collective-permute-start(f32[10,8,128]{2,1,0:T(8,128)S(1)} %slice_multiply_fusion.15), channel_id=1, source_target_pairs={{960,1020},{961,1019},{962,1018},{963,1017},{964,1016},{965,1015},... | collective-permute-start | bytes 122888 | tf_op jit(solution)/shard_map/cond/branch_15_fun/ppermute | solution.py:76
  84.5 5.4 %collective-permute-start.102 = (f32[10,64,8]{1,2,0:T(8,128)S(1)}, f32[10,64,8]{1,2,0:T(8,128)S(1)}, u32[]{:S(2)}, u32[]{:S(2)}) collective-permute-start(f32[10,64,8]{1,2,0:T(8,128)S(1)} %copy.196), channel_id=1, source_target_pairs={{0,1},{1,2},{2,3},{3,4},{4,5},{5,6},{6,7},{7,8},{8,9},{9,10},{10,1... | collective-permute-start | bytes 61448 | tf_op jit(solution)/shard_map/cond/branch_15_fun/ppermute | solution.py:77
  87.2 4.7 %collective-permute-start.103 = (f32[10,64,8]{1,2,0:T(8,128)S(1)}, f32[10,64,8]{1,2,0:T(8,128)S(1)}, u32[]{:S(2)}, u32[]{:S(2)}) collective-permute-start(f32[10,64,8]{1,2,0:T(8,128)S(1)} %copy.197), channel_id=1, source_target_pairs={{0,63},{1,0},{2,1},{3,2},{4,3},{5,4},{6,5},{7,6},{8,7},{9,8},{10,9... | collective-permute-start | bytes 61448 | tf_op jit(solution)/shard_map/cond/branch_15_fun/ppermute | solution.py:78
  92.4 23.5 %collective-permute-start.49 = (f32[10,8,144]{2,1,0:T(8,128)S(1)}, f32[10,8,144]{2,1,0:T(8,128)}, u32[]{:S(2)}, u32[]{:S(2)}) collective-permute-start(f32[10,8,144]{2,1,0:T(8,128)S(1)} %get-tuple-element.247), channel_id=1, source_target_pairs={{0,64},{64,128},{128,192},{192,256},{256,320},{320,384},{384,448},... | collective-permute-start | bytes 138248 | tf_op jit(solution)/shard_map/cond/branch_10_fun/ppermute | solution.py:100
  93.7 22.2 %collective-permute-start.50 = (f32[10,8,144]{2,1,0:T(8,128)S(1)}, f32[10,8,144]{2,1,0:T(8,128)}, u32[]{:S(2)}, u32[]{:S(2)}) collective-permute-start(f32[10,8,144]{2,1,0:T(8,128)S(1)} %get-tuple-element.248), channel_id=1, source_target_pairs={{64,0},{128,64},{192,128},{256,192},{320,256},{384,320},{448,384},... | collective-permute-start | bytes 138248 | tf_op jit(solution)/shard_map/cond/branch_10_fun/ppermute | solution.py:101
  97.4 17.1 %collective-permute-start.47 = (f32[10,8,128]{2,1,0:T(8,128)}, f32[10,8,128]{2,1,0:T(8,128)}, u32[]{:S(2)}, u32[]{:S(2)}) collective-permute-start(f32[10,8,128]{2,1,0:T(8,128)} %get-tuple-element.246), channel_id=1, source_target_pairs={{960,962},{961,963},{962,964},{963,965},{964,966},{965,967},{966,9... | collective-permute-start | bytes 122888 | tf_op jit(solution)/shard_map/cond/branch_10_fun/ppermute | solution.py:97
  104.6 11.4 %collective-permute-start.48 = (f32[10,8,128]{2,1,0:T(8,128)}, f32[10,8,128]{2,1,0:T(8,128)}, u32[]{:S(2)}, u32[]{:S(2)}) collective-permute-start(f32[10,8,128]{2,1,0:T(8,128)} %get-tuple-element.246), channel_id=1, source_target_pairs={{960,963},{961,964},{962,965},{963,966},{964,967},{965,968},{966,9... | collective-permute-start | bytes 122888 | tf_op jit(solution)/shard_map/cond/branch_10_fun/ppermute | solution.py:97
  123.5 0.6 copy-start.1
  123.5 0.8 copy-start.8

commit v13 on v11

--- a/solution.py
+++ b/solution.py
@@ -82,7 +82,7 @@
     mirrored, west, east = lax.switch(
         a,
         [stage_one(aa) for aa in range(nx // low)],
-        stack[:, -w:, :],
+        stack[:, -w:, :] * signs,
         stack[:, :, -w:],
         stack[:, :, :w],
     )
@@ -113,7 +113,7 @@
     lowest = jnp.where(span == 0, 2, 1)
     first = lowest * cols + fold_rest - (cols - 1) - w
     window = lax.dynamic_slice_in_dim(strip, first, cols + 2 * w, axis=2)
-    folded = jnp.flip(window, axis=(1, 2)) * signs
+    folded = jnp.flip(window, axis=(1, 2))
     north = jnp.where(lax.axis_index("gy") == ny - 1, folded, north)
     return jnp.concatenate([south, wide, north], axis=1)
 

time: 124 us -> 120 us (0.968)
  the two profiles are of different devices: /device:TPU:31 before, /device:TPU:29 now
where the time goes in v13:
time: 120 us; the launch traced here: 119 us
  starting transfers between devices  58.1 us (48%)
  waiting for transfers between devices  36.4 us (30%)
  local copies, waits for them, and re-layouts  12.6 us (10%)
  other arithmetic  7.94 us (7%)
  between operations  3.06 us (3%)
    all_to_all x1, waiting for transfers between devices, regroup_local(): lax.all_to_all(packed, 'gx', split_axis=0, concat_axis=0, tiled=True)  33.5 us
    all_to_all x1, starting transfers between devices, regroup_local(): lax.all_to_all(packed, 'gx', split_axis=0, concat_axis=0, tiled=True)  29.7 us
    ppermute x2, starting transfers between devices, run(): lax.ppermute(y, both, on_top(lambda e, t=t: e + bb + t))  8.89 us
    ppermute x1, starting transfers between devices, run(): north = lax.ppermute(north_in, 'gy', shift_pairs(ny, -1, False))  7.71 us
    ppermute x1, starting transfers between devices, run(): east = lax.ppermute(east_in, 'gx', shift_pairs(nx, -1, True))  5.2 us
    unnamed x25, local copies, waits for them, and re-layouts  4.53 us
    ppermute x1, starting transfers between devices, run(): west = lax.ppermute(west_in, 'gx', shift_pairs(nx, 1, True))  4.08 us
  transfers between devices with their start and end apart: 8, of which 3 were waited for; matrix products, arithmetic and copies ran while one was open for 2% of the time, Pallas kernels for 0%

profile of v13, /device:TPU:29, one launch (start us, length us, event | category | flops | bytes accessed | tf_op | source)
XLA Modules:
  0.0 118.8 jit_solution(9904514498613422970)
XLA Ops:
  0.6 0.5 broadcast.469
  1.3 0.7 reduce.3
  2.6 1.0 reshape.199
  3.5 0.4 fusion.144
  4.0 1.0 copy.164
  5.0 29.7 %all-to-all-start = ((f32[64,1,1026]{2,1,0:T(1,128)}), f32[64,1,1026]{2,1,0:T(1,128)S(1)}, u32[]{:S(2)}, u32[]{:S(2)}) async-start(f32[64,1,1026]{2,1,0:T(1,128)} %copy.164), calls=%async_computation | async-start | bytes 589824 | tf_op jit(solution)/shard_map/all_to_all | solution.py:48
  34.7 1.2 %slice.555 = s32[1]{0:T(128)} slice(s32[8192]{0:T(1024)} %param.50), slice={[0:1]} | slice | bytes 8 | tf_op jit(solution)/shard_map/slice | solution.py:233
  38.8 0.4 copy-done.3
  39.2 0.5 copy-done.4
  39.7 0.4 copy-done.2
  40.3 33.5 %all-to-all-done = f32[64,1,1026]{2,1,0:T(1,128)S(1)} async-done(((f32[64,1,1026]{2,1,0:T(1,128)}), f32[64,1,1026]{2,1,0:T(1,128)S(1)}, u32[]{:S(2)}, u32[]{:S(2)}) %all-to-all-start) | async-done | bytes 262688 | tf_op jit(solution)/shard_map/all_to_all | solution.py:48
  74.2 0.7 gather_fusion
  75.0 0.8 copy-done.6
  75.8 0.7 copy-done.7
  76.5 13.0 %conditional.2 = (f32[10,8,128]{2,1,0:T(8,128)}, f32[10,64,8]{2,1,0:T(8,128)S(1)}, f32[10,64,8]{2,1,0:T(8,128)S(1)}) conditional(s32[]{:T(128)} %clamp.7, (f32[10,64,128]{2,1,0:T(8,128)S(1)}, f32[10,64,128]{2,1,0:T(8,128)S(1)}, f32[10,64,128]{2,1,0:T(8,128)S(1)}, ()) %tuple.120, (f32[10,64,128]{2,1,0:T(8,128)S(1)}, ...), branch_computations={%region_4.5_spmd, %region_5.6_spmd, %region_6.7_spmd, %region_7.8_... | conditional | flops 10240 | bytes 614772 | solution.py:82
  76.6 0.6 copy-done.24
  77.3 1.3 %collective-permute-start.56 = (f32[10,8,128]{2,1,0:T(8,128)S(1)}, f32[10,8,128]{2,1,0:T(8,128)}, u32[]{:S(2)}, u32[]{:S(2)}) collective-permute-start(f32[10,8,128]{2,1,0:T(8,128)S(1)} %slice_multiply_fusion), channel_id=1, source_target_pairs={{960,960},{961,1023},{962,1022},{963,1021},{964,1020},{965,1019},{... | collective-permute-start | bytes 122888 | tf_op jit(solution)/shard_map/cond/branch_0_fun/ppermute | solution.py:75
  78.5 0.1 slice.709
  78.8 4.1 %collective-permute-start.57 = (f32[10,64,8]{1,2,0:T(8,128)S(1)}, f32[10,64,8]{1,2,0:T(8,128)S(1)}, u32[]{:S(2)}, u32[]{:S(2)}) collective-permute-start(f32[10,64,8]{1,2,0:T(8,128)S(1)} %copy.166), channel_id=1, source_target_pairs={{0,1},{1,2},{2,3},{3,4},{4,5},{5,6},{6,7},{7,8},{8,9},{9,10},{10,1... | collective-permute-start | bytes 61448 | tf_op jit(solution)/shard_map/cond/branch_0_fun/ppermute | solution.py:76
  83.0 5.2 %collective-permute-start.58 = (f32[10,64,8]{1,2,0:T(8,128)S(1)}, f32[10,64,8]{1,2,0:T(8,128)S(1)}, u32[]{:S(2)}, u32[]{:S(2)}) collective-permute-start(f32[10,64,8]{1,2,0:T(8,128)S(1)} %copy.167), channel_id=1, source_target_pairs={{0,63},{1,0},{2,1},{3,2},{4,3},{5,4},{6,5},{7,6},{8,7},{9,8},{10,9... | collective-permute-start | bytes 61448 | tf_op jit(solution)/shard_map/cond/branch_0_fun/ppermute | solution.py:77
  88.3 0.1 copy.200
  88.4 0.9 collective-permute-done.58
  89.7 20.7 %conditional.3 = (f32[10,8,128]{2,1,0:T(8,128)}, f32[10,8,128]{2,1,0:T(8,128)}, f32[10,8,128]{2,1,0:T(8,128)}, f32[10,8,144]{2,1,0:T(8,128)}, f32[10,8,144]{2,1,0:T(8,128)}) conditional(s32[]{:T(128)} %clamp.6, (f32[10,8,128]{2,1,0:T(8,128)}, f32[10,8,144]{2,1,0:T(8,128)S(1)}, ...), branch_computations={%region_20.21_spmd, %region_21.22_spmd, %region_22.23_spmd, %regio... | conditional | bytes 860400 | solution.py:105
  89.9 1.3 %collective-permute-start.35 = (f32[10,8,144]{2,1,0:T(8,128)S(1)}, f32[10,8,144]{2,1,0:T(8,128)}, u32[]{:S(2)}, u32[]{:S(2)}) collective-permute-start(f32[10,8,144]{2,1,0:T(8,128)S(1)} %get-tuple-element.238), channel_id=1, source_target_pairs={{0,64},{64,128},{128,192},{192,256},{256,320},{320,384},{384,448},... | collective-permute-start | bytes 138248 | tf_op jit(solution)/shard_map/cond/branch_7_fun/ppermute | solution.py:99
  91.2 7.7 %collective-permute-start.36 = (f32[10,8,144]{2,1,0:T(8,128)S(1)}, f32[10,8,144]{2,1,0:T(8,128)}, u32[]{:S(2)}, u32[]{:S(2)}) collective-permute-start(f32[10,8,144]{2,1,0:T(8,128)S(1)} %get-tuple-element.239), channel_id=1, source_target_pairs={{64,0},{128,64},{192,128},{256,192},{320,256},{384,320},{448,384},... | collective-permute-start | bytes 138248 | tf_op jit(solution)/shard_map/cond/branch_7_fun/ppermute | solution.py:100
  98.9 1.9 %collective-permute-start.33 = (f32[10,8,128]{2,1,0:T(8,128)}, f32[10,8,128]{2,1,0:T(8,128)}, u32[]{:S(2)}, u32[]{:S(2)}) collective-permute-start(f32[10,8,128]{2,1,0:T(8,128)} %get-tuple-element.237), channel_id=1, source_target_pairs={{960,961},{961,962},{962,963},{963,964},{964,965},{965,966},{966,9... | collective-permute-start | bytes 122888 | tf_op jit(solution)/shard_map/cond/branch_7_fun/ppermute | solution.py:96
  100.8 7.0 %collective-permute-start.34 = (f32[10,8,128]{2,1,0:T(8,128)}, f32[10,8,128]{2,1,0:T(8,128)}, u32[]{:S(2)}, u32[]{:S(2)}) collective-permute-start(f32[10,8,128]{2,1,0:T(8,128)} %get-tuple-element.237), channel_id=1, source_target_pairs={{960,962},{961,963},{962,964},{963,965},{964,966},{965,967},{966,9... | collective-permute-start | bytes 122888 | tf_op jit(solution)/shard_map/cond/branch_7_fun/ppermute | solution.py:96
  107.8 1.9 %collective-permute-done.34 = f32[10,8,128]{2,1,0:T(8,128)} collective-permute-done((f32[10,8,128]{2,1,0:T(8,128)}, f32[10,8,128]{2,1,0:T(8,128)}, u32[]{:S(2)}, u32[]{:S(2)}) %collective-permute-start.34) | collective-permute-done | bytes 40992 | tf_op jit(solution)/shard_map/cond/branch_7_fun/ppermute | solution.py:96
  109.7 0.6 broadcast.277
  110.4 0.9 fusion.1
  111.3 0.2 reverse
  111.6 1.2 %pad_maximum_fusion = f32[10,80,144]{2,1,0:T(8,128)S(1)} fusion(f32[10,8,144]{2,1,0:T(8,128)S(1)} %broadcast_select_fusion, f32[10,64,8]{2,1,0:T(8,128)S(1)} %get-tuple-element.512, f32[10,64,128]{2,1,0:T(8,128)S(1)} %bitcast_dynamic-update-slice_fusion, f32[10,64,8]{2,1,0:T(8,128)S(1)} %get-tuple-element.511, f32[10,8,144]{2,1,0:T(8,128)} %get-tuple-element.266), kind=kLoop, calls=%fused_computation.17 | loop fusion | flops 460800 | bytes 921600 | tf_op jit(solution)/shard_map/concatenate | solution.py:118
  112.8 0.2 fusion.45
  113.1 0.2 fusion.38
  113.4 0.3 fusion.30
  113.9 0.2 fusion.14
  114.1 0.2 fusion.7
  114.4 0.3 fusion.105
  114.8 0.2 fusion.89
  115.1 0.2 fusion.82
  115.4 0.3 fusion.74
  115.8 0.2 fusion.58
  116.0 0.2 fusion.51
  116.3 0.7 slice.890
  117.1 0.2 fusion.133
  117.4 0.6 copy-done.1
  117.9 0.2 copy-done.8
  118.1 0.7 maximum_multiply_fusion
  (86 shorter events, 3.8 us)
Async XLA Ops:
  0.6 0.7 copy-start.25
  5.0 68.8 %all-to-all-start = ((f32[64,1,1026]{2,1,0:T(1,128)}), f32[64,1,1026]{2,1,0:T(1,128)S(1)}, u32[]{:S(2)}, u32[]{:S(2)}) async-start(f32[64,1,1026]{2,1,0:T(1,128)} %copy.164), calls=%async_computation | async-start | bytes 589824 | tf_op jit(solution)/shard_map/all_to_all | solution.py:48
  37.8 1.4 %copy-start.5 = (f32[2,64,128]{2,1,0:T(8,128)S(1)}, f32[2,64,128]{2,1,0:T(8,128)}, u32[]{:S(2)}) copy-start(f32[2,64,128]{2,1,0:T(8,128)} %param.42) | copy-start | bytes 196612
  38.4 0.8 copy-start.3
  38.8 0.9 copy-start.4
  39.2 0.9 copy-start.2
  39.2 1.0 copy-start
  74.9 0.8 copy-start.6
  75.8 0.8 copy-start.7
  76.6 0.7 copy-start.24
  77.3 12.2 %collective-permute-start.56 = (f32[10,8,128]{2,1,0:T(8,128)S(1)}, f32[10,8,128]{2,1,0:T(8,128)}, u32[]{:S(2)}, u32[]{:S(2)}) collective-permute-start(f32[10,8,128]{2,1,0:T(8,128)S(1)} %slice_multiply_fusion), channel_id=1, source_target_pairs={{960,960},{961,1023},{962,1022},{963,1021},{964,1020},{965,1019},{... | collective-permute-start | bytes 122888 | tf_op jit(solution)/shard_map/cond/branch_0_fun/ppermute | solution.py:75
  78.8 9.4 %collective-permute-start.57 = (f32[10,64,8]{1,2,0:T(8,128)S(1)}, f32[10,64,8]{1,2,0:T(8,128)S(1)}, u32[]{:S(2)}, u32[]{:S(2)}) collective-permute-start(f32[10,64,8]{1,2,0:T(8,128)S(1)} %copy.166), channel_id=1, source_target_pairs={{0,1},{1,2},{2,3},{3,4},{4,5},{5,6},{6,7},{7,8},{8,9},{9,10},{10,1... | collective-permute-start | bytes 61448 | tf_op jit(solution)/shard_map/cond/branch_0_fun/ppermute | solution.py:76
  83.0 6.3 %collective-permute-start.58 = (f32[10,64,8]{1,2,0:T(8,128)S(1)}, f32[10,64,8]{1,2,0:T(8,128)S(1)}, u32[]{:S(2)}, u32[]{:S(2)}) collective-permute-start(f32[10,64,8]{1,2,0:T(8,128)S(1)} %copy.167), channel_id=1, source_target_pairs={{0,63},{1,0},{2,1},{3,2},{4,3},{5,4},{6,5},{7,6},{8,7},{9,8},{10,9... | collective-permute-start | bytes 61448 | tf_op jit(solution)/shard_map/cond/branch_0_fun/ppermute | solution.py:77
  89.9 19.9 %collective-permute-start.35 = (f32[10,8,144]{2,1,0:T(8,128)S(1)}, f32[10,8,144]{2,1,0:T(8,128)}, u32[]{:S(2)}, u32[]{:S(2)}) collective-permute-start(f32[10,8,144]{2,1,0:T(8,128)S(1)} %get-tuple-element.238), channel_id=1, source_target_pairs={{0,64},{64,128},{128,192},{192,256},{256,320},{320,384},{384,448},... | collective-permute-start | bytes 138248 | tf_op jit(solution)/shard_map/cond/branch_7_fun/ppermute | solution.py:99
  91.2 18.6 %collective-permute-start.36 = (f32[10,8,144]{2,1,0:T(8,128)S(1)}, f32[10,8,144]{2,1,0:T(8,128)}, u32[]{:S(2)}, u32[]{:S(2)}) collective-permute-start(f32[10,8,144]{2,1,0:T(8,128)S(1)} %get-tuple-element.239), channel_id=1, source_target_pairs={{64,0},{128,64},{192,128},{256,192},{320,256},{384,320},{448,384},... | collective-permute-start | bytes 138248 | tf_op jit(solution)/shard_map/cond/branch_7_fun/ppermute | solution.py:100
  98.9 8.9 %collective-permute-start.33 = (f32[10,8,128]{2,1,0:T(8,128)}, f32[10,8,128]{2,1,0:T(8,128)}, u32[]{:S(2)}, u32[]{:S(2)}) collective-permute-start(f32[10,8,128]{2,1,0:T(8,128)} %get-tuple-element.237), channel_id=1, source_target_pairs={{960,961},{961,962},{962,963},{963,964},{964,965},{965,966},{966,9... | collective-permute-start | bytes 122888 | tf_op jit(solution)/shard_map/cond/branch_7_fun/ppermute | solution.py:96
  100.8 8.9 %collective-permute-start.34 = (f32[10,8,128]{2,1,0:T(8,128)}, f32[10,8,128]{2,1,0:T(8,128)}, u32[]{:S(2)}, u32[]{:S(2)}) collective-permute-start(f32[10,8,128]{2,1,0:T(8,128)} %get-tuple-element.237), channel_id=1, source_target_pairs={{960,962},{961,963},{962,964},{963,965},{964,966},{965,967},{966,9... | collective-permute-start | bytes 122888 | tf_op jit(solution)/shard_map/cond/branch_7_fun/ppermute | solution.py:96
  117.3 0.6 copy-start.1
  117.3 0.8 copy-start.8
